TPU v7x, 512 devices: a whole 4x8x8 slice. The times are simulated.
512 devices in a mesh: chan: 16 (over z_hi, x), bl: 32 (over y, z_lo, core).
Axes of the slice: x: 4, y: 8, z: 8 (z_hi: 4, z_lo: 2; z = z_hi * 2 + z_lo), core: 2. Of those that a mesh axis runs over, the one named last changes fastest.
Arguments:
- grid: float32 [256, 128, 256], P('bl'), may hold values from -6 to 6
- tile_list: int32 [16, 2048], P('chan', 'bl'), may hold values from 0 to 255, as said below
- owner_map: int32 [256], replicated, may hold values from 0 to 255, as said below
- offsets: int32 [16, 2048, 2], P('chan', 'bl'), may hold values from 4 to 60
- positions: float32 [16, 2048, 2, 128], P('chan', 'bl'), may hold values from 0 to 64
- observed: float32 [16, 2048, 2, 128], P('chan', 'bl'), may hold values from -6 to 6
- weights: float32 [16, 2048, 128], P('chan', 'bl'), may hold values from 0.1 to 1
Outputs:
- new_grid: float32 [256, 128, 256], P('bl', 'chan')
- residual: float32 [16, 2048, 2, 128], P('chan', 'bl')
Inputs may be any that keep to these rules, and one draw needn't show every extreme that they name: A permutation: tile t lies on index owner_map[t] // 8 of bl, at place owner_map[t] % 8 there. `tile_list`: of the 64 blocks held by one device (one channel group, one index of bl), at most 4 name tiles of any one owner; in every channel group some owner receives exactly 4 blocks from every device of that group.
All inputs are finite; a program needn't handle non-finite values.
Results may differ from a plain program's by a relative error of at most 0.008.
Values sent between devices are 32-bit elements; how exact they have to be, the bound alone decides.
No kernel may reach another device: no remote copies, remote signals or barrier semaphores. Data moves between devices by JAX's collectives and lax.ppermute only.
A program may use at most 128 MiB of HBM per device.

v0:
```python
import math

import jax
import jax.numpy as jnp
from jax import lax
from jax.sharding import PartitionSpec as P

kernel_beta = 18.4
half_support = 4.0
step_length = 1.0
ridge_weight = 0.5


def spheroid(offset):
    scaled = offset / half_support
    inside = scaled * scaled < 1.0
    root_term = jnp.sqrt(jnp.maximum(1.0 - scaled * scaled, 0.0))
    return jnp.where(inside, jnp.exp(kernel_beta * (root_term - 1.0)), 0.0)


def shards(grid, tile_list, owner_map, offsets, positions, observed, weights):
    owners = lax.axis_size("bl")
    tile_dev = grid.shape[0]
    tile_width = grid.shape[1]
    block_count = tile_list.shape[1]
    capacity = 2 * block_count // owners
    slots_all = owners * capacity
    tile_ids = tile_list[0]
    tile_table = jnp.arange(owner_map.shape[0], dtype=jnp.int32)
    slot_index = jnp.sum(
        jnp.where(tile_ids[:, None] == tile_table[None, :], owner_map[None, :], 0), axis=1
    )
    owner_index = slot_index // tile_dev
    local_slot = slot_index % tile_dev
    owner_onehot = (owner_index[:, None] == jnp.arange(owners, dtype=jnp.int32)[None, :]).astype(
        jnp.int32
    )
    earlier_count = jnp.cumsum(owner_onehot, axis=0) - owner_onehot
    place_rank = jnp.sum(owner_onehot * earlier_count, axis=1)
    send_slot = owner_index * capacity + place_rank
    coords = offsets[0].astype(jnp.float32)[..., None] + positions[0]
    payload = jnp.concatenate([observed[0], weights[0][:, None, :], coords], axis=1)
    outgoing = jnp.zeros((slots_all,) + payload.shape[1:], jnp.float32).at[send_slot].set(payload)
    slot_labels = (
        jnp.zeros((slots_all,), jnp.float32).at[send_slot].set(local_slot.astype(jnp.float32))
    )
    incoming, in_labels = (
        lax.all_to_all(outgoing, "bl", split_axis=0, concat_axis=0, tiled=True),
        lax.all_to_all(slot_labels, "bl", split_axis=0, concat_axis=0, tiled=True),
    )
    grid_low = grid.astype(jnp.bfloat16)
    group_size = math.gcd(slots_all, 16)
    cell_index = jnp.arange(tile_width, dtype=jnp.float32)
    tile_places = jnp.arange(tile_dev, dtype=jnp.int32)

    def degrid(batch_data, tile_index):
        tiles_now = grid_low[tile_index]
        observed_now = batch_data[:, 0:2]
        weight_now = batch_data[:, 2]
        u_coord = batch_data[:, 3]
        v_coord = batch_data[:, 4]
        kernel_u = spheroid(cell_index[None, None, :] - u_coord[:, :, None]).astype(jnp.bfloat16)
        kernel_v = spheroid(cell_index[None, None, :] - v_coord[:, :, None]).astype(jnp.bfloat16)
        projected = jnp.einsum(
            "gju,guw->gjw", kernel_u, tiles_now, preferred_element_type=jnp.float32
        )
        kernel_wide = kernel_v.astype(jnp.float32)
        model_real = jnp.sum(projected[:, :, :tile_width] * kernel_wide, axis=2)
        model_imag = jnp.sum(projected[:, :, tile_width:] * kernel_wide, axis=2)
        residual_now = weight_now[:, None, :] * (
            jnp.stack([model_real, model_imag], axis=1) - observed_now
        )
        spread = jnp.concatenate(
            [residual_now[:, 0, :, None] * kernel_wide, residual_now[:, 1, :, None] * kernel_wide],
            axis=2,
        ).astype(jnp.bfloat16)
        return (residual_now, kernel_u, spread)

    batches = incoming.reshape(
        slots_all // group_size, group_size, incoming.shape[1], incoming.shape[2]
    )
    batch_labels = in_labels.reshape(slots_all // group_size, group_size).astype(jnp.int32)
    share_rows = tile_width // lax.axis_size("chan")
    share_start = lax.axis_index("chan") * share_rows

    def process(gradient, block_item):
        batch_data, tile_index = block_item
        residual_now, kernel_u, spread = degrid(batch_data, tile_index)
        contrib = jnp.einsum("gju,gjw->guw", kernel_u, spread, preferred_element_type=jnp.float32)
        selector = (tile_index[:, None] == tile_places[None, :]).astype(jnp.float32)
        gradient = gradient + jnp.einsum(
            "gt,guw->tuw", selector, contrib, precision=lax.Precision.HIGHEST
        )
        return (gradient, residual_now)

    gradient, residual_all = lax.scan(
        process, jnp.zeros(grid.shape, jnp.float32), (batches, batch_labels)
    )
    grad_share = lax.psum_scatter(gradient, "chan", scatter_dimension=1, tiled=True)
    residual_all = residual_all.reshape(slots_all, 2, residual_all.shape[-1])
    returned = lax.all_to_all(residual_all, "bl", split_axis=0, concat_axis=0, tiled=True)
    my_residual = returned[send_slot][None]
    own_rows = lax.dynamic_slice_in_dim(grid, share_start, share_rows, 1)
    new_grid = own_rows - step_length * (grad_share + ridge_weight * own_rows)
    return (new_grid, my_residual)


def solution(mesh):
    in_specs = (
        P("bl", None, None),
        P("chan", "bl"),
        P(),
        P("chan", "bl", None),
        P("chan", "bl", None, None),
        P("chan", "bl", None, None),
        P("chan", "bl", None),
    )
    out_specs = (P("bl", "chan", None), P("chan", "bl", None, None))
    return jax.shard_map(shards, mesh=mesh, in_specs=in_specs, out_specs=out_specs, check_vma=False)
```

profile of v0, /device:TPU:1, one launch (start us, length us, event | category | flops | bytes accessed | tf_op | source)
XLA Modules:
  0.0 233.2 jit_solution(8379492701357374620)
XLA Ops:
  7.2 0.9 select_reduce_fusion
  8.5 0.8 scatter_custom_fusion
  9.3 0.7 all_to_all.12
  10.0 10.6 %all-to-all-start = ((f32[32,4,1]{1,2,0:T(1,128)}), f32[32,4,1]{1,2,0:T(1,128)S(1)}, u32[]{:S(2)}, u32[]{:S(2)}) async-start(f32[32,4,1]{1,2,0:T(1,128)} %bitcast.4), calls=%async_computation | async-start | bytes 32768 | tf_op jit(solution)/shard_map/all_to_all | solution.py:49
  20.6 0.7 convert_bitcast_fusion
  21.4 1.0 bitcast_add_fusion
  22.3 1.0 pad_maximum_fusion
  23.3 0.8 broadcast_in_dim.56
  24.1 6.5 %scatter_fusion = f32[128,5,128]{2,1,0:T(8,128)} fusion(f32[128,5,128]{2,1,0:T(8,128)} %broadcast_in_dim.56, s32[64]{0:T(128)S(1)} %fusion.61, f32[64,5,128]{2,1,0:T(8,128)S(1)} %pad_maximum_fusion), kind=kCustom, calls=%fused_computation.3 | custom fusion | bytes 491776 | tf_op jit(solution)/shard_map/scatter | solution.py:43
  30.6 8.3 %all-to-all-start.1 = ((f32[128,5,128]{2,1,0:T(8,128)}), f32[128,5,128]{2,1,0:T(8,128)S(1)}, u32[]{:S(2)}, u32[]{:S(2)}) async-start(f32[128,5,128]{2,1,0:T(8,128)} %scatter_fusion), calls=%async_computation.1 | async-start | bytes 1048576 | tf_op jit(solution)/shard_map/all_to_all | solution.py:48
  39.1 16.3 %all-to-all-done.1 = f32[128,5,128]{2,1,0:T(8,128)S(1)} async-done(((f32[128,5,128]{2,1,0:T(8,128)}), f32[128,5,128]{2,1,0:T(8,128)S(1)}, u32[]{:S(2)}, u32[]{:S(2)}) %all-to-all-start.1) | async-done | bytes 327712 | tf_op jit(solution)/shard_map/all_to_all | solution.py:48
  55.5 75.1 %while.17 = (s32[]{:T(128)}, f32[8,128,256]{2,0,1:T(8,128)}, f32[8,16,2,128]{3,1,0,2:T(8,128)S(1)}, s32[8,16]{1,0:T(8,128)S(1)}, f32[8,16,5,128]{3,1,2,0:T(8,128...) while((s32[]{:T(128)}, f32[8,128,256]{2,0,1:T(8,128)}, ...), condition=%wide.region_8.9_spmd.clone.clone, body=%wide.region_5.8_spmd.clone.clone.sunk | while | flops 334505152 | bytes 16036399 | solution.py:96
  55.6 0.6 gather_fusion
  56.2 1.1 fusion.86
  57.3 1.2 fusion.87
  58.5 1.0 fusion.88
  59.5 1.3 fusion.89
  60.8 3.1 %fusion.91 = f32[8,128,256]{2,0,1:T(8,128)} fusion(f32[16,128,256]{2,1,0:T(8,128)S(1)} %fusion.89, f32[8,128,256]{2,0,1:T(8,128)} %get-tuple-element.295, pred[]{:T(512)S(6)} %compare.18, s32[16]{0:T(128)S(1)} %fusion.90), kind=kOutput, calls=%fused_computation.14.clone.1 | convolution fusion | flops 50856064 | bytes 4194369 | tf_op jit(solution)/shard_map/while/body/eval_jaxpr/gt,guw->tuw/dot_general | solution.py:91
  63.9 0.6 gather_fusion
  64.5 1.1 fusion.86
  65.6 1.2 fusion.87
  66.8 1.0 fusion.88
  67.8 1.3 fusion.89
  69.1 4.3 %fusion.91 = f32[8,128,256]{2,0,1:T(8,128)} fusion(f32[16,128,256]{2,1,0:T(8,128)S(1)} %fusion.89, f32[8,128,256]{2,0,1:T(8,128)} %get-tuple-element.295, pred[]{:T(512)S(6)} %compare.18, s32[16]{0:T(128)S(1)} %fusion.90), kind=kOutput, calls=%fused_computation.14.clone.1 | convolution fusion | flops 50856064 | bytes 4194369 | tf_op jit(solution)/shard_map/while/body/eval_jaxpr/gt,guw->tuw/dot_general | solution.py:91
  74.0 1.1 fusion.86
  75.1 1.2 fusion.87
  76.3 1.0 fusion.88
  77.3 1.3 fusion.89
  78.6 4.3 %fusion.91 = f32[8,128,256]{2,0,1:T(8,128)} fusion(f32[16,128,256]{2,1,0:T(8,128)S(1)} %fusion.89, f32[8,128,256]{2,0,1:T(8,128)} %get-tuple-element.295, pred[]{:T(512)S(6)} %compare.18, s32[16]{0:T(128)S(1)} %fusion.90), kind=kOutput, calls=%fused_computation.14.clone.1 | convolution fusion | flops 50856064 | bytes 4194369 | tf_op jit(solution)/shard_map/while/body/eval_jaxpr/gt,guw->tuw/dot_general | solution.py:91
  82.9 0.6 gather_fusion
  83.6 1.1 fusion.86
  84.6 1.2 fusion.87
  85.9 1.0 fusion.88
  86.9 1.3 fusion.89
  88.2 4.3 %fusion.91 = f32[8,128,256]{2,0,1:T(8,128)} fusion(f32[16,128,256]{2,1,0:T(8,128)S(1)} %fusion.89, f32[8,128,256]{2,0,1:T(8,128)} %get-tuple-element.295, pred[]{:T(512)S(6)} %compare.18, s32[16]{0:T(128)S(1)} %fusion.90), kind=kOutput, calls=%fused_computation.14.clone.1 | convolution fusion | flops 50856064 | bytes 4194369 | tf_op jit(solution)/shard_map/while/body/eval_jaxpr/gt,guw->tuw/dot_general | solution.py:91
  92.5 0.6 gather_fusion
  93.1 1.1 fusion.86
  94.2 1.2 fusion.87
  95.4 1.0 fusion.88
  96.4 1.3 fusion.89
  97.7 4.3 %fusion.91 = f32[8,128,256]{2,0,1:T(8,128)} fusion(f32[16,128,256]{2,1,0:T(8,128)S(1)} %fusion.89, f32[8,128,256]{2,0,1:T(8,128)} %get-tuple-element.295, pred[]{:T(512)S(6)} %compare.18, s32[16]{0:T(128)S(1)} %fusion.90), kind=kOutput, calls=%fused_computation.14.clone.1 | convolution fusion | flops 50856064 | bytes 4194369 | tf_op jit(solution)/shard_map/while/body/eval_jaxpr/gt,guw->tuw/dot_general | solution.py:91
  102.6 1.1 fusion.86
  103.7 1.2 fusion.87
  104.9 1.0 fusion.88
  105.9 1.3 fusion.89
  107.2 4.3 %fusion.91 = f32[8,128,256]{2,0,1:T(8,128)} fusion(f32[16,128,256]{2,1,0:T(8,128)S(1)} %fusion.89, f32[8,128,256]{2,0,1:T(8,128)} %get-tuple-element.295, pred[]{:T(512)S(6)} %compare.18, s32[16]{0:T(128)S(1)} %fusion.90), kind=kOutput, calls=%fused_computation.14.clone.1 | convolution fusion | flops 50856064 | bytes 4194369 | tf_op jit(solution)/shard_map/while/body/eval_jaxpr/gt,guw->tuw/dot_general | solution.py:91
  111.5 0.6 gather_fusion
  112.2 1.1 fusion.86
  113.2 1.2 fusion.87
  114.5 1.0 fusion.88
  115.5 1.3 fusion.89
  116.8 4.3 %fusion.91 = f32[8,128,256]{2,0,1:T(8,128)} fusion(f32[16,128,256]{2,1,0:T(8,128)S(1)} %fusion.89, f32[8,128,256]{2,0,1:T(8,128)} %get-tuple-element.295, pred[]{:T(512)S(6)} %compare.18, s32[16]{0:T(128)S(1)} %fusion.90), kind=kOutput, calls=%fused_computation.14.clone.1 | convolution fusion | flops 50856064 | bytes 4194369 | tf_op jit(solution)/shard_map/while/body/eval_jaxpr/gt,guw->tuw/dot_general | solution.py:91
  121.7 1.1 fusion.86
  122.8 1.2 fusion.87
  124.0 1.0 fusion.88
  125.0 1.3 fusion.89
  126.3 4.3 %fusion.91 = f32[8,128,256]{2,0,1:T(8,128)} fusion(f32[16,128,256]{2,1,0:T(8,128)S(1)} %fusion.89, f32[8,128,256]{2,0,1:T(8,128)} %get-tuple-element.295, pred[]{:T(512)S(6)} %compare.18, s32[16]{0:T(128)S(1)} %fusion.90), kind=kOutput, calls=%fused_computation.14.clone.1 | convolution fusion | flops 50856064 | bytes 4194369 | tf_op jit(solution)/shard_map/while/body/eval_jaxpr/gt,guw->tuw/dot_general | solution.py:91
  130.6 2.6 %copy.44 = f32[8,128,256]{2,1,0:T(8,128)} copy(f32[8,128,256]{2,0,1:T(8,128)} %get-tuple-element.129) | data formatting | bytes 2097152 | tf_op jit(solution)/shard_map/while | solution.py:96
  133.1 0.7 copy.46
  133.9 4.8 %all-to-all-start.2 = ((f32[128,2,128]{2,1,0:T(2,128)}), f32[128,2,128]{2,1,0:T(2,128)S(1)}, u32[]{:S(2)}, u32[]{:S(2)}) async-start(f32[128,2,128]{2,1,0:T(2,128)} %copy.46), calls=%async_computation.3 | async-start | bytes 262144 | tf_op jit(solution)/shard_map/all_to_all | solution.py:101
  138.7 9.4 %all-to-all-done.2 = f32[128,2,128]{2,1,0:T(2,128)S(1)} async-done(((f32[128,2,128]{2,1,0:T(2,128)}), f32[128,2,128]{2,1,0:T(2,128)S(1)}, u32[]{:S(2)}, u32[]{:S(2)}) %all-to-all-start.2) | async-done | bytes 131104 | tf_op jit(solution)/shard_map/all_to_all | solution.py:101
  148.2 1.3 gather_fusion.1
  149.4 75.4 %reduce-scatter.2.cloned.1.call-done = f32[8,8,256]{2,1,0:T(8,128)} async-done(((f32[8,128,256]{2,1,0:T(8,128)}), f32[8,8,256]{2,1,0:T(8,128)}) %reduce-scatter.2.cloned.1.call-update) | async-done | bytes 65552 | tf_op jit(solution)/shard_map/reduce_scatter | solution.py:99
  224.9 1.5 add_subtract_fusion
  (77 shorter events, 3.0 us)
Async XLA Ops:
  7.2 31.8 %copy-start = (f32[8,128,256]{2,1,0:T(8,128)S(1)}, f32[8,128,256]{2,1,0:T(8,128)}, u32[]{:S(2)}) copy-start(f32[8,128,256]{2,1,0:T(8,128)} %param.9) | copy-start | bytes 3145732
  10.0 20.6 %all-to-all-start = ((f32[32,4,1]{1,2,0:T(1,128)}), f32[32,4,1]{1,2,0:T(1,128)S(1)}, u32[]{:S(2)}, u32[]{:S(2)}) async-start(f32[32,4,1]{1,2,0:T(1,128)} %bitcast.4), calls=%async_computation | async-start | bytes 32768 | tf_op jit(solution)/shard_map/all_to_all | solution.py:49
  30.6 24.8 %all-to-all-start.1 = ((f32[128,5,128]{2,1,0:T(8,128)}), f32[128,5,128]{2,1,0:T(8,128)S(1)}, u32[]{:S(2)}, u32[]{:S(2)}) async-start(f32[128,5,128]{2,1,0:T(8,128)} %scatter_fusion), calls=%async_computation.1 | async-start | bytes 1048576 | tf_op jit(solution)/shard_map/all_to_all | solution.py:48
  38.9 186.0 %reduce-scatter.2.cloned.1.call-start = ((), (), s32[]{:S(2)}) async-start(), calls=%async_computation.4 | async-start | bytes 1114112 | tf_op jit(solution)/shard_map/reduce_scatter | solution.py:99
  133.9 14.3 %all-to-all-start.2 = ((f32[128,2,128]{2,1,0:T(2,128)}), f32[128,2,128]{2,1,0:T(2,128)S(1)}, u32[]{:S(2)}, u32[]{:S(2)}) async-start(f32[128,2,128]{2,1,0:T(2,128)} %copy.46), calls=%async_computation.3 | async-start | bytes 262144 | tf_op jit(solution)/shard_map/all_to_all | solution.py:101
Sparse Core Ops, SparseCore 0:
  133.3 91.5 reduce-scatter.1
where the time goes:
time: 235 us; the launch traced here: 233 us
  waiting for transfers between devices  101 us (43%)
  matrix products  51.6 us (22%)
  starting transfers between devices  23.7 us (10%)
  other arithmetic  23.2 us (10%)
  local copies, waits for them, and re-layouts  18.7 us (8%)
  between operations  14.2 us (6%)
    reduce_scatter x1, waiting for transfers between devices, shards(): lax.psum_scatter(gradient, 'chan', scatter_dimension=1, tiled=True)  75.4 us
    dot_general x8, matrix products, process(): jnp.einsum('gt,guw->tuw', selector, contrib, precision=lax.Precision.HIGH...  33 us
    all_to_all x1, waiting for transfers between devices, shards(): lax.all_to_all(outgoing, 'bl', split_axis=0, concat_axis=0, tiled=True)  16.3 us
    all_to_all x1, starting transfers between devices, shards(): lax.all_to_all(slot_labels, 'bl', split_axis=0, concat_axis=0, tiled=True)  10.6 us
    dot_general x8, matrix products, process(): jnp.einsum('gju,gjw->guw', kernel_u, spread, preferred_element_type=jnp.f...  10 us
    reduce_sum x8, other arithmetic, degrid(): model_real = jnp.sum(projected[:, :, :tile_width] * kernel_wide, axis=2)  9.42 us
    all_to_all x1, waiting for transfers between devices, shards(): lax.all_to_all(residual_all, 'bl', split_axis=0, concat_axis=0, tiled=True)  9.41 us
    dot_general x8, matrix products, degrid(): jnp.einsum('gju,guw->gjw', kernel_u, tiles_now, preferred_element_type=jn...  8.65 us
  transfers between devices with their start and end apart: 4, of which 3 were waited for; matrix products, arithmetic and copies ran while one was open for 5% of the time, Pallas kernels for 0%

commit v1 on v0

v1 whole, which is shorter than its diff:
```python
import functools

import jax
import jax.numpy as jnp
from jax import lax
from jax.experimental import pallas as pl
from jax.experimental.pallas import tpu as pltpu
from jax.sharding import PartitionSpec as P

kernel_beta = 18.4
half_support = 4.0
step_length = 1.0
ridge_weight = 0.5


def spheroid(offset):
    scaled = offset * (1.0 / half_support)
    inside = scaled * scaled < 1.0
    root_term = jnp.sqrt(jnp.maximum(1.0 - scaled * scaled, 0.0))
    return jnp.where(inside, jnp.exp(kernel_beta * (root_term - 1.0)), 0.0)


def _grid_kernel(labels_ref, data_ref, tiles_ref, res_ref, grad_ref):
    slots = data_ref.shape[0]
    width = tiles_ref.shape[2]
    vis = data_ref.shape[2]
    grad_ref[...] = jnp.zeros(grad_ref.shape, grad_ref.dtype)
    cells = lax.broadcasted_iota(jnp.int32, (width, vis), 0).astype(jnp.float32)

    def body(s, carry):
        d = data_ref[s]
        tile = labels_ref[s]
        ku_t = spheroid(cells - d[3:4, :]).astype(jnp.bfloat16)
        kv_t = spheroid(cells - d[4:5, :]).astype(jnp.bfloat16).astype(jnp.float32)
        proj_t = jnp.dot(tiles_ref[tile], ku_t, preferred_element_type=jnp.float32)
        model_re = jnp.sum(proj_t[:width] * kv_t, axis=0, keepdims=True)
        model_im = jnp.sum(proj_t[width:] * kv_t, axis=0, keepdims=True)
        weight = d[2:3, :]
        res_re = weight * (model_re - d[0:1, :])
        res_im = weight * (model_im - d[1:2, :])
        res_ref[s] = jnp.concatenate([res_re, res_im], axis=0)
        spread_t = jnp.concatenate([res_re * kv_t, res_im * kv_t], axis=0).astype(jnp.bfloat16)
        contrib = lax.dot_general(
            ku_t, spread_t, (((1,), (1,)), ((), ())), preferred_element_type=jnp.float32
        )
        grad_ref[tile] += contrib
        return carry

    lax.fori_loop(0, slots, body, 0)


def _grid_call(labels, data, tiles_t):
    slots, _, vis = data.shape
    tile_count, wide, width = tiles_t.shape
    vmem = pltpu.MemorySpace.VMEM
    return pl.pallas_call(
        _grid_kernel,
        out_shape=(
            jax.ShapeDtypeStruct((slots, 2, vis), jnp.float32),
            jax.ShapeDtypeStruct((tile_count, width, wide), jnp.float32),
        ),
        in_specs=[
            pl.BlockSpec(memory_space=pltpu.MemorySpace.SMEM),
            pl.BlockSpec(memory_space=vmem),
            pl.BlockSpec(memory_space=vmem),
        ],
        out_specs=(pl.BlockSpec(memory_space=vmem), pl.BlockSpec(memory_space=vmem)),
    )(labels, data, tiles_t)


def shards(grid, tile_list, owner_map, offsets, positions, observed, weights):
    owners = lax.axis_size("bl")
    chan = lax.axis_size("chan")
    tile_dev = grid.shape[0]
    tile_width = grid.shape[1]
    block_count = tile_list.shape[1]
    capacity = 2 * block_count // owners
    slots_all = owners * capacity
    tile_ids = tile_list[0]
    slot_index = jnp.take(owner_map, tile_ids, axis=0)
    owner_index = slot_index // tile_dev
    local_slot = slot_index % tile_dev
    owner_onehot = (owner_index[:, None] == jnp.arange(owners, dtype=jnp.int32)[None, :]).astype(
        jnp.int32
    )
    earlier_count = jnp.cumsum(owner_onehot, axis=0) - owner_onehot
    place_rank = jnp.sum(owner_onehot * earlier_count, axis=1)
    send_slot = owner_index * capacity + place_rank
    coords = offsets[0].astype(jnp.float32)[..., None] + positions[0]
    vis = coords.shape[-1]
    label_row = jnp.broadcast_to(local_slot.astype(jnp.float32)[:, None, None], (block_count, 1, vis))
    payload = jnp.concatenate([observed[0], weights[0][:, None, :], coords, label_row], axis=1)
    match = send_slot[None, :] == jnp.arange(slots_all, dtype=jnp.int32)[:, None]
    source = jnp.sum(jnp.where(match, jnp.arange(block_count, dtype=jnp.int32)[None, :], 0), axis=1)
    filled = jnp.any(match, axis=1)
    outgoing = jnp.where(filled[:, None, None], jnp.take(payload, source, axis=0), 0.0)
    incoming = lax.all_to_all(outgoing, "bl", split_axis=0, concat_axis=0, tiled=True)
    labels = incoming[:, 5, 0].astype(jnp.int32)
    tiles_t = jnp.swapaxes(grid.astype(jnp.bfloat16), 1, 2)
    residual_all, gradient = _grid_call(labels, incoming, tiles_t)
    share_rows = tile_width // chan
    parts = gradient.reshape(tile_dev, chan, share_rows, gradient.shape[-1])
    parts = lax.all_to_all(parts, "chan", split_axis=1, concat_axis=1, tiled=True)
    grad_share = jnp.sum(parts, axis=1)
    returned = lax.all_to_all(residual_all, "bl", split_axis=0, concat_axis=0, tiled=True)
    my_residual = jnp.take(returned, send_slot, axis=0)[None]
    share_start = lax.axis_index("chan") * share_rows
    own_rows = lax.dynamic_slice_in_dim(grid, share_start, share_rows, 1)
    new_grid = own_rows - step_length * (grad_share + ridge_weight * own_rows)
    return (new_grid, my_residual)


def solution(mesh):
    in_specs = (
        P("bl", None, None),
        P("chan", "bl"),
        P(),
        P("chan", "bl", None),
        P("chan", "bl", None, None),
        P("chan", "bl", None, None),
        P("chan", "bl", None),
    )
    out_specs = (P("bl", "chan", None), P("chan", "bl", None, None))
    return jax.shard_map(shards, mesh=mesh, in_specs=in_specs, out_specs=out_specs, check_vma=False)
```

time: 235 us -> 145 us (0.62)
  Pallas kernels: 0 us -> 53.3 us
  matrix products: 51.6 us -> 0 us
  waiting for transfers between devices: 101 us -> 49.6 us
  other arithmetic: 23.2 us -> 7.03 us
  between operations: 14.2 us -> 0.81 us
  local copies, waits for them, and re-layouts: 18.7 us -> 7.15 us
  starting transfers between devices: 23.7 us -> 27.1 us
    reduce_scatter x1 -> x0, waiting for transfers between devices: 75.4 us -> none  [shards(): lax.psum_scatter(gradient, 'chan', scatter_dimension=1, tiled=True)]
    pallas_call x0 -> x1, Pallas kernels: none -> 53.3 us  [_grid_call(): pl.pallas_call(_grid_kernel, out_shape=(jax.ShapeDtypeStruct((slots, 2, v...]
    dot_general x24 -> x0, matrix products: 51.6 us -> none  [the longest x8 33 us: process(): jnp.einsum('gt,guw->tuw', selector, contrib, precision=lax.Precision.HIGH...]
    all_to_all x1, waiting for transfers between devices: 0.01 us -> 27 us  [shards(): lax.all_to_all(parts, 'chan', split_axis=1, concat_axis=1, tiled=True)]
    reduce_sum x9 -> x2, other arithmetic: 10.4 us -> 0.16 us  [the longest x1 0.09 us: shards(): jnp.sum(jnp.where(match, jnp.arange(block_count, dtype=jnp.int32)[None, :...]
    another operation x8 -> x0, other arithmetic: 8.07 us -> none
    scatter x2 -> x0, local copies, waits for them, and re-layouts: 7.24 us -> none  [the longest x1 6.47 us: shards(): jnp.zeros((slots_all,) + payload.shape[1:], jnp.float32).at[send_slot]]
    gather x9 -> x3, local copies, waits for them, and re-layouts: 6.19 us -> 2.21 us  [the longest x1 0.79 us: shards(): slot_index = jnp.take(owner_map, tile_ids, axis=0)]
  transfers between devices with their start and end apart: 4 -> 3, of which waited for: 3 -> 3; matrix products, arithmetic and copies ran while one was open for 5% -> 3% of each run, Pallas kernels for 0% -> 0%
where the time goes in v1:
time: 145 us
  Pallas kernels  53.3 us (37%)
  waiting for transfers between devices  49.6 us (34%)
  starting transfers between devices  27.1 us (19%)
  local copies, waits for them, and re-layouts  7.15 us (5%)
  other arithmetic  7.03 us (5%)
    pallas_call x1, Pallas kernels, _grid_call(): pl.pallas_call(_grid_kernel, out_shape=(jax.ShapeDtypeStruct((slots, 2, v...  53.3 us
    all_to_all x1, waiting for transfers between devices, shards(): lax.all_to_all(parts, 'chan', split_axis=1, concat_axis=1, tiled=True)  27 us
    all_to_all x1, waiting for transfers between devices, shards(): lax.all_to_all(outgoing, 'bl', split_axis=0, concat_axis=0, tiled=True)  15.5 us
    all_to_all x1, starting transfers between devices, shards(): lax.all_to_all(parts, 'chan', split_axis=1, concat_axis=1, tiled=True)  11.7 us
    all_to_all x1, starting transfers between devices, shards(): lax.all_to_all(outgoing, 'bl', split_axis=0, concat_axis=0, tiled=True)  10.6 us
    all_to_all x1, waiting for transfers between devices, shards(): lax.all_to_all(residual_all, 'bl', split_axis=0, concat_axis=0, tiled=True)  7.06 us
    all_to_all x1, starting transfers between devices, shards(): lax.all_to_all(residual_all, 'bl', split_axis=0, concat_axis=0, tiled=True)  4.84 us
  transfers between devices with their start and end apart: 3, of which 3 were waited for; matrix products, arithmetic and copies ran while one was open for 3% of the time, Pallas kernels for 0%

profile of v1, /device:TPU:1, one launch (start us, length us, event | category | flops | bytes accessed | tf_op | source)
XLA Modules:
  0.0 144.9 jit_solution(5368962364595525077)
XLA Ops:
  0.6 0.0 copy-start
  0.6 0.7 fusion.7
  1.3 0.0 copy-done
  1.3 0.0 copy-start.6
  1.3 0.8 gather_fusion
  2.1 0.0 copy-done.6
  2.1 0.1 fusion.2
  2.2 0.0 copy-start.4
  2.2 0.1 reduce_window_sum.11
  2.3 0.2 select_reduce_fusion.1
  2.5 0.1 select_reduce_fusion
  2.6 0.1 fusion.1
  2.7 0.0 copy-start.7
  2.8 0.7 copy-done.7
  3.4 0.1 copy.19
  3.5 0.0 copy-done.4
  3.5 0.0 copy-start.3
  3.5 0.1 bitcast_add_fusion
  3.7 0.0 copy-start.5
  3.7 0.1 broadcast_in_dim.74
  3.8 0.6 copy-done.3
  4.4 0.1 copy-done.5
  4.4 0.1 pad_maximum_fusion
  4.6 0.8 gather_fusion.1
  5.3 0.0 copy-start.2
  5.4 1.1 select_select_fusion
  6.5 10.6 %all-to-all-start = ((f32[128,6,128]{2,1,0:T(8,128)}), f32[128,6,128]{2,1,0:T(8,128)S(1)}, u32[]{:S(2)}, u32[]{:S(2)}) async-start(f32[128,6,128]{2,1,0:T(8,128)} %select_select_fusion), calls=%async_computation | async-start | bytes 1048576 | tf_op jit(solution)/shard_map/all_to_all | solution.py:97
  17.0 0.0 copy-done.2
  17.1 1.0 copy.21
  18.1 15.5 %all-to-all-done.data_ref = f32[128,6,128]{2,1,0:T(8,128)S(1)} async-done(((f32[128,6,128]{2,1,0:T(8,128)}), f32[128,6,128]{2,1,0:T(8,128)S(1)}, u32[]{:S(2)}, u32[]{:S(2)}) %all-to-all-start) | async-done | bytes 393248 | tf_op jit(solution)/shard_map/all_to_all | solution.py:97
  33.6 0.0 copy-start.1
  33.6 2.9 %fusion.labels_ref = s32[128]{0:T(128)} fusion(f32[128,6,128]{2,1,0:T(8,128)S(1)} %all-to-all-done.data_ref), kind=kLoop, calls=%fused_computation.7 | loop fusion | flops 128 | bytes 1024 | tf_op jit(solution)/shard_map/convert_element_type | solution.py:98
  36.5 0.0 copy-done.1
  36.5 53.3 %shard_map.86 = (f32[128,2,128]{2,1,0:T(2,128)}, f32[8,128,256]{2,1,0:T(8,128)}) custom-call(s32[128]{0:T(128)} %fusion.labels_ref, f32[128,6,128]{2,1,0:T(8,128)} %copy-done.1, bf16[8,256,128]{2,1,0:T(8,128)(2,1)} %bitcast.49), custom_call_target="tpu_custom_call" | custom-call | tf_op jit(solution)/shard_map/pallas_call | solution.py:56
  89.7 4.8 %all-to-all-start.2 = ((f32[128,2,128]{2,1,0:T(2,128)}), f32[128,2,128]{2,1,0:T(2,128)S(1)}, u32[]{:S(2)}, u32[]{:S(2)}) async-start(f32[128,2,128]{2,1,0:T(2,128)} %get-tuple-element.5), calls=%async_computation.2 | async-start | bytes 262144 | tf_op jit(solution)/shard_map/all_to_all | solution.py:105
  94.6 2.4 %copy.22 = f32[8,16,8,256]{3,2,0,1:T(8,128)} copy(f32[8,16,8,256]{3,2,1,0:T(8,128)} %bitcast.50) | data formatting | bytes 2097152 | tf_op jit(solution)/shard_map/reshape | solution.py:102
  97.0 7.1 %all-to-all-done.2 = f32[128,2,128]{2,1,0:T(2,128)S(1)} async-done(((f32[128,2,128]{2,1,0:T(2,128)}), f32[128,2,128]{2,1,0:T(2,128)S(1)}, u32[]{:S(2)}, u32[]{:S(2)}) %all-to-all-start.2) | async-done | bytes 131104 | tf_op jit(solution)/shard_map/all_to_all | solution.py:105
  104.0 11.7 %all-to-all-start.1 = ((f32[8,16,8,256]{3,2,0,1:T(8,128)}), f32[8,16,8,256]{3,2,0,1:T(8,128)S(1)}, u32[]{:S(2)}, u32[]{:S(2)}) async-start(f32[8,16,8,256]{3,2,0,1:T(8,128)} %copy.22), calls=%async_computation.1 | async-start | bytes 2097152 | tf_op jit(solution)/shard_map/all_to_all | solution.py:103
  115.8 0.7 gather_fusion.2
  116.4 0.8 bitcast_select_fusion
  117.2 27.0 %all-to-all-done.1 = f32[8,16,8,256]{3,2,0,1:T(8,128)S(1)} async-done(((f32[8,16,8,256]{3,2,0,1:T(8,128)}), f32[8,16,8,256]{3,2,0,1:T(8,128)S(1)}, u32[]{:S(2)}, u32[]{:S(2)}) %all-to-all-start.1) | async-done | bytes 1048608 | tf_op jit(solution)/shard_map/all_to_all | solution.py:103
  144.2 0.1 reduce_sum.37
  144.3 0.6 add_subtract_fusion
  (11 shorter events, 0.1 us)
Async XLA Ops:
  0.6 0.7 copy-start
  1.3 0.8 copy-start.6
  2.2 1.3 copy-start.4
  2.7 0.7 copy-start.7
  3.5 0.8 copy-start.3
  3.7 0.8 copy-start.5
  5.3 11.7 %copy-start.2 = (f32[8,128,256]{2,1,0:T(8,128)S(1)}, f32[8,128,256]{2,1,0:T(8,128)}, u32[]{:S(2)}) copy-start(f32[8,128,256]{2,1,0:T(8,128)} %param.7) | copy-start | bytes 3145732
  6.5 27.1 %all-to-all-start = ((f32[128,6,128]{2,1,0:T(8,128)}), f32[128,6,128]{2,1,0:T(8,128)S(1)}, u32[]{:S(2)}, u32[]{:S(2)}) async-start(f32[128,6,128]{2,1,0:T(8,128)} %select_select_fusion), calls=%async_computation | async-start | bytes 1048576 | tf_op jit(solution)/shard_map/all_to_all | solution.py:97
  33.6 2.9 %copy-start.1 = (f32[128,6,128]{2,1,0:T(8,128)}, f32[128,6,128]{2,1,0:T(8,128)S(1)}, u32[]{:S(2)}) copy-start(f32[128,6,128]{2,1,0:T(8,128)S(1)} %all-to-all-done.data_ref) | copy-start | bytes 1179652
  89.7 14.3 %all-to-all-start.2 = ((f32[128,2,128]{2,1,0:T(2,128)}), f32[128,2,128]{2,1,0:T(2,128)S(1)}, u32[]{:S(2)}, u32[]{:S(2)}) async-start(f32[128,2,128]{2,1,0:T(2,128)} %get-tuple-element.5), calls=%async_computation.2 | async-start | bytes 262144 | tf_op jit(solution)/shard_map/all_to_all | solution.py:105
  104.0 40.2 %all-to-all-start.1 = ((f32[8,16,8,256]{3,2,0,1:T(8,128)}), f32[8,16,8,256]{3,2,0,1:T(8,128)S(1)}, u32[]{:S(2)}, u32[]{:S(2)}) async-start(f32[8,16,8,256]{3,2,0,1:T(8,128)} %copy.22), calls=%async_computation.1 | async-start | bytes 2097152 | tf_op jit(solution)/shard_map/all_to_all | solution.py:103

commit v2 on v1

--- a/solution.py
+++ b/solution.py
@@ -46,7 +46,7 @@
         grad_ref[tile] += contrib
         return carry
 
-    lax.fori_loop(0, slots, body, 0)
+    lax.fori_loop(0, slots, body, 0, unroll=16)
 
 
 def _grid_call(labels, data, tiles_t):
@@ -87,15 +87,20 @@
     place_rank = jnp.sum(owner_onehot * earlier_count, axis=1)
     send_slot = owner_index * capacity + place_rank
     coords = offsets[0].astype(jnp.float32)[..., None] + positions[0]
-    vis = coords.shape[-1]
-    label_row = jnp.broadcast_to(local_slot.astype(jnp.float32)[:, None, None], (block_count, 1, vis))
-    payload = jnp.concatenate([observed[0], weights[0][:, None, :], coords, label_row], axis=1)
+    payload = jnp.concatenate([observed[0], weights[0][:, None, :], coords], axis=1)
     match = send_slot[None, :] == jnp.arange(slots_all, dtype=jnp.int32)[:, None]
     source = jnp.sum(jnp.where(match, jnp.arange(block_count, dtype=jnp.int32)[None, :], 0), axis=1)
     filled = jnp.any(match, axis=1)
     outgoing = jnp.where(filled[:, None, None], jnp.take(payload, source, axis=0), 0.0)
     incoming = lax.all_to_all(outgoing, "bl", split_axis=0, concat_axis=0, tiled=True)
-    labels = incoming[:, 5, 0].astype(jnp.int32)
+    tiles_all = lax.all_gather(tile_ids, "bl")
+    slot_all = jnp.take(owner_map, tiles_all, axis=0)
+    mine = (slot_all // tile_dev == lax.axis_index("bl")).astype(jnp.int32)
+    rank_all = jnp.cumsum(mine, axis=1) - 1
+    pick = (mine[:, :, None] == 1) & (
+        rank_all[:, :, None] == jnp.arange(capacity, dtype=jnp.int32)[None, None, :]
+    )
+    labels = jnp.sum(jnp.where(pick, (slot_all % tile_dev)[:, :, None], 0), axis=1).reshape(slots_all)
     tiles_t = jnp.swapaxes(grid.astype(jnp.bfloat16), 1, 2)
     residual_all, gradient = _grid_call(labels, incoming, tiles_t)
     share_rows = tile_width // chan

time: 145 us -> 149 us (1.028)
  blocking collectives: 0 us -> 39.7 us
  Pallas kernels: 53.3 us -> 17.5 us
  waiting for transfers between devices: 49.6 us -> 33.3 us
  local copies, waits for them, and re-layouts: 7.15 us -> 21.9 us
  starting transfers between devices: 27.1 us -> 30.1 us
  other arithmetic: 7.03 us -> 4.53 us
    all_gather x0 -> x1, blocking collectives: none -> 39.7 us  [shards(): tiles_all = lax.all_gather(tile_ids, 'bl')]
    pallas_call x1, Pallas kernels: 53.3 us -> 17.5 us  [_grid_call(): pl.pallas_call(_grid_kernel, out_shape=(jax.ShapeDtypeStruct((slots, 2, v...]
    all_to_all x1, waiting for transfers between devices: 15.5 us -> 0.01 us  [shards(): lax.all_to_all(outgoing, 'bl', split_axis=0, concat_axis=0, tiled=True)]
    gather x0 -> x2, local copies, waits for them, and re-layouts: none -> 13.3 us  [shards(): slot_all = jnp.take(owner_map, tiles_all, axis=0)]
    all_to_all x1, starting transfers between devices: 4.84 us -> 7.86 us  [shards(): lax.all_to_all(residual_all, 'bl', split_axis=0, concat_axis=0, tiled=True)]
    convert_element_type x2 -> x0, other arithmetic: 2.88 us -> none  [the longest x1 2.87 us: shards(): labels = incoming[:, 5, 0].astype(jnp.int32)]
  transfers between devices with their start and end apart: 3 -> 3, of which waited for: 3 -> 2; matrix products, arithmetic and copies ran while one was open for 3% -> 13% of each run, Pallas kernels for 0% -> 0%
where the time goes in v2:
time: 149 us; the launch traced here: 148 us
  blocking collectives  39.7 us (27%)
  waiting for transfers between devices  33.3 us (22%)
  starting transfers between devices  30.1 us (20%)
  local copies, waits for them, and re-layouts  21.9 us (15%)
  Pallas kernels  17.5 us (12%)
  other arithmetic  4.53 us (3%)
    all_gather x1, blocking collectives, shards(): tiles_all = lax.all_gather(tile_ids, 'bl')  39.7 us
    all_to_all x1, waiting for transfers between devices, shards(): lax.all_to_all(parts, 'chan', split_axis=1, concat_axis=1, tiled=True)  26.4 us
    pallas_call x1, Pallas kernels, _grid_call(): pl.pallas_call(_grid_kernel, out_shape=(jax.ShapeDtypeStruct((slots, 2, v...  17.5 us
    gather x2, local copies, waits for them, and re-layouts, shards(): slot_all = jnp.take(owner_map, tiles_all, axis=0)  13.3 us
    all_to_all x1, starting transfers between devices, shards(): lax.all_to_all(parts, 'chan', split_axis=1, concat_axis=1, tiled=True)  11.7 us
    all_to_all x1, starting transfers between devices, shards(): lax.all_to_all(outgoing, 'bl', split_axis=0, concat_axis=0, tiled=True)  10.6 us
    all_to_all x1, starting transfers between devices, shards(): lax.all_to_all(residual_all, 'bl', split_axis=0, concat_axis=0, tiled=True)  7.86 us
    all_to_all x1, waiting for transfers between devices, shards(): lax.all_to_all(residual_all, 'bl', split_axis=0, concat_axis=0, tiled=True)  6.85 us
  transfers between devices with their start and end apart: 3, of which 2 were waited for; matrix products, arithmetic and copies ran while one was open for 13% of the time, Pallas kernels for 0%

profile of v2, /device:TPU:1, one launch (start us, length us, event | category | flops | bytes accessed | tf_op | source)
XLA Modules:
  0.0 147.9 jit_solution(14792882973613688934)
XLA Ops:
  0.6 0.0 copy-start
  0.6 0.7 fusion.10
  1.3 0.0 copy-done
  1.3 0.0 copy-start.6
  1.3 0.8 gather_fusion.1
  2.1 0.0 copy-done.6
  2.1 0.1 fusion.2
  2.2 0.0 copy-start.3
  2.2 0.1 reduce_window_sum.23
  2.3 0.2 select_reduce_fusion.2
  2.5 0.1 select_reduce_fusion.1
  2.6 0.1 fusion.1
  2.7 0.0 copy-start.7
  2.8 0.7 copy-done.7
  3.4 0.1 copy.22
  3.5 0.0 copy-done.3
  3.5 0.0 copy-start.4
  3.5 0.0 copy-start.5
  3.5 0.1 bitcast_add_fusion
  3.7 0.7 copy-done.4
  4.4 0.0 copy-done.5
  4.4 0.1 pad_maximum_fusion
  4.5 0.8 gather_fusion.2
  5.2 1.1 select_select_fusion
  6.4 10.6 %all-to-all-start = ((f32[128,5,128]{2,1,0:T(8,128)}), f32[128,5,128]{2,1,0:T(8,128)S(1)}, u32[]{:S(2)}, u32[]{:S(2)}) async-start(f32[128,5,128]{2,1,0:T(8,128)} %select_select_fusion), calls=%async_computation | async-start | bytes 1048576 | tf_op jit(solution)/shard_map/all_to_all | solution.py:95
  16.9 39.7 %all-gather = s32[32,1,64]{2,1,0:T(1,128)S(1)} all-gather(s32[1,1,64]{2,1,0:T(1,128)S(1)} %bitcast.59), channel_id=1, replica_groups=mesh['chan'=16,'bl'=32] {'bl'}, dimensions={0}, use_global_device_ids=true | all-gather | bytes 8448 | tf_op jit(solution)/shard_map/all_gather | solution.py:96
  56.6 0.1 reshape.236
  56.7 0.0 copy-start.2
  56.7 13.2 %gather_fusion = s32[2048]{0:T(1024)S(1)} fusion(s32[256]{0:T(256)S(1)} %copy-done, s32[2048]{0:T(1024)S(1)} %broadcast_clamp_fusion), kind=kCustom, calls=%fused_computation | custom fusion | bytes 24576 | tf_op jit(solution)/shard_map/jit(_take)/gather | solution.py:97
  69.9 0.1 reshape.235
  70.0 0.2 reduce_window_sum.22
  70.2 0.1 select_reduce_fusion
  70.4 0.1 copy.21
  70.5 0.6 reshape.232.labels_ref
  71.1 0.0 copy-done.2
  71.1 1.0 copy.24
  72.1 0.0 all-to-all-done.data_ref
  72.1 0.0 copy-start.1
  72.1 0.8 copy-done.1
  72.9 17.5 %shard_map.86 = (f32[128,2,128]{2,1,0:T(2,128)}, f32[8,128,256]{2,1,0:T(8,128)}) custom-call(s32[128]{0:T(128)} %reshape.232.labels_ref, f32[128,5,128]{2,1,0:T(8,128)} %copy-done.1, bf16[8,256,128]{2,1,0:T(8,128)(2,1)} %bitcast.52), custom_call_target="tpu_custom_call" | custom-call | tf_op jit(solution)/shard_map/pallas_call | solution.py:56
  90.5 7.9 %all-to-all-start.2 = ((f32[128,2,128]{2,1,0:T(2,128)}), f32[128,2,128]{2,1,0:T(2,128)S(1)}, u32[]{:S(2)}, u32[]{:S(2)}) async-start(f32[128,2,128]{2,1,0:T(2,128)} %get-tuple-element.5), calls=%async_computation.2 | async-start | bytes 262144 | tf_op jit(solution)/shard_map/all_to_all | solution.py:110
  98.3 2.4 %copy.25 = f32[8,16,8,256]{3,2,0,1:T(8,128)} copy(f32[8,16,8,256]{3,2,1,0:T(8,128)} %bitcast.53) | data formatting | bytes 2097152 | tf_op jit(solution)/shard_map/reshape | solution.py:107
  100.7 6.9 %all-to-all-done.2 = f32[128,2,128]{2,1,0:T(2,128)S(1)} async-done(((f32[128,2,128]{2,1,0:T(2,128)}), f32[128,2,128]{2,1,0:T(2,128)S(1)}, u32[]{:S(2)}, u32[]{:S(2)}) %all-to-all-start.2) | async-done | bytes 131104 | tf_op jit(solution)/shard_map/all_to_all | solution.py:110
  107.6 11.7 %all-to-all-start.1 = ((f32[8,16,8,256]{3,2,0,1:T(8,128)}), f32[8,16,8,256]{3,2,0,1:T(8,128)S(1)}, u32[]{:S(2)}, u32[]{:S(2)}) async-start(f32[8,16,8,256]{3,2,0,1:T(8,128)} %copy.25), calls=%async_computation.1 | async-start | bytes 2097152 | tf_op jit(solution)/shard_map/all_to_all | solution.py:108
  119.3 0.7 gather_fusion.3
  120.0 0.8 bitcast_select_fusion
  120.8 26.4 %all-to-all-done.1 = f32[8,16,8,256]{3,2,0,1:T(8,128)S(1)} async-done(((f32[8,16,8,256]{3,2,0,1:T(8,128)}), f32[8,16,8,256]{3,2,0,1:T(8,128)S(1)}, u32[]{:S(2)}, u32[]{:S(2)}) %all-to-all-start.1) | async-done | bytes 1048608 | tf_op jit(solution)/shard_map/all_to_all | solution.py:108
  147.2 0.1 reduce_sum.47
  147.2 0.6 add_subtract_fusion
  (14 shorter events, 0.1 us)
Async XLA Ops:
  0.6 0.7 copy-start
  1.3 0.8 copy-start.6
  2.2 1.3 copy-start.3
  2.7 0.7 copy-start.7
  3.5 0.8 copy-start.4
  3.5 0.8 copy-start.5
  6.4 65.8 %all-to-all-start = ((f32[128,5,128]{2,1,0:T(8,128)}), f32[128,5,128]{2,1,0:T(8,128)S(1)}, u32[]{:S(2)}, u32[]{:S(2)}) async-start(f32[128,5,128]{2,1,0:T(8,128)} %select_select_fusion), calls=%async_computation | async-start | bytes 1048576 | tf_op jit(solution)/shard_map/all_to_all | solution.py:95
  56.7 14.4 %copy-start.2 = (f32[8,128,256]{2,1,0:T(8,128)S(1)}, f32[8,128,256]{2,1,0:T(8,128)}, u32[]{:S(2)}) copy-start(f32[8,128,256]{2,1,0:T(8,128)} %param.7) | copy-start | bytes 3145732
  72.1 0.8 copy-start.1
  90.5 17.1 %all-to-all-start.2 = ((f32[128,2,128]{2,1,0:T(2,128)}), f32[128,2,128]{2,1,0:T(2,128)S(1)}, u32[]{:S(2)}, u32[]{:S(2)}) async-start(f32[128,2,128]{2,1,0:T(2,128)} %get-tuple-element.5), calls=%async_computation.2 | async-start | bytes 262144 | tf_op jit(solution)/shard_map/all_to_all | solution.py:110
  107.6 39.6 %all-to-all-start.1 = ((f32[8,16,8,256]{3,2,0,1:T(8,128)}), f32[8,16,8,256]{3,2,0,1:T(8,128)S(1)}, u32[]{:S(2)}, u32[]{:S(2)}) async-start(f32[8,16,8,256]{3,2,0,1:T(8,128)} %copy.25), calls=%async_computation.1 | async-start | bytes 2097152 | tf_op jit(solution)/shard_map/all_to_all | solution.py:108

commit v3 on v1

--- a/solution.py
+++ b/solution.py
@@ -22,6 +22,7 @@
 
 def _grid_kernel(labels_ref, data_ref, tiles_ref, res_ref, grad_ref):
     slots = data_ref.shape[0]
+    chunks, _, rows, _ = grad_ref.shape
     width = tiles_ref.shape[2]
     vis = data_ref.shape[2]
     grad_ref[...] = jnp.zeros(grad_ref.shape, grad_ref.dtype)
@@ -43,13 +44,13 @@
         contrib = lax.dot_general(
             ku_t, spread_t, (((1,), (1,)), ((), ())), preferred_element_type=jnp.float32
         )
-        grad_ref[tile] += contrib
+        grad_ref[:, pl.ds(tile, 1)] += contrib.reshape(chunks, 1, rows, 2 * width)
         return carry
 
-    lax.fori_loop(0, slots, body, 0)
+    lax.fori_loop(0, slots, body, 0, unroll=16)
 
 
-def _grid_call(labels, data, tiles_t):
+def _grid_call(labels, data, tiles_t, chunks):
     slots, _, vis = data.shape
     tile_count, wide, width = tiles_t.shape
     vmem = pltpu.MemorySpace.VMEM
@@ -57,7 +58,7 @@
         _grid_kernel,
         out_shape=(
             jax.ShapeDtypeStruct((slots, 2, vis), jnp.float32),
-            jax.ShapeDtypeStruct((tile_count, width, wide), jnp.float32),
+            jax.ShapeDtypeStruct((chunks, tile_count, width // chunks, wide), jnp.float32),
         ),
         in_specs=[
             pl.BlockSpec(memory_space=pltpu.MemorySpace.SMEM),
@@ -95,13 +96,12 @@
     filled = jnp.any(match, axis=1)
     outgoing = jnp.where(filled[:, None, None], jnp.take(payload, source, axis=0), 0.0)
     incoming = lax.all_to_all(outgoing, "bl", split_axis=0, concat_axis=0, tiled=True)
-    labels = incoming[:, 5, 0].astype(jnp.int32)
+    labels = jnp.max(incoming[:, 5, :], axis=1).astype(jnp.int32)
     tiles_t = jnp.swapaxes(grid.astype(jnp.bfloat16), 1, 2)
-    residual_all, gradient = _grid_call(labels, incoming, tiles_t)
+    residual_all, gradient = _grid_call(labels, incoming, tiles_t, chan)
     share_rows = tile_width // chan
-    parts = gradient.reshape(tile_dev, chan, share_rows, gradient.shape[-1])
-    parts = lax.all_to_all(parts, "chan", split_axis=1, concat_axis=1, tiled=True)
-    grad_share = jnp.sum(parts, axis=1)
+    parts = lax.all_to_all(gradient, "chan", split_axis=0, concat_axis=0, tiled=True)
+    grad_share = jnp.sum(parts, axis=0)
     returned = lax.all_to_all(residual_all, "bl", split_axis=0, concat_axis=0, tiled=True)
     my_residual = jnp.take(returned, send_slot, axis=0)[None]
     share_start = lax.axis_index("chan") * share_rows

time: 145 us -> 108 us (0.74)
  Pallas kernels: 53.3 us -> 17.6 us
  blocking collectives: 0 us -> 14.3 us
  waiting for transfers between devices: 49.6 us -> 42.5 us
  starting transfers between devices: 27.1 us -> 22.3 us
  local copies, waits for them, and re-layouts: 7.15 us -> 4.77 us
    pallas_call x1, Pallas kernels: 53.3 us -> 17.6 us  [_grid_call(): pl.pallas_call(_grid_kernel, out_shape=(jax.ShapeDtypeStruct((slots, 2, v...]
    all_to_all x0 -> x1, blocking collectives: none -> 14.3 us  [shards(): lax.all_to_all(residual_all, 'bl', split_axis=0, concat_axis=0, tiled=True)]
    all_to_all x2 -> x1, waiting for transfers between devices: 34.1 us -> 27 us  [shards(): lax.all_to_all(gradient, 'chan', split_axis=0, concat_axis=0, tiled=True)]
    all_to_all x2 -> x1, starting transfers between devices: 16.5 us -> 11.7 us  [shards(): lax.all_to_all(gradient, 'chan', split_axis=0, concat_axis=0, tiled=True)]
    reshape x1 -> x0, local copies, waits for them, and re-layouts: 2.37 us -> none  [shards(): parts = gradient.reshape(tile_dev, chan, share_rows, gradient.shape[-1])]
    convert_element_type x1, other arithmetic: 2.87 us -> 0.52 us  [shards(): labels = jnp.max(incoming[:, 5, :], axis=1).astype(jnp.int32)]
  transfers between devices with their start and end apart: 3 -> 2, of which waited for: 3 -> 2; matrix products, arithmetic and copies ran while one was open for 3% -> 2% of each run, Pallas kernels for 0% -> 0%
where the time goes in v3:
time: 108 us
  waiting for transfers between devices  42.5 us (39%)
  starting transfers between devices  22.3 us (21%)
  Pallas kernels  17.6 us (16%)
  blocking collectives  14.3 us (13%)
  other arithmetic  5.7 us (5%)
  local copies, waits for them, and re-layouts  4.77 us (4%)
    all_to_all x1, waiting for transfers between devices, shards(): lax.all_to_all(gradient, 'chan', split_axis=0, concat_axis=0, tiled=True)  27 us
    pallas_call x1, Pallas kernels, _grid_call(): pl.pallas_call(_grid_kernel, out_shape=(jax.ShapeDtypeStruct((slots, 2, v...  17.6 us
    all_to_all x1, waiting for transfers between devices, shards(): lax.all_to_all(outgoing, 'bl', split_axis=0, concat_axis=0, tiled=True)  15.5 us
    all_to_all x1, blocking collectives, shards(): lax.all_to_all(residual_all, 'bl', split_axis=0, concat_axis=0, tiled=True)  14.3 us
    all_to_all x1, starting transfers between devices, shards(): lax.all_to_all(gradient, 'chan', split_axis=0, concat_axis=0, tiled=True)  11.7 us
    all_to_all x1, starting transfers between devices, shards(): lax.all_to_all(outgoing, 'bl', split_axis=0, concat_axis=0, tiled=True)  10.6 us
    unnamed x17, local copies, waits for them, and re-layouts  2.35 us
  transfers between devices with their start and end apart: 2, of which 2 were waited for; matrix products, arithmetic and copies ran while one was open for 2% of the time, Pallas kernels for 0%

profile of v3, /device:TPU:1, one launch (start us, length us, event | category | flops | bytes accessed | tf_op | source)
XLA Modules:
  0.0 107.9 jit_solution(8230247300517710122)
XLA Ops:
  0.6 0.0 copy-start
  0.6 0.7 fusion.6
  1.3 0.0 copy-done
  1.3 0.0 copy-start.6
  1.3 0.8 gather_fusion
  2.1 0.0 copy-done.6
  2.1 0.1 fusion.1
  2.2 0.0 copy-start.4
  2.2 0.1 reduce_window_sum.11
  2.3 0.2 select_reduce_fusion.1
  2.5 0.1 select_reduce_fusion
  2.6 0.1 fusion
  2.7 0.0 copy-start.7
  2.8 0.7 copy-done.7
  3.4 0.1 copy.15
  3.5 0.0 copy-done.4
  3.5 0.0 copy-start.3
  3.5 0.1 bitcast_add_fusion
  3.7 0.0 copy-start.5
  3.7 0.1 broadcast_in_dim.74
  3.8 0.6 copy-done.3
  4.4 0.1 copy-done.5
  4.4 0.1 pad_maximum_fusion
  4.6 0.8 gather_fusion.1
  5.3 0.0 copy-start.2
  5.4 1.1 %select_select_fusion = f32[128,6,128]{2,1,0:T(8,128)} fusion(f32[128,6,128]{2,1,0:T(8,128)S(1)} %gather_fusion.1, pred[128]{0:T(512)(128)(4,1)S(1)} %compare_and_fusion.1, pred[128]{0:T(512)(128)(4,1)S(1)} %fusion), kind=kLoop, calls=%fused_computation.4 | loop fusion | flops 196608 | bytes 786688 | tf_op jit(solution)/shard_map/jit(_where)/select_n | solution.py:97
  6.5 10.6 %all-to-all-start = ((f32[128,6,128]{2,1,0:T(8,128)}), f32[128,6,128]{2,1,0:T(8,128)S(1)}, u32[]{:S(2)}, u32[]{:S(2)}) async-start(f32[128,6,128]{2,1,0:T(8,128)} %select_select_fusion), calls=%async_computation | async-start | bytes 1048576 | tf_op jit(solution)/shard_map/all_to_all | solution.py:98
  17.0 0.0 copy-done.2
  17.1 1.0 copy.17
  18.1 15.5 %all-to-all-done.data_ref = f32[128,6,128]{2,1,0:T(8,128)S(1)} async-done(((f32[128,6,128]{2,1,0:T(8,128)}), f32[128,6,128]{2,1,0:T(8,128)S(1)}, u32[]{:S(2)}, u32[]{:S(2)}) %all-to-all-start) | async-done | bytes 393248 | tf_op jit(solution)/shard_map/all_to_all | solution.py:98
  33.6 0.0 copy-start.1
  33.6 1.0 slice_reduce_fusion
  34.6 0.5 convert_element_type.30.labels_ref
  35.2 0.0 copy-done.1
  35.2 17.6 %shard_map.86 = (f32[128,2,128]{2,1,0:T(2,128)}, f32[16,8,8,256]{3,2,1,0:T(8,128)}) custom-call(s32[128]{0:T(128)} %convert_element_type.30.labels_ref, f32[128,6,128]{2,1,0:T(8,128)} %copy-done.1, bf16[8,256,128]{2,1,0:T(8,128)(2,1)} %bitcast.48), custom_call_target="tpu_custom_call" | custom-call | tf_op jit(solution)/shard_map/pallas_call | solution.py:57
  52.7 14.3 %all_to_all.15 = f32[128,2,128]{2,1,0:T(2,128)S(1)} all-to-all(f32[128,2,128]{2,1,0:T(2,128)} %get-tuple-element.5), channel_id=1, replica_groups=mesh['chan'=16,'bl'=32] {'bl'}, dimensions={0} | all-to-all | bytes 262144 | tf_op jit(solution)/shard_map/all_to_all | solution.py:105
  67.0 11.7 %all-to-all-start.1 = ((f32[16,8,8,256]{3,2,1,0:T(8,128)}), f32[16,8,8,256]{3,2,1,0:T(8,128)S(1)}, u32[]{:S(2)}, u32[]{:S(2)}) async-start(f32[16,8,8,256]{3,2,1,0:T(8,128)} %get-tuple-element.4), calls=%async_computation.1 | async-start | bytes 2097152 | tf_op jit(solution)/shard_map/all_to_all | solution.py:103
  78.7 0.7 gather_fusion.2
  79.4 0.8 bitcast_select_fusion
  80.2 27.0 %all-to-all-done.1 = f32[16,8,8,256]{3,2,1,0:T(8,128)S(1)} async-done(((f32[16,8,8,256]{3,2,1,0:T(8,128)}), f32[16,8,8,256]{3,2,1,0:T(8,128)S(1)}, u32[]{:S(2)}, u32[]{:S(2)}) %all-to-all-start.1) | async-done | bytes 1048608 | tf_op jit(solution)/shard_map/all_to_all | solution.py:103
  107.2 0.1 reduce_sum.37
  107.2 0.6 add_subtract_fusion
  (11 shorter events, 0.1 us)
Async XLA Ops:
  0.6 0.7 copy-start
  1.3 0.8 copy-start.6
  2.2 1.3 %copy-start.4 = (f32[1,64,2,128]{3,2,1,0:T(2,128)S(1)}, f32[1,64,2,128]{3,2,1,0:T(2,128)}, u32[]{:S(2)}) copy-start(f32[1,64,2,128]{3,2,1,0:T(2,128)} %param.11) | copy-start | bytes 196612
  2.7 0.7 copy-start.7
  3.5 0.8 copy-start.3
  3.7 0.8 copy-start.5
  5.3 11.7 %copy-start.2 = (f32[8,128,256]{2,1,0:T(8,128)S(1)}, f32[8,128,256]{2,1,0:T(8,128)}, u32[]{:S(2)}) copy-start(f32[8,128,256]{2,1,0:T(8,128)} %param.7) | copy-start | bytes 3145732
  6.5 27.1 %all-to-all-start = ((f32[128,6,128]{2,1,0:T(8,128)}), f32[128,6,128]{2,1,0:T(8,128)S(1)}, u32[]{:S(2)}, u32[]{:S(2)}) async-start(f32[128,6,128]{2,1,0:T(8,128)} %select_select_fusion), calls=%async_computation | async-start | bytes 1048576 | tf_op jit(solution)/shard_map/all_to_all | solution.py:98
  33.6 1.6 %copy-start.1 = (f32[128,6,128]{2,1,0:T(8,128)}, f32[128,6,128]{2,1,0:T(8,128)S(1)}, u32[]{:S(2)}) copy-start(f32[128,6,128]{2,1,0:T(8,128)S(1)} %all-to-all-done.data_ref) | copy-start | bytes 1179652
  67.0 40.2 %all-to-all-start.1 = ((f32[16,8,8,256]{3,2,1,0:T(8,128)}), f32[16,8,8,256]{3,2,1,0:T(8,128)S(1)}, u32[]{:S(2)}, u32[]{:S(2)}) async-start(f32[16,8,8,256]{3,2,1,0:T(8,128)} %get-tuple-element.4), calls=%async_computation.1 | async-start | bytes 2097152 | tf_op jit(solution)/shard_map/all_to_all | solution.py:103

commit v4 on v3

--- a/solution.py
+++ b/solution.py
@@ -100,8 +100,10 @@
     tiles_t = jnp.swapaxes(grid.astype(jnp.bfloat16), 1, 2)
     residual_all, gradient = _grid_call(labels, incoming, tiles_t, chan)
     share_rows = tile_width // chan
-    parts = lax.all_to_all(gradient, "chan", split_axis=0, concat_axis=0, tiled=True)
-    grad_share = jnp.sum(parts, axis=0)
+    sc_tiles = tile_dev // 4
+    sc_share = lax.psum_scatter(gradient[:, :sc_tiles], "chan", scatter_dimension=0, tiled=True)
+    parts = lax.all_to_all(gradient[:, sc_tiles:], "chan", split_axis=0, concat_axis=0, tiled=True)
+    grad_share = jnp.concatenate([sc_share[0], jnp.sum(parts, axis=0)], axis=0)
     returned = lax.all_to_all(residual_all, "bl", split_axis=0, concat_axis=0, tiled=True)
     my_residual = jnp.take(returned, send_slot, axis=0)[None]
     share_start = lax.axis_index("chan") * share_rows

time: 108 us -> 188 us (1.74); the launches traced: 108 us -> 186 us
  waiting for transfers between devices: 42.5 us -> 112 us
  blocking collectives: 14.3 us -> 0 us
  between operations: 0.8 us -> 14.2 us
  starting transfers between devices: 22.3 us -> 27.1 us
  local copies, waits for them, and re-layouts: 4.77 us -> 8.58 us
    reduce_scatter x0 -> x1, waiting for transfers between devices: none -> 70 us  [shards(): lax.psum_scatter(gradient[:, :sc_tiles], 'chan', scatter_dimension=0, til...]
    all_to_all x1 -> x0, blocking collectives: 14.3 us -> none  [shards(): lax.all_to_all(residual_all, 'bl', split_axis=0, concat_axis=0, tiled=True)]
    all_to_all x1 -> x2, starting transfers between devices: 11.7 us -> 16.5 us  [the longest x1 11.7 us: shards(): lax.all_to_all(gradient[:, sc_tiles:], 'chan', split_axis=0, concat_axis=...]
    slice x0 -> x2, local copies, waits for them, and re-layouts: none -> 3.8 us  [the longest x1 2.12 us: shards(): gradient[:, sc_tiles:]]
    all_to_all x1 -> x2, waiting for transfers between devices: 27 us -> 26.4 us  [the longest x1 19.1 us: shards(): lax.all_to_all(gradient[:, sc_tiles:], 'chan', split_axis=0, concat_axis=...]
  transfers between devices with their start and end apart: 2 -> 4, of which waited for: 2 -> 4; matrix products, arithmetic and copies ran while one was open for 2% -> 3% of each run, Pallas kernels for 0% -> 0%
where the time goes in v4:
time: 188 us; the launch traced here: 186 us
  waiting for transfers between devices  112 us (60%)
  starting transfers between devices  27.1 us (14%)
  Pallas kernels  17.6 us (9%)
  between operations  14.2 us (8%)
  local copies, waits for them, and re-layouts  8.58 us (5%)
  other arithmetic  6.39 us (3%)
    reduce_scatter x1, waiting for transfers between devices, shards(): lax.psum_scatter(gradient[:, :sc_tiles], 'chan', scatter_dimension=0, til...  70 us
    all_to_all x1, waiting for transfers between devices, shards(): lax.all_to_all(gradient[:, sc_tiles:], 'chan', split_axis=0, concat_axis=...  19.1 us
    pallas_call x1, Pallas kernels, _grid_call(): pl.pallas_call(_grid_kernel, out_shape=(jax.ShapeDtypeStruct((slots, 2, v...  17.6 us
    all_to_all x1, waiting for transfers between devices, shards(): lax.all_to_all(outgoing, 'bl', split_axis=0, concat_axis=0, tiled=True)  15.5 us
    all_to_all x1, starting transfers between devices, shards(): lax.all_to_all(gradient[:, sc_tiles:], 'chan', split_axis=0, concat_axis=...  11.7 us
    all_to_all x1, starting transfers between devices, shards(): lax.all_to_all(outgoing, 'bl', split_axis=0, concat_axis=0, tiled=True)  10.6 us
    all_to_all x1, waiting for transfers between devices, shards(): lax.all_to_all(residual_all, 'bl', split_axis=0, concat_axis=0, tiled=True)  7.31 us
    all_to_all x1, starting transfers between devices, shards(): lax.all_to_all(residual_all, 'bl', split_axis=0, concat_axis=0, tiled=True)  4.84 us
  transfers between devices with their start and end apart: 4, of which 4 were waited for; matrix products, arithmetic and copies ran while one was open for 3% of the time, Pallas kernels for 0%

profile of v4, /device:TPU:1, one launch (start us, length us, event | category | flops | bytes accessed | tf_op | source)
XLA Modules:
  0.0 185.9 jit_solution(4567226417965063)
XLA Ops:
  7.2 0.0 copy-start
  7.2 0.7 fusion.7
  7.9 0.0 copy-done
  7.9 0.0 copy-start.6
  7.9 0.8 gather_fusion
  8.7 0.0 copy-done.6
  8.7 0.1 fusion.2
  8.7 0.0 copy-start.4
  8.8 0.1 reduce_window_sum.11
  8.9 0.2 select_reduce_fusion.1
  9.1 0.1 select_reduce_fusion
  9.2 0.1 fusion.1
  9.3 0.0 copy-start.7
  9.3 0.7 copy-done.7
  10.0 0.1 copy.15
  10.1 0.0 copy-done.4
  10.1 0.0 copy-start.3
  10.1 0.1 bitcast_add_fusion
  10.2 0.0 copy-start.5
  10.2 0.1 broadcast_in_dim.74
  10.4 0.6 copy-done.3
  10.9 0.1 copy-done.5
  11.0 0.1 pad_maximum_fusion
  11.1 0.8 gather_fusion.1
  11.9 0.0 copy-start.2
  11.9 1.1 select_select_fusion
  13.0 10.6 %all-to-all-start = ((f32[128,6,128]{2,1,0:T(8,128)}), f32[128,6,128]{2,1,0:T(8,128)S(1)}, u32[]{:S(2)}, u32[]{:S(2)}) async-start(f32[128,6,128]{2,1,0:T(8,128)} %select_select_fusion), calls=%async_computation | async-start | bytes 1048576 | tf_op jit(solution)/shard_map/all_to_all | solution.py:98
  23.6 0.0 copy-done.2
  23.6 1.0 copy.17
  24.6 15.5 %all-to-all-done.data_ref = f32[128,6,128]{2,1,0:T(8,128)S(1)} async-done(((f32[128,6,128]{2,1,0:T(8,128)}), f32[128,6,128]{2,1,0:T(8,128)S(1)}, u32[]{:S(2)}, u32[]{:S(2)}) %all-to-all-start) | async-done | bytes 393248 | tf_op jit(solution)/shard_map/all_to_all | solution.py:98
  40.1 0.0 copy-start.1
  40.1 1.0 slice_reduce_fusion
  41.2 0.5 convert_element_type.30.labels_ref
  41.7 0.0 copy-done.1
  41.7 17.6 %shard_map.86 = (f32[128,2,128]{2,1,0:T(2,128)}, f32[16,8,8,256]{3,2,1,0:T(8,128)}) custom-call(s32[128]{0:T(128)} %convert_element_type.30.labels_ref, f32[128,6,128]{2,1,0:T(8,128)} %copy-done.1, bf16[8,256,128]{2,1,0:T(8,128)(2,1)} %bitcast.49), custom_call_target="tpu_custom_call" | custom-call | tf_op jit(solution)/shard_map/pallas_call | solution.py:57
  59.3 4.8 %all-to-all-start.2 = ((f32[128,2,128]{2,1,0:T(2,128)}), f32[128,2,128]{2,1,0:T(2,128)S(1)}, u32[]{:S(2)}, u32[]{:S(2)}) async-start(f32[128,2,128]{2,1,0:T(2,128)} %get-tuple-element.5), calls=%async_computation.3 | async-start | bytes 262144 | tf_op jit(solution)/shard_map/all_to_all | solution.py:107
  64.1 2.1 %slice.11 = f32[16,6,8,256]{3,2,1,0:T(8,128)} slice(f32[16,8,8,256]{3,2,1,0:T(8,128)} %get-tuple-element.4), slice={[0:16], [2:8], [0:8], [0:256]} | slice | bytes 1572864 | tf_op jit(solution)/shard_map/slice | solution.py:105
  66.2 7.3 %all-to-all-done.2 = f32[128,2,128]{2,1,0:T(2,128)S(1)} async-done(((f32[128,2,128]{2,1,0:T(2,128)}), f32[128,2,128]{2,1,0:T(2,128)S(1)}, u32[]{:S(2)}, u32[]{:S(2)}) %all-to-all-start.2) | async-done | bytes 131104 | tf_op jit(solution)/shard_map/all_to_all | solution.py:107
  73.5 11.7 %all-to-all-start.1 = ((f32[16,6,8,256]{3,2,1,0:T(8,128)}), f32[16,6,8,256]{3,2,1,0:T(8,128)S(1)}, u32[]{:S(2)}, u32[]{:S(2)}) async-start(f32[16,6,8,256]{3,2,1,0:T(8,128)} %slice.11), calls=%async_computation.2 | async-start | bytes 1572864 | tf_op jit(solution)/shard_map/all_to_all | solution.py:105
  85.2 0.0 reduce-scatter.2.cloned.1.call-start
  85.3 1.7 slice.10
  87.0 0.0 reduce-scatter.2.cloned.1.call-update
  87.0 0.7 gather_fusion.2
  87.7 0.8 bitcast_select_fusion
  88.5 19.1 %all-to-all-done.1 = f32[16,6,8,256]{3,2,1,0:T(8,128)S(1)} async-done(((f32[16,6,8,256]{3,2,1,0:T(8,128)}), f32[16,6,8,256]{3,2,1,0:T(8,128)S(1)}, u32[]{:S(2)}, u32[]{:S(2)}) %all-to-all-start.1) | async-done | bytes 786464 | tf_op jit(solution)/shard_map/all_to_all | solution.py:105
  107.6 0.1 reduce_sum.37
  107.7 70.0 %reduce-scatter.2.cloned.1.call-done = f32[1,2,8,256]{3,2,1,0:T(8,128)} async-done(((f32[16,2,8,256]{3,2,1,0:T(8,128)}), f32[1,2,8,256]{3,2,1,0:T(8,128)}) %reduce-scatter.2.cloned.1.call-update) | async-done | bytes 16400 | tf_op jit(solution)/shard_map/reduce_scatter | solution.py:104
  177.7 1.4 fusion
  (11 shorter events, 0.1 us)
Async XLA Ops:
  7.2 0.7 copy-start
  7.9 0.8 copy-start.6
  8.7 1.3 copy-start.4
  9.3 0.7 copy-start.7
  10.1 0.8 copy-start.3
  10.2 0.8 copy-start.5
  11.9 11.7 %copy-start.2 = (f32[8,128,256]{2,1,0:T(8,128)S(1)}, f32[8,128,256]{2,1,0:T(8,128)}, u32[]{:S(2)}) copy-start(f32[8,128,256]{2,1,0:T(8,128)} %param.7) | copy-start | bytes 3145732
  13.0 27.1 %all-to-all-start = ((f32[128,6,128]{2,1,0:T(8,128)}), f32[128,6,128]{2,1,0:T(8,128)S(1)}, u32[]{:S(2)}, u32[]{:S(2)}) async-start(f32[128,6,128]{2,1,0:T(8,128)} %select_select_fusion), calls=%async_computation | async-start | bytes 1048576 | tf_op jit(solution)/shard_map/all_to_all | solution.py:98
  40.1 1.6 copy-start.1
  59.3 14.3 %all-to-all-start.2 = ((f32[128,2,128]{2,1,0:T(2,128)}), f32[128,2,128]{2,1,0:T(2,128)S(1)}, u32[]{:S(2)}, u32[]{:S(2)}) async-start(f32[128,2,128]{2,1,0:T(2,128)} %get-tuple-element.5), calls=%async_computation.3 | async-start | bytes 262144 | tf_op jit(solution)/shard_map/all_to_all | solution.py:107
  73.5 34.1 %all-to-all-start.1 = ((f32[16,6,8,256]{3,2,1,0:T(8,128)}), f32[16,6,8,256]{3,2,1,0:T(8,128)S(1)}, u32[]{:S(2)}, u32[]{:S(2)}) async-start(f32[16,6,8,256]{3,2,1,0:T(8,128)} %slice.11), calls=%async_computation.2 | async-start | bytes 1572864 | tf_op jit(solution)/shard_map/all_to_all | solution.py:105
  85.2 92.5 %reduce-scatter.2.cloned.1.call-start = ((), (), s32[]{:S(2)}) async-start(), calls=%async_computation.4 | async-start | bytes 278528 | tf_op jit(solution)/shard_map/reduce_scatter | solution.py:104
Sparse Core Ops, SparseCore 0:
  90.1 87.5 reduce-scatter.1

commit v5 on v3

--- a/solution.py
+++ b/solution.py
@@ -20,10 +20,37 @@
     return jnp.where(inside, jnp.exp(kernel_beta * (root_term - 1.0)), 0.0)
 
 
-def _grid_kernel(labels_ref, data_ref, tiles_ref, res_ref, grad_ref):
+def _kernels(data, width, cells):
+    ku_t = spheroid(cells - data[3:4, :]).astype(jnp.bfloat16)
+    kv_t = spheroid(cells - data[4:5, :]).astype(jnp.bfloat16).astype(jnp.float32)
+    return ku_t, kv_t
+
+
+def _degrid_kernel(labels_ref, data_ref, tiles_ref, res_ref):
     slots = data_ref.shape[0]
-    chunks, _, rows, _ = grad_ref.shape
     width = tiles_ref.shape[2]
+    vis = data_ref.shape[2]
+    cells = lax.broadcasted_iota(jnp.int32, (width, vis), 0).astype(jnp.float32)
+
+    def body(s, carry):
+        d = data_ref[s]
+        ku_t, kv_t = _kernels(d, width, cells)
+        proj_t = jnp.dot(tiles_ref[labels_ref[s]], ku_t, preferred_element_type=jnp.float32)
+        model_re = jnp.sum(proj_t[:width] * kv_t, axis=0, keepdims=True)
+        model_im = jnp.sum(proj_t[width:] * kv_t, axis=0, keepdims=True)
+        weight = d[2:3, :]
+        res_re = weight * (model_re - d[0:1, :])
+        res_im = weight * (model_im - d[1:2, :])
+        res_ref[s] = jnp.concatenate([res_re, res_im], axis=0)
+        return carry
+
+    lax.fori_loop(0, slots, body, 0, unroll=16)
+
+
+def _spread_kernel(labels_ref, data_ref, res_ref, grad_ref):
+    slots = data_ref.shape[0]
+    chunks, _, rows, wide = grad_ref.shape
+    width = wide // 2
     vis = data_ref.shape[2]
     grad_ref[...] = jnp.zeros(grad_ref.shape, grad_ref.dtype)
     cells = lax.broadcasted_iota(jnp.int32, (width, vis), 0).astype(jnp.float32)
@@ -31,42 +58,45 @@
     def body(s, carry):
         d = data_ref[s]
         tile = labels_ref[s]
-        ku_t = spheroid(cells - d[3:4, :]).astype(jnp.bfloat16)
-        kv_t = spheroid(cells - d[4:5, :]).astype(jnp.bfloat16).astype(jnp.float32)
-        proj_t = jnp.dot(tiles_ref[tile], ku_t, preferred_element_type=jnp.float32)
-        model_re = jnp.sum(proj_t[:width] * kv_t, axis=0, keepdims=True)
-        model_im = jnp.sum(proj_t[width:] * kv_t, axis=0, keepdims=True)
-        weight = d[2:3, :]
-        res_re = weight * (model_re - d[0:1, :])
-        res_im = weight * (model_im - d[1:2, :])
-        res_ref[s] = jnp.concatenate([res_re, res_im], axis=0)
-        spread_t = jnp.concatenate([res_re * kv_t, res_im * kv_t], axis=0).astype(jnp.bfloat16)
+        ku_t, kv_t = _kernels(d, width, cells)
+        r = res_ref[s]
+        spread_t = jnp.concatenate([r[0:1] * kv_t, r[1:2] * kv_t], axis=0).astype(jnp.bfloat16)
         contrib = lax.dot_general(
             ku_t, spread_t, (((1,), (1,)), ((), ())), preferred_element_type=jnp.float32
         )
-        grad_ref[:, pl.ds(tile, 1)] += contrib.reshape(chunks, 1, rows, 2 * width)
+        grad_ref[:, pl.ds(tile, 1)] += contrib.reshape(chunks, 1, rows, wide)
         return carry
 
     lax.fori_loop(0, slots, body, 0, unroll=16)
 
 
-def _grid_call(labels, data, tiles_t, chunks):
+def _degrid_call(labels, data, tiles_t):
     slots, _, vis = data.shape
-    tile_count, wide, width = tiles_t.shape
     vmem = pltpu.MemorySpace.VMEM
     return pl.pallas_call(
-        _grid_kernel,
-        out_shape=(
-            jax.ShapeDtypeStruct((slots, 2, vis), jnp.float32),
-            jax.ShapeDtypeStruct((chunks, tile_count, width // chunks, wide), jnp.float32),
-        ),
+        _degrid_kernel,
+        out_shape=jax.ShapeDtypeStruct((slots, 2, vis), jnp.float32),
         in_specs=[
             pl.BlockSpec(memory_space=pltpu.MemorySpace.SMEM),
             pl.BlockSpec(memory_space=vmem),
             pl.BlockSpec(memory_space=vmem),
         ],
-        out_specs=(pl.BlockSpec(memory_space=vmem), pl.BlockSpec(memory_space=vmem)),
+        out_specs=pl.BlockSpec(memory_space=vmem),
     )(labels, data, tiles_t)
+
+
+def _spread_call(labels, data, residual, tile_count, width, chunks):
+    vmem = pltpu.MemorySpace.VMEM
+    return pl.pallas_call(
+        _spread_kernel,
+        out_shape=jax.ShapeDtypeStruct((chunks, tile_count, width // chunks, 2 * width), jnp.float32),
+        in_specs=[
+            pl.BlockSpec(memory_space=pltpu.MemorySpace.SMEM),
+            pl.BlockSpec(memory_space=vmem),
+            pl.BlockSpec(memory_space=vmem),
+        ],
+        out_specs=pl.BlockSpec(memory_space=vmem),
+    )(labels, data, residual)
 
 
 def shards(grid, tile_list, owner_map, offsets, positions, observed, weights):
@@ -98,11 +128,12 @@
     incoming = lax.all_to_all(outgoing, "bl", split_axis=0, concat_axis=0, tiled=True)
     labels = jnp.max(incoming[:, 5, :], axis=1).astype(jnp.int32)
     tiles_t = jnp.swapaxes(grid.astype(jnp.bfloat16), 1, 2)
-    residual_all, gradient = _grid_call(labels, incoming, tiles_t, chan)
+    residual_all = _degrid_call(labels, incoming, tiles_t)
+    returned = lax.all_to_all(residual_all, "bl", split_axis=0, concat_axis=0, tiled=True)
+    gradient = _spread_call(labels, incoming, residual_all, tile_dev, tile_width, chan)
     share_rows = tile_width // chan
     parts = lax.all_to_all(gradient, "chan", split_axis=0, concat_axis=0, tiled=True)
     grad_share = jnp.sum(parts, axis=0)
-    returned = lax.all_to_all(residual_all, "bl", split_axis=0, concat_axis=0, tiled=True)
     my_residual = jnp.take(returned, send_slot, axis=0)[None]
     share_start = lax.axis_index("chan") * share_rows
     own_rows = lax.dynamic_slice_in_dim(grid, share_start, share_rows, 1)

time: 108 us -> 112 us (1.037)
  the two profiles are of different devices: /device:TPU:1 before, /device:TPU:72 now
where the time goes in v5:
time: 112 us; the launch traced here: 111 us
  waiting for transfers between devices  45.3 us (40%)
  Pallas kernels  29.4 us (26%)
  starting transfers between devices  25.2 us (22%)
  other arithmetic  5.72 us (5%)
  local copies, waits for them, and re-layouts  4.75 us (4%)
    all_to_all x1, waiting for transfers between devices, shards(): lax.all_to_all(gradient, 'chan', split_axis=0, concat_axis=0, tiled=True)  29.5 us
    all_to_all x1, waiting for transfers between devices, shards(): lax.all_to_all(outgoing, 'bl', split_axis=0, concat_axis=0, tiled=True)  15.8 us
    pallas_call x1, Pallas kernels, _degrid_call(): pl.pallas_call(_degrid_kernel, out_shape=jax.ShapeDtypeStruct((slots, 2,...  14.8 us
    pallas_call x1, Pallas kernels, _spread_call(): pl.pallas_call(_spread_kernel, out_shape=jax.ShapeDtypeStruct((chunks, ti...  14.6 us
    all_to_all x1, starting transfers between devices, shards(): lax.all_to_all(gradient, 'chan', split_axis=0, concat_axis=0, tiled=True)  12 us
    all_to_all x1, starting transfers between devices, shards(): lax.all_to_all(outgoing, 'bl', split_axis=0, concat_axis=0, tiled=True)  8.6 us
    all_to_all x1, starting transfers between devices, shards(): lax.all_to_all(residual_all, 'bl', split_axis=0, concat_axis=0, tiled=True)  4.61 us
    unnamed x17, local copies, waits for them, and re-layouts  2.32 us
  transfers between devices with their start and end apart: 3, of which 2 were waited for; matrix products, arithmetic and copies ran while one was open for 2% of the time, Pallas kernels for 13%

profile of v5, /device:TPU:72, one launch (start us, length us, event | category | flops | bytes accessed | tf_op | source)
XLA Modules:
  0.0 111.2 jit_solution(1494266585657602041)
XLA Ops:
  0.6 0.0 copy-start
  0.6 0.7 fusion.6
  1.3 0.0 copy-done
  1.3 0.0 copy-start.6
  1.3 0.8 gather_fusion
  2.1 0.0 copy-done.6
  2.1 0.1 fusion.1
  2.2 0.0 copy-start.4
  2.2 0.1 reduce_window_sum.11
  2.3 0.2 select_reduce_fusion.1
  2.5 0.1 select_reduce_fusion
  2.6 0.1 fusion
  2.7 0.0 copy-start.7
  2.8 0.7 copy-done.7
  3.4 0.1 copy.15
  3.5 0.0 copy-done.4
  3.5 0.0 copy-start.3
  3.5 0.1 bitcast_add_fusion
  3.7 0.0 copy-start.5
  3.7 0.1 broadcast_in_dim.74
  3.8 0.6 copy-done.3
  4.4 0.1 copy-done.5
  4.5 0.1 pad_maximum_fusion
  4.6 0.8 gather_fusion.1
  5.3 0.0 copy-start.2
  5.4 1.1 %select_select_fusion = f32[128,6,128]{2,1,0:T(8,128)} fusion(f32[128,6,128]{2,1,0:T(8,128)S(1)} %gather_fusion.1, pred[128]{0:T(512)(128)(4,1)S(1)} %compare_and_fusion.1, pred[128]{0:T(512)(128)(4,1)S(1)} %fusion), kind=kLoop, calls=%fused_computation.4 | loop fusion | flops 196608 | bytes 786688 | tf_op jit(solution)/shard_map/jit(_where)/select_n | solution.py:127
  6.5 8.6 %all-to-all-start = ((f32[128,6,128]{2,1,0:T(8,128)}), f32[128,6,128]{2,1,0:T(8,128)S(1)}, u32[]{:S(2)}, u32[]{:S(2)}) async-start(f32[128,6,128]{2,1,0:T(8,128)} %select_select_fusion), calls=%async_computation | async-start | bytes 1048576 | tf_op jit(solution)/shard_map/all_to_all | solution.py:128
  15.1 0.0 copy-done.2
  15.1 1.0 copy.17
  16.1 15.8 %all-to-all-done.data_ref = f32[128,6,128]{2,1,0:T(8,128)S(1)} async-done(((f32[128,6,128]{2,1,0:T(8,128)}), f32[128,6,128]{2,1,0:T(8,128)S(1)}, u32[]{:S(2)}, u32[]{:S(2)}) %all-to-all-start) | async-done | bytes 393248 | tf_op jit(solution)/shard_map/all_to_all | solution.py:128
  31.9 0.0 copy-start.1
  31.9 1.0 slice_reduce_fusion
  33.0 0.5 convert_element_type.30.labels_ref
  33.5 0.0 copy-done.1
  33.5 14.8 %shard_map.86.res_ref = f32[128,2,128]{2,1,0:T(2,128)} custom-call(s32[128]{0:T(128)} %convert_element_type.30.labels_ref, f32[128,6,128]{2,1,0:T(8,128)} %copy-done.1, bf16[8,256,128]{2,1,0:T(8,128)(2,1)} %bitcast.48), custom_call_target="tpu_custom_call" | custom-call | tf_op jit(solution)/shard_map/pallas_call | solution.py:76
  48.3 4.6 %all-to-all-start.2 = ((f32[128,2,128]{2,1,0:T(2,128)}), f32[128,2,128]{2,1,0:T(2,128)S(1)}, u32[]{:S(2)}, u32[]{:S(2)}) async-start(f32[128,2,128]{2,1,0:T(2,128)} %shard_map.86.res_ref), calls=%async_computation.2 | async-start | bytes 262144 | tf_op jit(solution)/shard_map/all_to_all | solution.py:132
  52.9 14.6 %shard_map.87 = f32[16,8,8,256]{3,2,1,0:T(8,128)} custom-call(s32[128]{0:T(128)} %convert_element_type.30.labels_ref, f32[128,6,128]{2,1,0:T(8,128)} %copy-done.1, f32[128,2,128]{2,1,0:T(2,128)} %shard_map.86.res_ref), custom_call_target="tpu_custom_call" | custom-call | tf_op jit(solution)/shard_map/pallas_call | solution.py:90
  67.5 0.0 all-to-all-done.2
  67.5 12.0 %all-to-all-start.1 = ((f32[16,8,8,256]{3,2,1,0:T(8,128)}), f32[16,8,8,256]{3,2,1,0:T(8,128)S(1)}, u32[]{:S(2)}, u32[]{:S(2)}) async-start(f32[16,8,8,256]{3,2,1,0:T(8,128)} %shard_map.87), calls=%async_computation.1 | async-start | bytes 2097152 | tf_op jit(solution)/shard_map/all_to_all | solution.py:135
  79.5 0.7 gather_fusion.2
  80.2 0.8 bitcast_select_fusion
  81.0 29.5 %all-to-all-done.1 = f32[16,8,8,256]{3,2,1,0:T(8,128)S(1)} async-done(((f32[16,8,8,256]{3,2,1,0:T(8,128)}), f32[16,8,8,256]{3,2,1,0:T(8,128)S(1)}, u32[]{:S(2)}, u32[]{:S(2)}) %all-to-all-start.1) | async-done | bytes 1048608 | tf_op jit(solution)/shard_map/all_to_all | solution.py:135
  110.5 0.1 reduce_sum.37
  110.5 0.6 add_subtract_fusion
  (11 shorter events, 0.1 us)
Async XLA Ops:
  0.6 0.7 copy-start
  1.3 0.8 copy-start.6
  2.2 1.3 %copy-start.4 = (f32[1,64,2,128]{3,2,1,0:T(2,128)S(1)}, f32[1,64,2,128]{3,2,1,0:T(2,128)}, u32[]{:S(2)}) copy-start(f32[1,64,2,128]{3,2,1,0:T(2,128)} %param.11) | copy-start | bytes 196612
  2.7 0.7 copy-start.7
  3.5 0.8 copy-start.3
  3.7 0.8 copy-start.5
  5.3 9.8 %copy-start.2 = (f32[8,128,256]{2,1,0:T(8,128)S(1)}, f32[8,128,256]{2,1,0:T(8,128)}, u32[]{:S(2)}) copy-start(f32[8,128,256]{2,1,0:T(8,128)} %param.7) | copy-start | bytes 3145732
  6.5 25.4 %all-to-all-start = ((f32[128,6,128]{2,1,0:T(8,128)}), f32[128,6,128]{2,1,0:T(8,128)S(1)}, u32[]{:S(2)}, u32[]{:S(2)}) async-start(f32[128,6,128]{2,1,0:T(8,128)} %select_select_fusion), calls=%async_computation | async-start | bytes 1048576 | tf_op jit(solution)/shard_map/all_to_all | solution.py:128
  31.9 1.6 %copy-start.1 = (f32[128,6,128]{2,1,0:T(8,128)}, f32[128,6,128]{2,1,0:T(8,128)S(1)}, u32[]{:S(2)}) copy-start(f32[128,6,128]{2,1,0:T(8,128)S(1)} %all-to-all-done.data_ref) | copy-start | bytes 1179652
  48.3 19.2 %all-to-all-start.2 = ((f32[128,2,128]{2,1,0:T(2,128)}), f32[128,2,128]{2,1,0:T(2,128)S(1)}, u32[]{:S(2)}, u32[]{:S(2)}) async-start(f32[128,2,128]{2,1,0:T(2,128)} %shard_map.86.res_ref), calls=%async_computation.2 | async-start | bytes 262144 | tf_op jit(solution)/shard_map/all_to_all | solution.py:132
  67.5 43.0 %all-to-all-start.1 = ((f32[16,8,8,256]{3,2,1,0:T(8,128)}), f32[16,8,8,256]{3,2,1,0:T(8,128)S(1)}, u32[]{:S(2)}, u32[]{:S(2)}) async-start(f32[16,8,8,256]{3,2,1,0:T(8,128)} %shard_map.87), calls=%async_computation.1 | async-start | bytes 2097152 | tf_op jit(solution)/shard_map/all_to_all | solution.py:135

commit v6 on v3

--- a/solution.py
+++ b/solution.py
@@ -20,19 +20,27 @@
     return jnp.where(inside, jnp.exp(kernel_beta * (root_term - 1.0)), 0.0)
 
 
+def _spheroid_scaled(scaled):
+    inside = scaled * scaled < 1.0
+    rest = 1.0 - scaled * scaled
+    root_term = rest * lax.rsqrt(rest)
+    return jnp.where(inside, jnp.exp(kernel_beta * (root_term - 1.0)), 0.0)
+
+
 def _grid_kernel(labels_ref, data_ref, tiles_ref, res_ref, grad_ref):
     slots = data_ref.shape[0]
     chunks, _, rows, _ = grad_ref.shape
     width = tiles_ref.shape[2]
     vis = data_ref.shape[2]
     grad_ref[...] = jnp.zeros(grad_ref.shape, grad_ref.dtype)
-    cells = lax.broadcasted_iota(jnp.int32, (width, vis), 0).astype(jnp.float32)
+    cells = lax.broadcasted_iota(jnp.int32, (width, vis), 0).astype(jnp.float32) * (1.0 / half_support)
 
     def body(s, carry):
         d = data_ref[s]
         tile = labels_ref[s]
-        ku_t = spheroid(cells - d[3:4, :]).astype(jnp.bfloat16)
-        kv_t = spheroid(cells - d[4:5, :]).astype(jnp.bfloat16).astype(jnp.float32)
+        quarter = d[3:5, :] * (1.0 / half_support)
+        ku_t = _spheroid_scaled(cells - quarter[0:1]).astype(jnp.bfloat16)
+        kv_t = _spheroid_scaled(cells - quarter[1:2]).astype(jnp.bfloat16).astype(jnp.float32)
         proj_t = jnp.dot(tiles_ref[tile], ku_t, preferred_element_type=jnp.float32)
         model_re = jnp.sum(proj_t[:width] * kv_t, axis=0, keepdims=True)
         model_im = jnp.sum(proj_t[width:] * kv_t, axis=0, keepdims=True)

time: 108 us -> 105 us (0.972)
  Pallas kernels: 17.6 us -> 14.5 us
    pallas_call x1, Pallas kernels: 17.6 us -> 14.5 us  [_grid_call(): pl.pallas_call(_grid_kernel, out_shape=(jax.ShapeDtypeStruct((slots, 2, v...]
where the time goes in v6:
time: 105 us
  waiting for transfers between devices  42.5 us (40%)
  starting transfers between devices  22.2 us (21%)
  Pallas kernels  14.5 us (14%)
  blocking collectives  14.3 us (14%)
  other arithmetic  5.7 us (5%)
  local copies, waits for them, and re-layouts  4.77 us (5%)
    all_to_all x1, waiting for transfers between devices, shards(): lax.all_to_all(gradient, 'chan', split_axis=0, concat_axis=0, tiled=True)  27 us
    all_to_all x1, waiting for transfers between devices, shards(): lax.all_to_all(outgoing, 'bl', split_axis=0, concat_axis=0, tiled=True)  15.5 us
    pallas_call x1, Pallas kernels, _grid_call(): pl.pallas_call(_grid_kernel, out_shape=(jax.ShapeDtypeStruct((slots, 2, v...  14.5 us
    all_to_all x1, blocking collectives, shards(): lax.all_to_all(residual_all, 'bl', split_axis=0, concat_axis=0, tiled=True)  14.3 us
    all_to_all x1, starting transfers between devices, shards(): lax.all_to_all(gradient, 'chan', split_axis=0, concat_axis=0, tiled=True)  11.7 us
    all_to_all x1, starting transfers between devices, shards(): lax.all_to_all(outgoing, 'bl', split_axis=0, concat_axis=0, tiled=True)  10.6 us
    unnamed x17, local copies, waits for them, and re-layouts  2.35 us
  transfers between devices with their start and end apart: 2, of which 2 were waited for; matrix products, arithmetic and copies ran while one was open for 2% of the time, Pallas kernels for 0%

profile of v6, /device:TPU:1, one launch (start us, length us, event | category | flops | bytes accessed | tf_op | source)
XLA Modules:
  0.0 104.8 jit_solution(6990876026479189198)
XLA Ops:
  0.6 0.0 copy-start
  0.6 0.7 fusion.6
  1.3 0.0 copy-done
  1.3 0.0 copy-start.6
  1.3 0.8 gather_fusion
  2.1 0.0 copy-done.6
  2.1 0.1 fusion.1
  2.2 0.0 copy-start.4
  2.2 0.1 reduce_window_sum.11
  2.3 0.2 select_reduce_fusion.1
  2.5 0.1 select_reduce_fusion
  2.6 0.1 fusion
  2.7 0.0 copy-start.7
  2.8 0.7 copy-done.7
  3.4 0.1 copy.15
  3.5 0.0 copy-done.4
  3.5 0.0 copy-start.3
  3.5 0.1 bitcast_add_fusion
  3.7 0.0 copy-start.5
  3.7 0.1 broadcast_in_dim.74
  3.8 0.6 copy-done.3
  4.4 0.1 copy-done.5
  4.4 0.1 pad_maximum_fusion
  4.6 0.8 gather_fusion.1
  5.3 0.0 copy-start.2
  5.4 1.1 %select_select_fusion = f32[128,6,128]{2,1,0:T(8,128)} fusion(f32[128,6,128]{2,1,0:T(8,128)S(1)} %gather_fusion.1, pred[128]{0:T(512)(128)(4,1)S(1)} %compare_and_fusion.1, pred[128]{0:T(512)(128)(4,1)S(1)} %fusion), kind=kLoop, calls=%fused_computation.4 | loop fusion | flops 196608 | bytes 786688 | tf_op jit(solution)/shard_map/jit(_where)/select_n | solution.py:105
  6.5 10.6 %all-to-all-start = ((f32[128,6,128]{2,1,0:T(8,128)}), f32[128,6,128]{2,1,0:T(8,128)S(1)}, u32[]{:S(2)}, u32[]{:S(2)}) async-start(f32[128,6,128]{2,1,0:T(8,128)} %select_select_fusion), calls=%async_computation | async-start | bytes 1048576 | tf_op jit(solution)/shard_map/all_to_all | solution.py:106
  17.0 0.0 copy-done.2
  17.1 1.0 copy.17
  18.1 15.5 %all-to-all-done.data_ref = f32[128,6,128]{2,1,0:T(8,128)S(1)} async-done(((f32[128,6,128]{2,1,0:T(8,128)}), f32[128,6,128]{2,1,0:T(8,128)S(1)}, u32[]{:S(2)}, u32[]{:S(2)}) %all-to-all-start) | async-done | bytes 393248 | tf_op jit(solution)/shard_map/all_to_all | solution.py:106
  33.6 0.0 copy-start.1
  33.6 1.0 slice_reduce_fusion
  34.6 0.5 convert_element_type.30.labels_ref
  35.2 0.0 copy-done.1
  35.2 14.5 %shard_map.86 = (f32[128,2,128]{2,1,0:T(2,128)}, f32[16,8,8,256]{3,2,1,0:T(8,128)}) custom-call(s32[128]{0:T(128)} %convert_element_type.30.labels_ref, f32[128,6,128]{2,1,0:T(8,128)} %copy-done.1, bf16[8,256,128]{2,1,0:T(8,128)(2,1)} %bitcast.48), custom_call_target="tpu_custom_call" | custom-call | tf_op jit(solution)/shard_map/pallas_call | solution.py:65
  49.6 14.3 %all_to_all.15 = f32[128,2,128]{2,1,0:T(2,128)S(1)} all-to-all(f32[128,2,128]{2,1,0:T(2,128)} %get-tuple-element.5), channel_id=1, replica_groups=mesh['chan'=16,'bl'=32] {'bl'}, dimensions={0} | all-to-all | bytes 262144 | tf_op jit(solution)/shard_map/all_to_all | solution.py:113
  63.9 11.7 %all-to-all-start.1 = ((f32[16,8,8,256]{3,2,1,0:T(8,128)}), f32[16,8,8,256]{3,2,1,0:T(8,128)S(1)}, u32[]{:S(2)}, u32[]{:S(2)}) async-start(f32[16,8,8,256]{3,2,1,0:T(8,128)} %get-tuple-element.4), calls=%async_computation.1 | async-start | bytes 2097152 | tf_op jit(solution)/shard_map/all_to_all | solution.py:111
  75.6 0.7 gather_fusion.2
  76.3 0.8 bitcast_select_fusion
  77.1 27.0 %all-to-all-done.1 = f32[16,8,8,256]{3,2,1,0:T(8,128)S(1)} async-done(((f32[16,8,8,256]{3,2,1,0:T(8,128)}), f32[16,8,8,256]{3,2,1,0:T(8,128)S(1)}, u32[]{:S(2)}, u32[]{:S(2)}) %all-to-all-start.1) | async-done | bytes 1048608 | tf_op jit(solution)/shard_map/all_to_all | solution.py:111
  104.1 0.1 reduce_sum.37
  104.2 0.6 add_subtract_fusion
  (11 shorter events, 0.1 us)
Async XLA Ops:
  0.6 0.7 copy-start
  1.3 0.8 copy-start.6
  2.2 1.3 %copy-start.4 = (f32[1,64,2,128]{3,2,1,0:T(2,128)S(1)}, f32[1,64,2,128]{3,2,1,0:T(2,128)}, u32[]{:S(2)}) copy-start(f32[1,64,2,128]{3,2,1,0:T(2,128)} %param.11) | copy-start | bytes 196612
  2.7 0.7 copy-start.7
  3.5 0.8 copy-start.3
  3.7 0.8 copy-start.5
  5.3 11.7 %copy-start.2 = (f32[8,128,256]{2,1,0:T(8,128)S(1)}, f32[8,128,256]{2,1,0:T(8,128)}, u32[]{:S(2)}) copy-start(f32[8,128,256]{2,1,0:T(8,128)} %param.7) | copy-start | bytes 3145732
  6.5 27.1 %all-to-all-start = ((f32[128,6,128]{2,1,0:T(8,128)}), f32[128,6,128]{2,1,0:T(8,128)S(1)}, u32[]{:S(2)}, u32[]{:S(2)}) async-start(f32[128,6,128]{2,1,0:T(8,128)} %select_select_fusion), calls=%async_computation | async-start | bytes 1048576 | tf_op jit(solution)/shard_map/all_to_all | solution.py:106
  33.6 1.6 %copy-start.1 = (f32[128,6,128]{2,1,0:T(8,128)}, f32[128,6,128]{2,1,0:T(8,128)S(1)}, u32[]{:S(2)}) copy-start(f32[128,6,128]{2,1,0:T(8,128)S(1)} %all-to-all-done.data_ref) | copy-start | bytes 1179652
  63.9 40.2 %all-to-all-start.1 = ((f32[16,8,8,256]{3,2,1,0:T(8,128)}), f32[16,8,8,256]{3,2,1,0:T(8,128)S(1)}, u32[]{:S(2)}, u32[]{:S(2)}) async-start(f32[16,8,8,256]{3,2,1,0:T(8,128)} %get-tuple-element.4), calls=%async_computation.1 | async-start | bytes 2097152 | tf_op jit(solution)/shard_map/all_to_all | solution.py:111

commit v7 on v6

--- a/solution.py
+++ b/solution.py
@@ -77,6 +77,35 @@
     )(labels, data, tiles_t)
 
 
+def _ring_pairs(size_hi, size_lo, shift, along_lo):
+    pairs = []
+    for hi in range(size_hi):
+        for lo in range(size_lo):
+            if along_lo:
+                pairs.append((hi * size_lo + lo, hi * size_lo + (lo + shift) % size_lo))
+            else:
+                pairs.append((hi * size_lo + lo, ((hi + shift) % size_hi) * size_lo + lo))
+    return pairs
+
+
+def _chan_reduce(gradient):
+    chunks = gradient.shape[0]
+    size_lo = 4
+    size_hi = chunks // size_lo
+    c = lax.axis_index("chan")
+    hi, lo = c // size_lo, c % size_lo
+    parts = gradient.reshape((size_hi, size_lo) + gradient.shape[1:])
+    acc = lax.dynamic_index_in_dim(parts, lo, 1, keepdims=False)
+    for k in range(1, size_lo):
+        piece = lax.dynamic_index_in_dim(parts, (lo + k) % size_lo, 1, keepdims=False)
+        acc = acc + lax.ppermute(piece, "chan", _ring_pairs(size_hi, size_lo, k, True))
+    out = lax.dynamic_index_in_dim(acc, hi, 0, keepdims=False)
+    for k in range(1, size_hi):
+        piece = lax.dynamic_index_in_dim(acc, (hi + k) % size_hi, 0, keepdims=False)
+        out = out + lax.ppermute(piece, "chan", _ring_pairs(size_hi, size_lo, k, False))
+    return out
+
+
 def shards(grid, tile_list, owner_map, offsets, positions, observed, weights):
     owners = lax.axis_size("bl")
     chan = lax.axis_size("chan")
@@ -108,8 +137,7 @@
     tiles_t = jnp.swapaxes(grid.astype(jnp.bfloat16), 1, 2)
     residual_all, gradient = _grid_call(labels, incoming, tiles_t, chan)
     share_rows = tile_width // chan
-    parts = lax.all_to_all(gradient, "chan", split_axis=0, concat_axis=0, tiled=True)
-    grad_share = jnp.sum(parts, axis=0)
+    grad_share = _chan_reduce(gradient)
     returned = lax.all_to_all(residual_all, "bl", split_axis=0, concat_axis=0, tiled=True)
     my_residual = jnp.take(returned, send_slot, axis=0)[None]
     share_start = lax.axis_index("chan") * share_rows

time: 105 us -> 99.1 us (0.944)
  the two profiles are of different devices: /device:TPU:1 before, /device:TPU:10 now
where the time goes in v7:
time: 99.1 us; the launch traced here: 98.5 us
  starting transfers between devices  42 us (42%)
  waiting for transfers between devices  28.4 us (29%)
  Pallas kernels  14.5 us (15%)
  other arithmetic  6.68 us (7%)
  local copies, waits for them, and re-layouts  5.99 us (6%)
  between operations  1.03 us (1%)
    ppermute x3, starting transfers between devices, _chan_reduce(): lax.ppermute(piece, 'chan', _ring_pairs(size_hi, size_lo, k, False))  18 us
    all_to_all x1, waiting for transfers between devices, shards(): lax.all_to_all(outgoing, 'bl', split_axis=0, concat_axis=0, tiled=True)  15.7 us
    pallas_call x1, Pallas kernels, _grid_call(): pl.pallas_call(_grid_kernel, out_shape=(jax.ShapeDtypeStruct((slots, 2, v...  14.5 us
    ppermute x3, starting transfers between devices, _chan_reduce(): lax.ppermute(piece, 'chan', _ring_pairs(size_hi, size_lo, k, True))  9.9 us
    all_to_all x1, starting transfers between devices, shards(): lax.all_to_all(outgoing, 'bl', split_axis=0, concat_axis=0, tiled=True)  9.51 us
    ppermute x3, waiting for transfers between devices, _chan_reduce(): lax.ppermute(piece, 'chan', _ring_pairs(size_hi, size_lo, k, True))  8.92 us
    all_to_all x1, starting transfers between devices, shards(): lax.all_to_all(residual_all, 'bl', split_axis=0, concat_axis=0, tiled=True)  4.6 us
    ppermute x3, waiting for transfers between devices, _chan_reduce(): lax.ppermute(piece, 'chan', _ring_pairs(size_hi, size_lo, k, False))  3.79 us
  transfers between devices with their start and end apart: 8, of which 4 were waited for; matrix products, arithmetic and copies ran while one was open for 4% of the time, Pallas kernels for 0%

profile of v7, /device:TPU:10, one launch (start us, length us, event | category | flops | bytes accessed | tf_op | source)
XLA Modules:
  0.0 98.5 jit_solution(18249306041705963974)
XLA Ops:
  0.6 0.0 copy-start
  0.6 0.7 fusion.12
  1.3 0.0 copy-done
  1.3 0.0 copy-start.6
  1.3 0.8 gather_fusion
  2.1 0.0 copy-done.6
  2.1 0.1 fusion.7
  2.2 0.0 copy-start.4
  2.2 0.1 reduce_window_sum.11
  2.3 0.2 select_reduce_fusion.1
  2.5 0.1 select_reduce_fusion
  2.6 0.1 fusion.6
  2.7 0.0 copy-start.7
  2.8 0.7 copy-done.7
  3.4 0.1 copy.15
  3.5 0.0 copy-done.4
  3.5 0.0 copy-start.3
  3.5 0.1 bitcast_add_fusion.2
  3.7 0.0 copy-start.5
  3.7 0.1 broadcast_in_dim.74
  3.8 0.6 copy-done.3
  4.4 0.1 copy-done.5
  4.5 0.1 pad_maximum_fusion
  4.6 0.8 gather_fusion.1
  5.3 0.0 copy-start.2
  5.4 1.1 %select_select_fusion = f32[128,6,128]{2,1,0:T(8,128)} fusion(f32[128,6,128]{2,1,0:T(8,128)S(1)} %gather_fusion.1, pred[128]{0:T(512)(128)(4,1)S(1)} %compare_and_fusion.1, pred[128]{0:T(512)(128)(4,1)S(1)} %fusion.6), kind=kLoop, calls=%fused_computation.4 | loop fusion | flops 196608 | bytes 786688 | tf_op jit(solution)/shard_map/jit(_where)/select_n | solution.py:134
  6.5 9.5 %all-to-all-start = ((f32[128,6,128]{2,1,0:T(8,128)}), f32[128,6,128]{2,1,0:T(8,128)S(1)}, u32[]{:S(2)}, u32[]{:S(2)}) async-start(f32[128,6,128]{2,1,0:T(8,128)} %select_select_fusion), calls=%async_computation | async-start | bytes 1048576 | tf_op jit(solution)/shard_map/all_to_all | solution.py:135
  16.1 0.0 copy-done.2
  16.1 1.0 %copy.17 = bf16[8,128,256]{1,2,0:T(8,128)(2,1)} copy(f32[8,128,256]{2,1,0:T(8,128)S(1)} %copy-done.2) | data formatting | bytes 1572864 | tf_op args[0]
  17.1 15.7 %all-to-all-done.data_ref = f32[128,6,128]{2,1,0:T(8,128)S(1)} async-done(((f32[128,6,128]{2,1,0:T(8,128)}), f32[128,6,128]{2,1,0:T(8,128)S(1)}, u32[]{:S(2)}, u32[]{:S(2)}) %all-to-all-start) | async-done | bytes 393248 | tf_op jit(solution)/shard_map/all_to_all | solution.py:135
  32.8 0.0 copy-start.1
  32.8 1.0 %slice_reduce_fusion = f32[128]{0:T(128)S(1)} fusion(f32[128,6,128]{2,1,0:T(8,128)S(1)} %all-to-all-done.data_ref), kind=kLoop, calls=%fused_computation.12 | loop fusion | flops 16256 | bytes 66048 | tf_op jit(solution)/shard_map/reduce_max | solution.py:136
  33.8 0.5 convert_element_type.30.labels_ref
  34.3 0.0 copy-done.1
  34.3 14.5 %shard_map.86 = (f32[128,2,128]{2,1,0:T(2,128)}, f32[16,8,8,256]{3,2,1,0:T(8,128)}) custom-call(s32[128]{0:T(128)} %convert_element_type.30.labels_ref, f32[128,6,128]{2,1,0:T(8,128)} %copy-done.1, bf16[8,256,128]{2,1,0:T(8,128)(2,1)} %bitcast.77), custom_call_target="tpu_custom_call" | custom-call | tf_op jit(solution)/shard_map/pallas_call | solution.py:65
  48.8 4.6 %all-to-all-start.1 = ((f32[128,2,128]{2,1,0:T(2,128)}), f32[128,2,128]{2,1,0:T(2,128)S(1)}, u32[]{:S(2)}, u32[]{:S(2)}) async-start(f32[128,2,128]{2,1,0:T(2,128)} %get-tuple-element.5), calls=%async_computation.1 | async-start | bytes 262144 | tf_op jit(solution)/shard_map/all_to_all | solution.py:141
  53.4 1.2 %dynamic-slice_bitcast_fusion.2 = (f32[4,8,8,256]{3,2,1,0:T(8,128)S(1)}, f32[4,8,8,256]{3,2,1,0:T(8,128)S(1)}, f32[4,8,8,256]{3,2,1,0:T(8,128)S(1)}) fusion(f32[4,4,8,8,256]{4,3,2,1,0:T(8,128)} %bitcast.78, s32[]{:T(128)S(6)} %select_n.223, s32[]{:T(128)S(6)} %select_n.227, s32[]{:T(128)S(6)} %select_n.225), kind=kLoop, calls=%fused_computation.11 | loop fusion | bytes 1572876 | tf_op jit(solution)/shard_map/jit(dynamic_index_in_dim)/squeeze | solution.py:100
  54.6 3.4 %collective-permute-start = (f32[4,8,8,256]{3,2,1,0:T(8,128)S(1)}, f32[4,8,8,256]{3,2,1,0:T(8,128)S(1)}, u32[]{:S(2)}, u32[]{:S(2)}) collective-permute-start(f32[4,8,8,256]{3,2,1,0:T(8,128)S(1)} %get-tuple-element.8), channel_id=1, source_target_pairs={{0,32},{32,64},{64,96},{96,0},{128,160},{160,192},{192,224},{224,1... | collective-permute-start | bytes 786440 | tf_op jit(solution)/shard_map/ppermute | solution.py:101
  58.1 2.4 %collective-permute-start.2 = (f32[4,8,8,256]{3,2,1,0:T(8,128)S(1)}, f32[4,8,8,256]{3,2,1,0:T(8,128)S(1)}, u32[]{:S(2)}, u32[]{:S(2)}) collective-permute-start(f32[4,8,8,256]{3,2,1,0:T(8,128)S(1)} %get-tuple-element.9), channel_id=1, source_target_pairs={{0,96},{32,0},{64,32},{96,64},{128,224},{160,128},{192,160},{224,1... | collective-permute-start | bytes 786440 | tf_op jit(solution)/shard_map/ppermute | solution.py:101
  60.5 4.1 %collective-permute-start.1 = (f32[4,8,8,256]{3,2,1,0:T(8,128)S(1)}, f32[4,8,8,256]{3,2,1,0:T(8,128)S(1)}, u32[]{:S(2)}, u32[]{:S(2)}) collective-permute-start(f32[4,8,8,256]{3,2,1,0:T(8,128)S(1)} %get-tuple-element.10), channel_id=1, source_target_pairs={{0,64},{32,96},{64,0},{96,32},{128,192},{160,224},{192,128},{224,1... | collective-permute-start | bytes 786440 | tf_op jit(solution)/shard_map/ppermute | solution.py:101
  64.7 0.0 all-to-all-done.1
  64.7 0.7 gather_fusion.2
  65.3 0.0 collective-permute-done
  65.3 3.1 %collective-permute-done.2 = f32[4,8,8,256]{3,2,1,0:T(8,128)S(1)} collective-permute-done((f32[4,8,8,256]{3,2,1,0:T(8,128)S(1)}, f32[4,8,8,256]{3,2,1,0:T(8,128)S(1)}, u32[]{:S(2)}, u32[]{:S(2)}) %collective-permute-start.2) | collective-permute-done | bytes 262176 | tf_op jit(solution)/shard_map/ppermute | solution.py:101
  68.5 5.8 %collective-permute-done.1 = f32[4,8,8,256]{3,2,1,0:T(8,128)S(1)} collective-permute-done((f32[4,8,8,256]{3,2,1,0:T(8,128)S(1)}, f32[4,8,8,256]{3,2,1,0:T(8,128)S(1)}, u32[]{:S(2)}, u32[]{:S(2)}) %collective-permute-start.1) | collective-permute-done | bytes 262176 | tf_op jit(solution)/shard_map/ppermute | solution.py:101
  74.3 1.0 %fusion.1 = f32[4,8,8,256]{3,2,1,0:T(8,128)S(1)} fusion(f32[4,8,8,256]{3,2,1,0:T(8,128)S(1)} %collective-permute-done.2, f32[4,8,8,256]{3,2,1,0:T(8,128)S(1)} %collective-permute-done.1, f32[4,8,8,256]{3,2,1,0:T(8,128)S(1)} %collective-permute-done, f32[4,4,8,8,256]{4,3,2,1,0:T(8,128)} %bitcast.79, s32[]{:T(128)S(6)} %select_n.221), kind=kLoop, calls=%fused_computation.8 | loop fusion | flops 196608 | bytes 1310724 | tf_op jit(solution)/shard_map/add | solution.py:101
  75.3 6.1 %collective-permute-start.3 = (f32[8,8,256]{2,1,0:T(8,128)S(1)}, f32[8,8,256]{2,1,0:T(8,128)S(1)}, u32[]{:S(2)}, u32[]{:S(2)}) collective-permute-start(f32[8,8,256]{2,1,0:T(8,128)S(1)} %get-tuple-element.11), channel_id=1, source_target_pairs={{0,128},{32,160},{64,192},{96,224},{128,256},{160,288},{192,320},{... | collective-permute-start | bytes 196616 | tf_op jit(solution)/shard_map/ppermute | solution.py:105
  81.4 5.9 %collective-permute-start.5 = (f32[8,8,256]{2,1,0:T(8,128)S(1)}, f32[8,8,256]{2,1,0:T(8,128)S(1)}, u32[]{:S(2)}, u32[]{:S(2)}) collective-permute-start(f32[8,8,256]{2,1,0:T(8,128)S(1)} %get-tuple-element.12), channel_id=1, source_target_pairs={{0,384},{32,416},{64,448},{96,480},{128,0},{160,32},{192,64},{224,... | collective-permute-start | bytes 196616 | tf_op jit(solution)/shard_map/ppermute | solution.py:105
  87.3 6.0 %collective-permute-start.4 = (f32[8,8,256]{2,1,0:T(8,128)S(1)}, f32[8,8,256]{2,1,0:T(8,128)S(1)}, u32[]{:S(2)}, u32[]{:S(2)}) collective-permute-start(f32[8,8,256]{2,1,0:T(8,128)S(1)} %get-tuple-element.13), channel_id=1, source_target_pairs={{0,256},{32,288},{64,320},{96,352},{128,384},{160,416},{192,448},{... | collective-permute-start | bytes 196616 | tf_op jit(solution)/shard_map/ppermute | solution.py:105
  93.3 0.8 bitcast_select_fusion
  94.1 0.0 collective-permute-done.3
  94.1 0.0 collective-permute-done.5
  94.1 3.8 %collective-permute-done.4 = f32[8,8,256]{2,1,0:T(8,128)S(1)} collective-permute-done((f32[8,8,256]{2,1,0:T(8,128)S(1)}, f32[8,8,256]{2,1,0:T(8,128)S(1)}, u32[]{:S(2)}, u32[]{:S(2)}) %collective-permute-start.4) | collective-permute-done | bytes 65568 | tf_op jit(solution)/shard_map/ppermute | solution.py:105
  97.9 0.7 fusion.5
  (12 shorter events, 0.1 us)
Async XLA Ops:
  0.6 0.7 copy-start
  1.3 0.8 copy-start.6
  2.2 1.3 %copy-start.4 = (f32[1,64,2,128]{3,2,1,0:T(2,128)S(1)}, f32[1,64,2,128]{3,2,1,0:T(2,128)}, u32[]{:S(2)}) copy-start(f32[1,64,2,128]{3,2,1,0:T(2,128)} %param.11) | copy-start | bytes 196612
  2.7 0.7 copy-start.7
  3.5 0.8 copy-start.3
  3.7 0.8 copy-start.5
  5.3 10.7 %copy-start.2 = (f32[8,128,256]{2,1,0:T(8,128)S(1)}, f32[8,128,256]{2,1,0:T(8,128)}, u32[]{:S(2)}) copy-start(f32[8,128,256]{2,1,0:T(8,128)} %param.7) | copy-start | bytes 3145732
  6.5 26.3 %all-to-all-start = ((f32[128,6,128]{2,1,0:T(8,128)}), f32[128,6,128]{2,1,0:T(8,128)S(1)}, u32[]{:S(2)}, u32[]{:S(2)}) async-start(f32[128,6,128]{2,1,0:T(8,128)} %select_select_fusion), calls=%async_computation | async-start | bytes 1048576 | tf_op jit(solution)/shard_map/all_to_all | solution.py:135
  32.8 1.6 %copy-start.1 = (f32[128,6,128]{2,1,0:T(8,128)}, f32[128,6,128]{2,1,0:T(8,128)S(1)}, u32[]{:S(2)}) copy-start(f32[128,6,128]{2,1,0:T(8,128)S(1)} %all-to-all-done.data_ref) | copy-start | bytes 1179652
  48.8 15.9 %all-to-all-start.1 = ((f32[128,2,128]{2,1,0:T(2,128)}), f32[128,2,128]{2,1,0:T(2,128)S(1)}, u32[]{:S(2)}, u32[]{:S(2)}) async-start(f32[128,2,128]{2,1,0:T(2,128)} %get-tuple-element.5), calls=%async_computation.1 | async-start | bytes 262144 | tf_op jit(solution)/shard_map/all_to_all | solution.py:141
  54.6 10.7 %collective-permute-start = (f32[4,8,8,256]{3,2,1,0:T(8,128)S(1)}, f32[4,8,8,256]{3,2,1,0:T(8,128)S(1)}, u32[]{:S(2)}, u32[]{:S(2)}) collective-permute-start(f32[4,8,8,256]{3,2,1,0:T(8,128)S(1)} %get-tuple-element.8), channel_id=1, source_target_pairs={{0,32},{32,64},{64,96},{96,0},{128,160},{160,192},{192,224},{224,1... | collective-permute-start | bytes 786440 | tf_op jit(solution)/shard_map/ppermute | solution.py:101
  58.1 10.4 %collective-permute-start.2 = (f32[4,8,8,256]{3,2,1,0:T(8,128)S(1)}, f32[4,8,8,256]{3,2,1,0:T(8,128)S(1)}, u32[]{:S(2)}, u32[]{:S(2)}) collective-permute-start(f32[4,8,8,256]{3,2,1,0:T(8,128)S(1)} %get-tuple-element.9), channel_id=1, source_target_pairs={{0,96},{32,0},{64,32},{96,64},{128,224},{160,128},{192,160},{224,1... | collective-permute-start | bytes 786440 | tf_op jit(solution)/shard_map/ppermute | solution.py:101
  60.5 13.8 %collective-permute-start.1 = (f32[4,8,8,256]{3,2,1,0:T(8,128)S(1)}, f32[4,8,8,256]{3,2,1,0:T(8,128)S(1)}, u32[]{:S(2)}, u32[]{:S(2)}) collective-permute-start(f32[4,8,8,256]{3,2,1,0:T(8,128)S(1)} %get-tuple-element.10), channel_id=1, source_target_pairs={{0,64},{32,96},{64,0},{96,32},{128,192},{160,224},{192,128},{224,1... | collective-permute-start | bytes 786440 | tf_op jit(solution)/shard_map/ppermute | solution.py:101
  75.3 18.8 %collective-permute-start.3 = (f32[8,8,256]{2,1,0:T(8,128)S(1)}, f32[8,8,256]{2,1,0:T(8,128)S(1)}, u32[]{:S(2)}, u32[]{:S(2)}) collective-permute-start(f32[8,8,256]{2,1,0:T(8,128)S(1)} %get-tuple-element.11), channel_id=1, source_target_pairs={{0,128},{32,160},{64,192},{96,224},{128,256},{160,288},{192,320},{... | collective-permute-start | bytes 196616 | tf_op jit(solution)/shard_map/ppermute | solution.py:105
  81.4 12.7 %collective-permute-start.5 = (f32[8,8,256]{2,1,0:T(8,128)S(1)}, f32[8,8,256]{2,1,0:T(8,128)S(1)}, u32[]{:S(2)}, u32[]{:S(2)}) collective-permute-start(f32[8,8,256]{2,1,0:T(8,128)S(1)} %get-tuple-element.12), channel_id=1, source_target_pairs={{0,384},{32,416},{64,448},{96,480},{128,0},{160,32},{192,64},{224,... | collective-permute-start | bytes 196616 | tf_op jit(solution)/shard_map/ppermute | solution.py:105
  87.3 10.6 %collective-permute-start.4 = (f32[8,8,256]{2,1,0:T(8,128)S(1)}, f32[8,8,256]{2,1,0:T(8,128)S(1)}, u32[]{:S(2)}, u32[]{:S(2)}) collective-permute-start(f32[8,8,256]{2,1,0:T(8,128)S(1)} %get-tuple-element.13), channel_id=1, source_target_pairs={{0,256},{32,288},{64,320},{96,352},{128,384},{160,416},{192,448},{... | collective-permute-start | bytes 196616 | tf_op jit(solution)/shard_map/ppermute | solution.py:105

commit v8 on v7

--- a/solution.py
+++ b/solution.py
@@ -99,11 +99,18 @@
     for k in range(1, size_lo):
         piece = lax.dynamic_index_in_dim(parts, (lo + k) % size_lo, 1, keepdims=False)
         acc = acc + lax.ppermute(piece, "chan", _ring_pairs(size_hi, size_lo, k, True))
-    out = lax.dynamic_index_in_dim(acc, hi, 0, keepdims=False)
-    for k in range(1, size_hi):
-        piece = lax.dynamic_index_in_dim(acc, (hi + k) % size_hi, 0, keepdims=False)
-        out = out + lax.ppermute(piece, "chan", _ring_pairs(size_hi, size_lo, k, False))
-    return out
+    for bit in (2, 1):
+        halves = acc.reshape((2, acc.shape[0] // 2) + acc.shape[1:]) if bit == 2 else acc.reshape(
+            (2, 1) + acc.shape[1:]
+        )
+        mine = (hi // bit) % 2
+        keep = lax.dynamic_index_in_dim(halves, mine, 0, keepdims=False)
+        give = lax.dynamic_index_in_dim(halves, 1 - mine, 0, keepdims=False)
+        pairs = [
+            (h * size_lo + l, (h ^ bit) * size_lo + l) for h in range(size_hi) for l in range(size_lo)
+        ]
+        acc = keep + lax.ppermute(give, "chan", pairs)
+    return acc[0]
 
 
 def shards(grid, tile_list, owner_map, offsets, positions, observed, weights):

time: 99.1 us -> 93.1 us (0.939)
  starting transfers between devices: 42 us -> 38.9 us
  waiting for transfers between devices: 28.4 us -> 25.7 us
    ppermute x3, waiting for transfers between devices: 8.92 us -> 4.63 us  [_chan_reduce(): lax.ppermute(piece, 'chan', _ring_pairs(size_hi, size_lo, k, True))]
    ppermute x3 -> x2, starting transfers between devices: 18 us -> 14.9 us  [_chan_reduce(): acc = keep + lax.ppermute(give, 'chan', pairs)]
    ppermute x3 -> x2, waiting for transfers between devices: 3.79 us -> 5.38 us  [_chan_reduce(): acc = keep + lax.ppermute(give, 'chan', pairs)]
  transfers between devices with their start and end apart: 8 -> 7, of which waited for: 4 -> 4; matrix products, arithmetic and copies ran while one was open for 4% -> 4% of each run, Pallas kernels for 0% -> 0%
where the time goes in v8:
time: 93.1 us; the launch traced here: 92.5 us
  starting transfers between devices  38.9 us (42%)
  waiting for transfers between devices  25.7 us (28%)
  Pallas kernels  14.3 us (15%)
  other arithmetic  6.67 us (7%)
  local copies, waits for them, and re-layouts  5.96 us (6%)
  between operations  1.05 us (1%)
    all_to_all x1, waiting for transfers between devices, shards(): lax.all_to_all(outgoing, 'bl', split_axis=0, concat_axis=0, tiled=True)  15.7 us
    ppermute x2, starting transfers between devices, _chan_reduce(): acc = keep + lax.ppermute(give, 'chan', pairs)  14.9 us
    pallas_call x1, Pallas kernels, _grid_call(): pl.pallas_call(_grid_kernel, out_shape=(jax.ShapeDtypeStruct((slots, 2, v...  14.3 us
    ppermute x3, starting transfers between devices, _chan_reduce(): lax.ppermute(piece, 'chan', _ring_pairs(size_hi, size_lo, k, True))  9.88 us
    all_to_all x1, starting transfers between devices, shards(): lax.all_to_all(outgoing, 'bl', split_axis=0, concat_axis=0, tiled=True)  9.51 us
    ppermute x2, waiting for transfers between devices, _chan_reduce(): acc = keep + lax.ppermute(give, 'chan', pairs)  5.38 us
    ppermute x3, waiting for transfers between devices, _chan_reduce(): lax.ppermute(piece, 'chan', _ring_pairs(size_hi, size_lo, k, True))  4.63 us
    all_to_all x1, starting transfers between devices, shards(): lax.all_to_all(residual_all, 'bl', split_axis=0, concat_axis=0, tiled=True)  4.63 us
  transfers between devices with their start and end apart: 7, of which 4 were waited for; matrix products, arithmetic and copies ran while one was open for 4% of the time, Pallas kernels for 0%

profile of v8, /device:TPU:10, one launch (start us, length us, event | category | flops | bytes accessed | tf_op | source)
XLA Modules:
  0.0 92.5 jit_solution(2967579765603310219)
XLA Ops:
  0.6 0.0 copy-start
  0.6 0.7 fusion.9
  1.3 0.0 copy-done
  1.3 0.0 copy-start.6
  1.3 0.8 gather_fusion
  2.1 0.0 copy-done.6
  2.1 0.1 fusion.4
  2.2 0.0 copy-start.4
  2.2 0.1 reduce_window_sum.11
  2.3 0.2 select_reduce_fusion.1
  2.5 0.1 select_reduce_fusion
  2.6 0.1 fusion.3
  2.7 0.0 copy-start.7
  2.8 0.7 copy-done.7
  3.4 0.1 copy.15
  3.5 0.0 copy-done.4
  3.5 0.0 copy-start.3
  3.5 0.1 bitcast_add_fusion.3
  3.7 0.0 copy-start.5
  3.7 0.1 broadcast_in_dim.74
  3.8 0.6 copy-done.3
  4.4 0.1 copy-done.5
  4.5 0.1 pad_maximum_fusion
  4.6 0.8 gather_fusion.1
  5.3 0.0 copy-start.2
  5.4 1.1 %select_select_fusion = f32[128,6,128]{2,1,0:T(8,128)} fusion(f32[128,6,128]{2,1,0:T(8,128)S(1)} %gather_fusion.1, pred[128]{0:T(512)(128)(4,1)S(1)} %compare_and_fusion.1, pred[128]{0:T(512)(128)(4,1)S(1)} %fusion.3), kind=kLoop, calls=%fused_computation.4 | loop fusion | flops 196608 | bytes 786688 | tf_op jit(solution)/shard_map/jit(_where)/select_n | solution.py:141
  6.5 9.5 %all-to-all-start = ((f32[128,6,128]{2,1,0:T(8,128)}), f32[128,6,128]{2,1,0:T(8,128)S(1)}, u32[]{:S(2)}, u32[]{:S(2)}) async-start(f32[128,6,128]{2,1,0:T(8,128)} %select_select_fusion), calls=%async_computation | async-start | bytes 1048576 | tf_op jit(solution)/shard_map/all_to_all | solution.py:142
  16.1 0.0 copy-done.2
  16.1 1.0 %copy.17 = bf16[8,128,256]{1,2,0:T(8,128)(2,1)} copy(f32[8,128,256]{2,1,0:T(8,128)S(1)} %copy-done.2) | data formatting | bytes 1572864 | tf_op args[0]
  17.1 15.7 %all-to-all-done.data_ref = f32[128,6,128]{2,1,0:T(8,128)S(1)} async-done(((f32[128,6,128]{2,1,0:T(8,128)}), f32[128,6,128]{2,1,0:T(8,128)S(1)}, u32[]{:S(2)}, u32[]{:S(2)}) %all-to-all-start) | async-done | bytes 393248 | tf_op jit(solution)/shard_map/all_to_all | solution.py:142
  32.8 0.0 copy-start.1
  32.8 1.0 %slice_reduce_fusion = f32[128]{0:T(128)S(1)} fusion(f32[128,6,128]{2,1,0:T(8,128)S(1)} %all-to-all-done.data_ref), kind=kLoop, calls=%fused_computation.14 | loop fusion | flops 16256 | bytes 66048 | tf_op jit(solution)/shard_map/reduce_max | solution.py:143
  33.8 0.5 convert_element_type.30.labels_ref
  34.3 0.0 copy-done.1
  34.3 14.3 %shard_map.86 = (f32[128,2,128]{2,1,0:T(2,128)}, f32[16,8,8,256]{3,2,1,0:T(8,128)}) custom-call(s32[128]{0:T(128)} %convert_element_type.30.labels_ref, f32[128,6,128]{2,1,0:T(8,128)} %copy-done.1, bf16[8,256,128]{2,1,0:T(8,128)(2,1)} %bitcast.70), custom_call_target="tpu_custom_call" | custom-call | tf_op jit(solution)/shard_map/pallas_call | solution.py:65
  48.6 1.2 %dynamic-slice_bitcast_fusion.2 = (f32[4,8,8,256]{3,2,1,0:T(8,128)S(1)}, f32[4,8,8,256]{3,2,1,0:T(8,128)S(1)}, f32[4,8,8,256]{3,2,1,0:T(8,128)S(1)}) fusion(f32[4,4,8,8,256]{4,3,2,1,0:T(8,128)} %bitcast.71, s32[]{:T(128)S(6)} %select_n.224, s32[]{:T(128)S(6)} %select_n.228, s32[]{:T(128)S(6)} %select_n.226), kind=kLoop, calls=%fused_computation.11 | loop fusion | bytes 1572876 | tf_op jit(solution)/shard_map/jit(dynamic_index_in_dim)/squeeze | solution.py:100
  49.8 3.4 %collective-permute-start = (f32[4,8,8,256]{3,2,1,0:T(8,128)S(1)}, f32[4,8,8,256]{3,2,1,0:T(8,128)S(1)}, u32[]{:S(2)}, u32[]{:S(2)}) collective-permute-start(f32[4,8,8,256]{3,2,1,0:T(8,128)S(1)} %get-tuple-element.8), channel_id=1, source_target_pairs={{0,32},{32,64},{64,96},{96,0},{128,160},{160,192},{192,224},{224,1... | collective-permute-start | bytes 786440 | tf_op jit(solution)/shard_map/ppermute | solution.py:101
  53.2 2.4 %collective-permute-start.2 = (f32[4,8,8,256]{3,2,1,0:T(8,128)S(1)}, f32[4,8,8,256]{3,2,1,0:T(8,128)S(1)}, u32[]{:S(2)}, u32[]{:S(2)}) collective-permute-start(f32[4,8,8,256]{3,2,1,0:T(8,128)S(1)} %get-tuple-element.9), channel_id=1, source_target_pairs={{0,96},{32,0},{64,32},{96,64},{128,224},{160,128},{192,160},{224,1... | collective-permute-start | bytes 786440 | tf_op jit(solution)/shard_map/ppermute | solution.py:101
  55.6 4.0 %collective-permute-start.1 = (f32[4,8,8,256]{3,2,1,0:T(8,128)S(1)}, f32[4,8,8,256]{3,2,1,0:T(8,128)S(1)}, u32[]{:S(2)}, u32[]{:S(2)}) collective-permute-start(f32[4,8,8,256]{3,2,1,0:T(8,128)S(1)} %get-tuple-element.10), channel_id=1, source_target_pairs={{0,64},{32,96},{64,0},{96,32},{128,192},{160,224},{192,128},{224,1... | collective-permute-start | bytes 786440 | tf_op jit(solution)/shard_map/ppermute | solution.py:101
  59.8 4.6 %all-to-all-start.1 = ((f32[128,2,128]{2,1,0:T(2,128)}), f32[128,2,128]{2,1,0:T(2,128)S(1)}, u32[]{:S(2)}, u32[]{:S(2)}) async-start(f32[128,2,128]{2,1,0:T(2,128)} %get-tuple-element.5), calls=%async_computation.1 | async-start | bytes 262144 | tf_op jit(solution)/shard_map/all_to_all | solution.py:148
  64.4 0.0 collective-permute-done
  64.4 0.0 collective-permute-done.2
  64.4 4.6 %collective-permute-done.1 = f32[4,8,8,256]{3,2,1,0:T(8,128)S(1)} collective-permute-done((f32[4,8,8,256]{3,2,1,0:T(8,128)S(1)}, f32[4,8,8,256]{3,2,1,0:T(8,128)S(1)}, u32[]{:S(2)}, u32[]{:S(2)}) %collective-permute-start.1) | collective-permute-done | bytes 262176 | tf_op jit(solution)/shard_map/ppermute | solution.py:101
  69.0 1.0 %fusion.1 = f32[4,8,8,256]{3,2,1,0:T(8,128)S(1)} fusion(f32[4,8,8,256]{3,2,1,0:T(8,128)S(1)} %collective-permute-done.2, f32[4,8,8,256]{3,2,1,0:T(8,128)S(1)} %collective-permute-done.1, f32[4,8,8,256]{3,2,1,0:T(8,128)S(1)} %collective-permute-done, f32[4,4,8,8,256]{4,3,2,1,0:T(8,128)} %bitcast.72, s32[]{:T(128)S(6)} %select_n.222), kind=kLoop, calls=%fused_computation.8 | loop fusion | flops 196608 | bytes 1310724 | tf_op jit(solution)/shard_map/add | solution.py:101
  70.1 10.0 %collective-permute-start.3 = (f32[2,8,8,256]{3,2,1,0:T(8,128)S(1)}, f32[2,8,8,256]{3,2,1,0:T(8,128)S(1)}, u32[]{:S(2)}, u32[]{:S(2)}) collective-permute-start(f32[2,8,8,256]{3,2,1,0:T(8,128)S(1)} %dynamic-slice_bitcast_fusion.3), channel_id=1, source_target_pairs={{0,256},{32,288},{64,320},{96,352},{128,384},{160,416},{192,448},{... | collective-permute-start | bytes 393224 | tf_op jit(solution)/shard_map/ppermute | solution.py:112
  80.1 0.0 all-to-all-done.1
  80.1 0.7 gather_fusion.2
  80.8 3.9 %collective-permute-done.3 = f32[2,8,8,256]{3,2,1,0:T(8,128)S(1)} collective-permute-done((f32[2,8,8,256]{3,2,1,0:T(8,128)S(1)}, f32[2,8,8,256]{3,2,1,0:T(8,128)S(1)}, u32[]{:S(2)}, u32[]{:S(2)}) %collective-permute-start.3) | collective-permute-done | bytes 131104 | tf_op jit(solution)/shard_map/ppermute | solution.py:112
  84.8 4.9 %collective-permute-start.4 = (f32[1,8,8,256]{3,2,1,0:T(8,128)S(1)}, f32[1,8,8,256]{3,2,1,0:T(8,128)S(1)}, u32[]{:S(2)}, u32[]{:S(2)}) collective-permute-start(f32[1,8,8,256]{3,2,1,0:T(8,128)S(1)} %constant_dynamic-slice_fusion), channel_id=1, source_target_pairs={{0,128},{32,160},{64,192},{96,224},{128,0},{160,32},{192,64},{224,... | collective-permute-start | bytes 196616 | tf_op jit(solution)/shard_map/ppermute | solution.py:112
  89.7 0.8 bitcast_select_fusion
  90.4 1.5 %collective-permute-done.4 = f32[1,8,8,256]{3,2,1,0:T(8,128)S(1)} collective-permute-done((f32[1,8,8,256]{3,2,1,0:T(8,128)S(1)}, f32[1,8,8,256]{3,2,1,0:T(8,128)S(1)}, u32[]{:S(2)}, u32[]{:S(2)}) %collective-permute-start.4) | collective-permute-done | bytes 65568 | tf_op jit(solution)/shard_map/ppermute | solution.py:112
  91.9 0.6 fusion.2
  (14 shorter events, 0.1 us)
Async XLA Ops:
  0.6 0.7 copy-start
  1.3 0.8 copy-start.6
  2.2 1.3 %copy-start.4 = (f32[1,64,2,128]{3,2,1,0:T(2,128)S(1)}, f32[1,64,2,128]{3,2,1,0:T(2,128)}, u32[]{:S(2)}) copy-start(f32[1,64,2,128]{3,2,1,0:T(2,128)} %param.11) | copy-start | bytes 196612
  2.7 0.7 copy-start.7
  3.5 0.8 copy-start.3
  3.7 0.8 copy-start.5
  5.3 10.7 %copy-start.2 = (f32[8,128,256]{2,1,0:T(8,128)S(1)}, f32[8,128,256]{2,1,0:T(8,128)}, u32[]{:S(2)}) copy-start(f32[8,128,256]{2,1,0:T(8,128)} %param.7) | copy-start | bytes 3145732
  6.5 26.3 %all-to-all-start = ((f32[128,6,128]{2,1,0:T(8,128)}), f32[128,6,128]{2,1,0:T(8,128)S(1)}, u32[]{:S(2)}, u32[]{:S(2)}) async-start(f32[128,6,128]{2,1,0:T(8,128)} %select_select_fusion), calls=%async_computation | async-start | bytes 1048576 | tf_op jit(solution)/shard_map/all_to_all | solution.py:142
  32.8 1.6 %copy-start.1 = (f32[128,6,128]{2,1,0:T(8,128)}, f32[128,6,128]{2,1,0:T(8,128)S(1)}, u32[]{:S(2)}) copy-start(f32[128,6,128]{2,1,0:T(8,128)S(1)} %all-to-all-done.data_ref) | copy-start | bytes 1179652
  49.8 14.6 %collective-permute-start = (f32[4,8,8,256]{3,2,1,0:T(8,128)S(1)}, f32[4,8,8,256]{3,2,1,0:T(8,128)S(1)}, u32[]{:S(2)}, u32[]{:S(2)}) collective-permute-start(f32[4,8,8,256]{3,2,1,0:T(8,128)S(1)} %get-tuple-element.8), channel_id=1, source_target_pairs={{0,32},{32,64},{64,96},{96,0},{128,160},{160,192},{192,224},{224,1... | collective-permute-start | bytes 786440 | tf_op jit(solution)/shard_map/ppermute | solution.py:101
  53.2 11.2 %collective-permute-start.2 = (f32[4,8,8,256]{3,2,1,0:T(8,128)S(1)}, f32[4,8,8,256]{3,2,1,0:T(8,128)S(1)}, u32[]{:S(2)}, u32[]{:S(2)}) collective-permute-start(f32[4,8,8,256]{3,2,1,0:T(8,128)S(1)} %get-tuple-element.9), channel_id=1, source_target_pairs={{0,96},{32,0},{64,32},{96,64},{128,224},{160,128},{192,160},{224,1... | collective-permute-start | bytes 786440 | tf_op jit(solution)/shard_map/ppermute | solution.py:101
  55.6 13.4 %collective-permute-start.1 = (f32[4,8,8,256]{3,2,1,0:T(8,128)S(1)}, f32[4,8,8,256]{3,2,1,0:T(8,128)S(1)}, u32[]{:S(2)}, u32[]{:S(2)}) collective-permute-start(f32[4,8,8,256]{3,2,1,0:T(8,128)S(1)} %get-tuple-element.10), channel_id=1, source_target_pairs={{0,64},{32,96},{64,0},{96,32},{128,192},{160,224},{192,128},{224,1... | collective-permute-start | bytes 786440 | tf_op jit(solution)/shard_map/ppermute | solution.py:101
  59.8 20.4 %all-to-all-start.1 = ((f32[128,2,128]{2,1,0:T(2,128)}), f32[128,2,128]{2,1,0:T(2,128)S(1)}, u32[]{:S(2)}, u32[]{:S(2)}) async-start(f32[128,2,128]{2,1,0:T(2,128)} %get-tuple-element.5), calls=%async_computation.1 | async-start | bytes 262144 | tf_op jit(solution)/shard_map/all_to_all | solution.py:148
  70.1 14.6 %collective-permute-start.3 = (f32[2,8,8,256]{3,2,1,0:T(8,128)S(1)}, f32[2,8,8,256]{3,2,1,0:T(8,128)S(1)}, u32[]{:S(2)}, u32[]{:S(2)}) collective-permute-start(f32[2,8,8,256]{3,2,1,0:T(8,128)S(1)} %dynamic-slice_bitcast_fusion.3), channel_id=1, source_target_pairs={{0,256},{32,288},{64,320},{96,352},{128,384},{160,416},{192,448},{... | collective-permute-start | bytes 393224 | tf_op jit(solution)/shard_map/ppermute | solution.py:112
  84.8 7.1 %collective-permute-start.4 = (f32[1,8,8,256]{3,2,1,0:T(8,128)S(1)}, f32[1,8,8,256]{3,2,1,0:T(8,128)S(1)}, u32[]{:S(2)}, u32[]{:S(2)}) collective-permute-start(f32[1,8,8,256]{3,2,1,0:T(8,128)S(1)} %constant_dynamic-slice_fusion), channel_id=1, source_target_pairs={{0,128},{32,160},{64,192},{96,224},{128,0},{160,32},{192,64},{224,... | collective-permute-start | bytes 196616 | tf_op jit(solution)/shard_map/ppermute | solution.py:112

commit v9 on v8

--- a/solution.py
+++ b/solution.py
@@ -99,18 +99,17 @@
     for k in range(1, size_lo):
         piece = lax.dynamic_index_in_dim(parts, (lo + k) % size_lo, 1, keepdims=False)
         acc = acc + lax.ppermute(piece, "chan", _ring_pairs(size_hi, size_lo, k, True))
-    for bit in (2, 1):
-        halves = acc.reshape((2, acc.shape[0] // 2) + acc.shape[1:]) if bit == 2 else acc.reshape(
-            (2, 1) + acc.shape[1:]
-        )
+    for bit in (1, 2):
+        axis = 1 if bit == 1 else 0
+        halves = acc.reshape((2, acc.shape[0] // 2) + acc.shape[1:]) if bit == 1 else acc
         mine = (hi // bit) % 2
-        keep = lax.dynamic_index_in_dim(halves, mine, 0, keepdims=False)
-        give = lax.dynamic_index_in_dim(halves, 1 - mine, 0, keepdims=False)
+        keep = lax.dynamic_index_in_dim(halves, mine, axis, keepdims=False)
+        give = lax.dynamic_index_in_dim(halves, 1 - mine, axis, keepdims=False)
         pairs = [
             (h * size_lo + l, (h ^ bit) * size_lo + l) for h in range(size_hi) for l in range(size_lo)
         ]
         acc = keep + lax.ppermute(give, "chan", pairs)
-    return acc[0]
+    return acc
 
 
 def shards(grid, tile_list, owner_map, offsets, positions, observed, weights):

time: 93.1 us -> 93.9 us (level)
  waiting for transfers between devices: 25.7 us -> 26.9 us
    ppermute x2, waiting for transfers between devices: 5.38 us -> 6.53 us  [_chan_reduce(): acc = keep + lax.ppermute(give, 'chan', pairs)]
where the time goes in v9:
time: 93.9 us; the launch traced here: 93.4 us
  starting transfers between devices  38.6 us (41%)
  waiting for transfers between devices  26.9 us (29%)
  Pallas kernels  14.2 us (15%)
  other arithmetic  6.67 us (7%)
  local copies, waits for them, and re-layouts  5.96 us (6%)
  between operations  1.06 us (1%)
    all_to_all x1, waiting for transfers between devices, shards(): lax.all_to_all(outgoing, 'bl', split_axis=0, concat_axis=0, tiled=True)  15.7 us
    ppermute x2, starting transfers between devices, _chan_reduce(): acc = keep + lax.ppermute(give, 'chan', pairs)  14.6 us
    pallas_call x1, Pallas kernels, _grid_call(): pl.pallas_call(_grid_kernel, out_shape=(jax.ShapeDtypeStruct((slots, 2, v...  14.2 us
    ppermute x3, starting transfers between devices, _chan_reduce(): lax.ppermute(piece, 'chan', _ring_pairs(size_hi, size_lo, k, True))  9.87 us
    all_to_all x1, starting transfers between devices, shards(): lax.all_to_all(outgoing, 'bl', split_axis=0, concat_axis=0, tiled=True)  9.51 us
    ppermute x2, waiting for transfers between devices, _chan_reduce(): acc = keep + lax.ppermute(give, 'chan', pairs)  6.53 us
    all_to_all x1, starting transfers between devices, shards(): lax.all_to_all(residual_all, 'bl', split_axis=0, concat_axis=0, tiled=True)  4.66 us
    ppermute x3, waiting for transfers between devices, _chan_reduce(): lax.ppermute(piece, 'chan', _ring_pairs(size_hi, size_lo, k, True))  4.62 us
  transfers between devices with their start and end apart: 7, of which 4 were waited for; matrix products, arithmetic and copies ran while one was open for 4% of the time, Pallas kernels for 0%

profile of v9, /device:TPU:10, one launch (start us, length us, event | category | flops | bytes accessed | tf_op | source)
XLA Modules:
  0.0 93.4 jit_solution(1533339592488380288)
XLA Ops:
  0.6 0.0 copy-start
  0.6 0.7 fusion.10
  1.3 0.0 copy-done
  1.3 0.0 copy-start.6
  1.3 0.8 gather_fusion
  2.1 0.0 copy-done.6
  2.1 0.1 fusion.5
  2.2 0.0 copy-start.4
  2.2 0.1 reduce_window_sum.11
  2.3 0.2 select_reduce_fusion.1
  2.5 0.1 select_reduce_fusion
  2.6 0.1 fusion.4
  2.7 0.0 copy-start.7
  2.8 0.7 copy-done.7
  3.4 0.1 copy.15
  3.5 0.0 copy-done.4
  3.5 0.0 copy-start.3
  3.5 0.1 bitcast_add_fusion.3
  3.7 0.0 copy-start.5
  3.7 0.1 broadcast_in_dim.74
  3.8 0.6 copy-done.3
  4.4 0.1 copy-done.5
  4.5 0.1 pad_maximum_fusion
  4.6 0.8 gather_fusion.1
  5.3 0.0 copy-start.2
  5.4 1.1 %select_select_fusion = f32[128,6,128]{2,1,0:T(8,128)} fusion(f32[128,6,128]{2,1,0:T(8,128)S(1)} %gather_fusion.1, pred[128]{0:T(512)(128)(4,1)S(1)} %compare_and_fusion.1, pred[128]{0:T(512)(128)(4,1)S(1)} %fusion.4), kind=kLoop, calls=%fused_computation.4 | loop fusion | flops 196608 | bytes 786688 | tf_op jit(solution)/shard_map/jit(_where)/select_n | solution.py:140
  6.5 9.5 %all-to-all-start = ((f32[128,6,128]{2,1,0:T(8,128)}), f32[128,6,128]{2,1,0:T(8,128)S(1)}, u32[]{:S(2)}, u32[]{:S(2)}) async-start(f32[128,6,128]{2,1,0:T(8,128)} %select_select_fusion), calls=%async_computation | async-start | bytes 1048576 | tf_op jit(solution)/shard_map/all_to_all | solution.py:141
  16.1 0.0 copy-done.2
  16.1 1.0 %copy.17 = bf16[8,128,256]{1,2,0:T(8,128)(2,1)} copy(f32[8,128,256]{2,1,0:T(8,128)S(1)} %copy-done.2) | data formatting | bytes 1572864 | tf_op args[0]
  17.1 15.7 %all-to-all-done.data_ref = f32[128,6,128]{2,1,0:T(8,128)S(1)} async-done(((f32[128,6,128]{2,1,0:T(8,128)}), f32[128,6,128]{2,1,0:T(8,128)S(1)}, u32[]{:S(2)}, u32[]{:S(2)}) %all-to-all-start) | async-done | bytes 393248 | tf_op jit(solution)/shard_map/all_to_all | solution.py:141
  32.8 0.0 copy-start.1
  32.8 1.0 %slice_reduce_fusion = f32[128]{0:T(128)S(1)} fusion(f32[128,6,128]{2,1,0:T(8,128)S(1)} %all-to-all-done.data_ref), kind=kLoop, calls=%fused_computation.14 | loop fusion | flops 16256 | bytes 66048 | tf_op jit(solution)/shard_map/reduce_max | solution.py:142
  33.8 0.5 convert_element_type.30.labels_ref
  34.3 0.0 copy-done.1
  34.3 14.2 %shard_map.86 = (f32[128,2,128]{2,1,0:T(2,128)}, f32[16,8,8,256]{3,2,1,0:T(8,128)}) custom-call(s32[128]{0:T(128)} %convert_element_type.30.labels_ref, f32[128,6,128]{2,1,0:T(8,128)} %copy-done.1, bf16[8,256,128]{2,1,0:T(8,128)(2,1)} %bitcast.74), custom_call_target="tpu_custom_call" | custom-call | tf_op jit(solution)/shard_map/pallas_call | solution.py:65
  48.6 1.2 %dynamic-slice_bitcast_fusion.2 = (f32[4,8,8,256]{3,2,1,0:T(8,128)S(1)}, f32[4,8,8,256]{3,2,1,0:T(8,128)S(1)}, f32[4,8,8,256]{3,2,1,0:T(8,128)S(1)}) fusion(f32[4,4,8,8,256]{4,3,2,1,0:T(8,128)} %bitcast.75, s32[]{:T(128)S(6)} %select_n.224, s32[]{:T(128)S(6)} %select_n.228, s32[]{:T(128)S(6)} %select_n.226), kind=kLoop, calls=%fused_computation.11 | loop fusion | bytes 1572876 | tf_op jit(solution)/shard_map/jit(dynamic_index_in_dim)/squeeze | solution.py:100
  49.7 3.4 %collective-permute-start = (f32[4,8,8,256]{3,2,1,0:T(8,128)S(1)}, f32[4,8,8,256]{3,2,1,0:T(8,128)S(1)}, u32[]{:S(2)}, u32[]{:S(2)}) collective-permute-start(f32[4,8,8,256]{3,2,1,0:T(8,128)S(1)} %get-tuple-element.8), channel_id=1, source_target_pairs={{0,32},{32,64},{64,96},{96,0},{128,160},{160,192},{192,224},{224,1... | collective-permute-start | bytes 786440 | tf_op jit(solution)/shard_map/ppermute | solution.py:101
  53.2 2.4 %collective-permute-start.2 = (f32[4,8,8,256]{3,2,1,0:T(8,128)S(1)}, f32[4,8,8,256]{3,2,1,0:T(8,128)S(1)}, u32[]{:S(2)}, u32[]{:S(2)}) collective-permute-start(f32[4,8,8,256]{3,2,1,0:T(8,128)S(1)} %get-tuple-element.9), channel_id=1, source_target_pairs={{0,96},{32,0},{64,32},{96,64},{128,224},{160,128},{192,160},{224,1... | collective-permute-start | bytes 786440 | tf_op jit(solution)/shard_map/ppermute | solution.py:101
  55.6 4.0 %collective-permute-start.1 = (f32[4,8,8,256]{3,2,1,0:T(8,128)S(1)}, f32[4,8,8,256]{3,2,1,0:T(8,128)S(1)}, u32[]{:S(2)}, u32[]{:S(2)}) collective-permute-start(f32[4,8,8,256]{3,2,1,0:T(8,128)S(1)} %get-tuple-element.10), channel_id=1, source_target_pairs={{0,64},{32,96},{64,0},{96,32},{128,192},{160,224},{192,128},{224,1... | collective-permute-start | bytes 786440 | tf_op jit(solution)/shard_map/ppermute | solution.py:101
  59.7 4.7 %all-to-all-start.1 = ((f32[128,2,128]{2,1,0:T(2,128)}), f32[128,2,128]{2,1,0:T(2,128)S(1)}, u32[]{:S(2)}, u32[]{:S(2)}) async-start(f32[128,2,128]{2,1,0:T(2,128)} %get-tuple-element.5), calls=%async_computation.1 | async-start | bytes 262144 | tf_op jit(solution)/shard_map/all_to_all | solution.py:147
  64.4 0.0 collective-permute-done
  64.4 0.0 collective-permute-done.2
  64.4 4.6 %collective-permute-done.1 = f32[4,8,8,256]{3,2,1,0:T(8,128)S(1)} collective-permute-done((f32[4,8,8,256]{3,2,1,0:T(8,128)S(1)}, f32[4,8,8,256]{3,2,1,0:T(8,128)S(1)}, u32[]{:S(2)}, u32[]{:S(2)}) %collective-permute-start.1) | collective-permute-done | bytes 262176 | tf_op jit(solution)/shard_map/ppermute | solution.py:101
  69.0 1.0 %fusion.1 = f32[4,8,8,256]{3,2,1,0:T(8,128)S(1)} fusion(f32[4,8,8,256]{3,2,1,0:T(8,128)S(1)} %collective-permute-done.2, f32[4,8,8,256]{3,2,1,0:T(8,128)S(1)} %collective-permute-done.1, f32[4,8,8,256]{3,2,1,0:T(8,128)S(1)} %collective-permute-done, f32[4,4,8,8,256]{4,3,2,1,0:T(8,128)} %bitcast.76, s32[]{:T(128)S(6)} %select_n.222), kind=kLoop, calls=%fused_computation.8 | loop fusion | flops 196608 | bytes 1310724 | tf_op jit(solution)/shard_map/add | solution.py:101
  70.1 6.1 %collective-permute-start.3 = (f32[2,8,8,256]{3,2,1,0:T(8,128)S(1)}, f32[2,8,8,256]{3,2,1,0:T(8,128)S(1)}, u32[]{:S(2)}, u32[]{:S(2)}) collective-permute-start(f32[2,8,8,256]{3,2,1,0:T(8,128)S(1)} %dynamic-slice_bitcast_fusion.3), channel_id=1, source_target_pairs={{0,128},{32,160},{64,192},{96,224},{128,0},{160,32},{192,64},{224,... | collective-permute-start | bytes 393224 | tf_op jit(solution)/shard_map/ppermute | solution.py:111
  76.3 0.0 all-to-all-done.1
  76.3 0.7 gather_fusion.2
  76.9 4.4 %collective-permute-done.3 = f32[2,8,8,256]{3,2,1,0:T(8,128)S(1)} collective-permute-done((f32[2,8,8,256]{3,2,1,0:T(8,128)S(1)}, f32[2,8,8,256]{3,2,1,0:T(8,128)S(1)}, u32[]{:S(2)}, u32[]{:S(2)}) %collective-permute-start.3) | collective-permute-done | bytes 131104 | tf_op jit(solution)/shard_map/ppermute | solution.py:111
  81.3 8.4 %collective-permute-start.4 = (f32[8,8,256]{2,1,0:T(8,128)S(1)}, f32[8,8,256]{2,1,0:T(8,128)S(1)}, u32[]{:S(2)}, u32[]{:S(2)}) collective-permute-start(f32[8,8,256]{2,1,0:T(8,128)S(1)} %dynamic-slice_bitcast_fusion.4), channel_id=1, source_target_pairs={{0,256},{32,288},{64,320},{96,352},{128,384},{160,416},{192,448},{... | collective-permute-start | bytes 196616 | tf_op jit(solution)/shard_map/ppermute | solution.py:111
  89.8 0.8 bitcast_select_fusion
  90.5 2.2 %collective-permute-done.4 = f32[8,8,256]{2,1,0:T(8,128)S(1)} collective-permute-done((f32[8,8,256]{2,1,0:T(8,128)S(1)}, f32[8,8,256]{2,1,0:T(8,128)S(1)}, u32[]{:S(2)}, u32[]{:S(2)}) %collective-permute-start.4) | collective-permute-done | bytes 65568 | tf_op jit(solution)/shard_map/ppermute | solution.py:111
  92.7 0.6 fusion.3
  (14 shorter events, 0.1 us)
Async XLA Ops:
  0.6 0.7 copy-start
  1.3 0.8 copy-start.6
  2.2 1.3 %copy-start.4 = (f32[1,64,2,128]{3,2,1,0:T(2,128)S(1)}, f32[1,64,2,128]{3,2,1,0:T(2,128)}, u32[]{:S(2)}) copy-start(f32[1,64,2,128]{3,2,1,0:T(2,128)} %param.11) | copy-start | bytes 196612
  2.7 0.7 copy-start.7
  3.5 0.8 copy-start.3
  3.7 0.8 copy-start.5
  5.3 10.7 %copy-start.2 = (f32[8,128,256]{2,1,0:T(8,128)S(1)}, f32[8,128,256]{2,1,0:T(8,128)}, u32[]{:S(2)}) copy-start(f32[8,128,256]{2,1,0:T(8,128)} %param.7) | copy-start | bytes 3145732
  6.5 26.3 %all-to-all-start = ((f32[128,6,128]{2,1,0:T(8,128)}), f32[128,6,128]{2,1,0:T(8,128)S(1)}, u32[]{:S(2)}, u32[]{:S(2)}) async-start(f32[128,6,128]{2,1,0:T(8,128)} %select_select_fusion), calls=%async_computation | async-start | bytes 1048576 | tf_op jit(solution)/shard_map/all_to_all | solution.py:141
  32.8 1.6 %copy-start.1 = (f32[128,6,128]{2,1,0:T(8,128)}, f32[128,6,128]{2,1,0:T(8,128)S(1)}, u32[]{:S(2)}) copy-start(f32[128,6,128]{2,1,0:T(8,128)S(1)} %all-to-all-done.data_ref) | copy-start | bytes 1179652
  49.7 14.6 %collective-permute-start = (f32[4,8,8,256]{3,2,1,0:T(8,128)S(1)}, f32[4,8,8,256]{3,2,1,0:T(8,128)S(1)}, u32[]{:S(2)}, u32[]{:S(2)}) collective-permute-start(f32[4,8,8,256]{3,2,1,0:T(8,128)S(1)} %get-tuple-element.8), channel_id=1, source_target_pairs={{0,32},{32,64},{64,96},{96,0},{128,160},{160,192},{192,224},{224,1... | collective-permute-start | bytes 786440 | tf_op jit(solution)/shard_map/ppermute | solution.py:101
  53.2 11.2 %collective-permute-start.2 = (f32[4,8,8,256]{3,2,1,0:T(8,128)S(1)}, f32[4,8,8,256]{3,2,1,0:T(8,128)S(1)}, u32[]{:S(2)}, u32[]{:S(2)}) collective-permute-start(f32[4,8,8,256]{3,2,1,0:T(8,128)S(1)} %get-tuple-element.9), channel_id=1, source_target_pairs={{0,96},{32,0},{64,32},{96,64},{128,224},{160,128},{192,160},{224,1... | collective-permute-start | bytes 786440 | tf_op jit(solution)/shard_map/ppermute | solution.py:101
  55.6 13.4 %collective-permute-start.1 = (f32[4,8,8,256]{3,2,1,0:T(8,128)S(1)}, f32[4,8,8,256]{3,2,1,0:T(8,128)S(1)}, u32[]{:S(2)}, u32[]{:S(2)}) collective-permute-start(f32[4,8,8,256]{3,2,1,0:T(8,128)S(1)} %get-tuple-element.10), channel_id=1, source_target_pairs={{0,64},{32,96},{64,0},{96,32},{128,192},{160,224},{192,128},{224,1... | collective-permute-start | bytes 786440 | tf_op jit(solution)/shard_map/ppermute | solution.py:101
  59.7 16.6 %all-to-all-start.1 = ((f32[128,2,128]{2,1,0:T(2,128)}), f32[128,2,128]{2,1,0:T(2,128)S(1)}, u32[]{:S(2)}, u32[]{:S(2)}) async-start(f32[128,2,128]{2,1,0:T(2,128)} %get-tuple-element.5), calls=%async_computation.1 | async-start | bytes 262144 | tf_op jit(solution)/shard_map/all_to_all | solution.py:147
  70.1 11.2 %collective-permute-start.3 = (f32[2,8,8,256]{3,2,1,0:T(8,128)S(1)}, f32[2,8,8,256]{3,2,1,0:T(8,128)S(1)}, u32[]{:S(2)}, u32[]{:S(2)}) collective-permute-start(f32[2,8,8,256]{3,2,1,0:T(8,128)S(1)} %dynamic-slice_bitcast_fusion.3), channel_id=1, source_target_pairs={{0,128},{32,160},{64,192},{96,224},{128,0},{160,32},{192,64},{224,... | collective-permute-start | bytes 393224 | tf_op jit(solution)/shard_map/ppermute | solution.py:111
  81.3 11.4 %collective-permute-start.4 = (f32[8,8,256]{2,1,0:T(8,128)S(1)}, f32[8,8,256]{2,1,0:T(8,128)S(1)}, u32[]{:S(2)}, u32[]{:S(2)}) collective-permute-start(f32[8,8,256]{2,1,0:T(8,128)S(1)} %dynamic-slice_bitcast_fusion.4), channel_id=1, source_target_pairs={{0,256},{32,288},{64,320},{96,352},{128,384},{160,416},{192,448},{... | collective-permute-start | bytes 196616 | tf_op jit(solution)/shard_map/ppermute | solution.py:111

commit v10 on v8

--- a/solution.py
+++ b/solution.py
@@ -77,28 +77,21 @@
     )(labels, data, tiles_t)
 
 
-def _ring_pairs(size_hi, size_lo, shift, along_lo):
-    pairs = []
-    for hi in range(size_hi):
-        for lo in range(size_lo):
-            if along_lo:
-                pairs.append((hi * size_lo + lo, hi * size_lo + (lo + shift) % size_lo))
-            else:
-                pairs.append((hi * size_lo + lo, ((hi + shift) % size_hi) * size_lo + lo))
-    return pairs
-
-
 def _chan_reduce(gradient):
     chunks = gradient.shape[0]
     size_lo = 4
     size_hi = chunks // size_lo
     c = lax.axis_index("chan")
     hi, lo = c // size_lo, c % size_lo
-    parts = gradient.reshape((size_hi, size_lo) + gradient.shape[1:])
-    acc = lax.dynamic_index_in_dim(parts, lo, 1, keepdims=False)
-    for k in range(1, size_lo):
-        piece = lax.dynamic_index_in_dim(parts, (lo + k) % size_lo, 1, keepdims=False)
-        acc = acc + lax.ppermute(piece, "chan", _ring_pairs(size_hi, size_lo, k, True))
+    acc = gradient.reshape((size_hi, 2, 2) + gradient.shape[1:])
+    for bit in (2, 1):
+        mine = (lo // bit) % 2
+        keep = lax.dynamic_index_in_dim(acc, mine, 1, keepdims=False)
+        give = lax.dynamic_index_in_dim(acc, 1 - mine, 1, keepdims=False)
+        pairs = [
+            (h * size_lo + l, h * size_lo + (l ^ bit)) for h in range(size_hi) for l in range(size_lo)
+        ]
+        acc = keep + lax.ppermute(give, "chan", pairs)
     for bit in (2, 1):
         halves = acc.reshape((2, acc.shape[0] // 2) + acc.shape[1:]) if bit == 2 else acc.reshape(
             (2, 1) + acc.shape[1:]

time: 93.1 us -> 103 us (1.11)
  the two profiles are of different devices: /device:TPU:10 before, /device:TPU:1 now
where the time goes in v10:
time: 103 us; the launch traced here: 102 us
  starting transfers between devices  42.2 us (41%)
  waiting for transfers between devices  32.7 us (32%)
  Pallas kernels  14.2 us (14%)
  local copies, waits for them, and re-layouts  6 us (6%)
  other arithmetic  5.76 us (6%)
  between operations  1.07 us (1%)
    ppermute x4, starting transfers between devices, _chan_reduce(): acc = keep + lax.ppermute(give, 'chan', pairs)  25.3 us
    ppermute x4, waiting for transfers between devices, _chan_reduce(): acc = keep + lax.ppermute(give, 'chan', pairs)  17.3 us
    all_to_all x1, waiting for transfers between devices, shards(): lax.all_to_all(outgoing, 'bl', split_axis=0, concat_axis=0, tiled=True)  15.5 us
    pallas_call x1, Pallas kernels, _grid_call(): pl.pallas_call(_grid_kernel, out_shape=(jax.ShapeDtypeStruct((slots, 2, v...  14.2 us
    all_to_all x1, starting transfers between devices, shards(): lax.all_to_all(outgoing, 'bl', split_axis=0, concat_axis=0, tiled=True)  10.6 us
    all_to_all x1, starting transfers between devices, shards(): lax.all_to_all(residual_all, 'bl', split_axis=0, concat_axis=0, tiled=True)  6.36 us
    unnamed x19, local copies, waits for them, and re-layouts  2.35 us
  transfers between devices with their start and end apart: 6, of which 4 were waited for; matrix products, arithmetic and copies ran while one was open for 2% of the time, Pallas kernels for 0%

profile of v10, /device:TPU:1, one launch (start us, length us, event | category | flops | bytes accessed | tf_op | source)
XLA Modules:
  0.0 102.0 jit_solution(14587036922309350634)
XLA Ops:
  0.6 0.0 copy-start
  0.6 0.7 fusion.7
  1.3 0.0 copy-done
  1.3 0.0 copy-start.7
  1.3 0.8 gather_fusion
  2.1 0.0 copy-done.7
  2.1 0.1 fusion.2
  2.2 0.0 copy-start.5
  2.2 0.1 reduce_window_sum.11
  2.3 0.2 select_reduce_fusion.1
  2.5 0.1 select_reduce_fusion
  2.6 0.1 fusion.1
  2.7 0.0 copy-start.8
  2.8 0.7 copy-done.8
  3.4 0.1 copy.15
  3.5 0.0 copy-done.5
  3.5 0.0 copy-start.4
  3.5 0.1 bitcast_add_fusion.4
  3.7 0.0 copy-start.6
  3.7 0.1 broadcast_in_dim.74
  3.8 0.6 copy-done.4
  4.4 0.1 copy-done.6
  4.5 0.1 pad_maximum_fusion
  4.6 0.8 gather_fusion.1
  5.3 0.0 copy-start.2
  5.4 1.1 %select_select_fusion = f32[128,6,128]{2,1,0:T(8,128)} fusion(f32[128,6,128]{2,1,0:T(8,128)S(1)} %gather_fusion.1, pred[128]{0:T(512)(128)(4,1)S(1)} %compare_and_fusion.1, pred[128]{0:T(512)(128)(4,1)S(1)} %fusion.1), kind=kLoop, calls=%fused_computation.6 | loop fusion | flops 196608 | bytes 786688 | tf_op jit(solution)/shard_map/jit(_where)/select_n | solution.py:134
  6.5 10.6 %all-to-all-start = ((f32[128,6,128]{2,1,0:T(8,128)}), f32[128,6,128]{2,1,0:T(8,128)S(1)}, u32[]{:S(2)}, u32[]{:S(2)}) async-start(f32[128,6,128]{2,1,0:T(8,128)} %select_select_fusion), calls=%async_computation | async-start | bytes 1048576 | tf_op jit(solution)/shard_map/all_to_all | solution.py:135
  17.1 0.0 copy-done.2
  17.1 1.0 copy.17
  18.1 15.5 %all-to-all-done.data_ref = f32[128,6,128]{2,1,0:T(8,128)S(1)} async-done(((f32[128,6,128]{2,1,0:T(8,128)}), f32[128,6,128]{2,1,0:T(8,128)S(1)}, u32[]{:S(2)}, u32[]{:S(2)}) %all-to-all-start) | async-done | bytes 393248 | tf_op jit(solution)/shard_map/all_to_all | solution.py:135
  33.6 0.0 copy-start.1
  33.6 1.0 %slice_reduce_fusion = f32[128]{0:T(128)S(1)} fusion(f32[128,6,128]{2,1,0:T(8,128)S(1)} %all-to-all-done.data_ref), kind=kLoop, calls=%fused_computation.12 | loop fusion | flops 16256 | bytes 66048 | tf_op jit(solution)/shard_map/reduce_max | solution.py:136
  34.6 0.5 convert_element_type.30.labels_ref
  35.2 0.0 copy-done.1
  35.2 14.2 %shard_map.86 = (f32[128,2,128]{2,1,0:T(2,128)}, f32[16,8,8,256]{3,2,1,0:T(8,128)}) custom-call(s32[128]{0:T(128)} %convert_element_type.30.labels_ref, f32[128,6,128]{2,1,0:T(8,128)} %copy-done.1, bf16[8,256,128]{2,1,0:T(8,128)(2,1)} %bitcast.66), custom_call_target="tpu_custom_call" | custom-call | tf_op jit(solution)/shard_map/pallas_call | solution.py:65
  49.4 0.0 copy-start.3
  49.4 1.2 %dynamic-slice_bitcast_fusion = f32[4,2,8,8,256]{4,3,2,1,0:T(8,128)S(1)} fusion(f32[4,2,2,8,8,256]{5,4,3,2,1,0:T(8,128)} %bitcast.67, s32[]{:T(128)S(6)} %select_n.226), kind=kLoop, calls=%fused_computation.4 | loop fusion | bytes 1048580 | tf_op jit(solution)/shard_map/jit(dynamic_index_in_dim)/squeeze | solution.py:90
  50.6 4.7 %collective-permute-start = (f32[4,2,8,8,256]{4,3,2,1,0:T(8,128)S(1)}, f32[4,2,8,8,256]{4,3,2,1,0:T(8,128)S(1)}, u32[]{:S(2)}, u32[]{:S(2)}) collective-permute-start(f32[4,2,8,8,256]{4,3,2,1,0:T(8,128)S(1)} %dynamic-slice_bitcast_fusion), channel_id=1, source_target_pairs={{0,64},{32,96},{64,0},{96,32},{128,192},{160,224},{192,128},{224,1... | collective-permute-start | bytes 1572872 | tf_op jit(solution)/shard_map/ppermute | solution.py:94
  55.3 10.8 %collective-permute-done = f32[4,2,8,8,256]{4,3,2,1,0:T(8,128)S(1)} collective-permute-done((f32[4,2,8,8,256]{4,3,2,1,0:T(8,128)S(1)}, f32[4,2,8,8,256]{4,3,2,1,0:T(8,128)S(1)}, u32[]{:S(2)}, u32[]{:S(2)}) %collective-permute-start) | collective-permute-done | bytes 524320 | tf_op jit(solution)/shard_map/ppermute | solution.py:94
  66.1 0.0 copy-done.3
  66.1 0.1 bitcast_add_fusion
  66.2 3.1 %collective-permute-start.1 = (f32[4,8,8,256]{3,2,1,0:T(8,128)S(1)}, f32[4,8,8,256]{3,2,1,0:T(8,128)S(1)}, u32[]{:S(2)}, u32[]{:S(2)}) collective-permute-start(f32[4,8,8,256]{3,2,1,0:T(8,128)S(1)} %dynamic-slice_bitcast_fusion.1), channel_id=1, source_target_pairs={{0,32},{32,0},{64,96},{96,64},{128,160},{160,128},{192,224},{224,1... | collective-permute-start | bytes 786440 | tf_op jit(solution)/shard_map/ppermute | solution.py:94
  69.4 6.4 %all-to-all-start.1 = ((f32[128,2,128]{2,1,0:T(2,128)}), f32[128,2,128]{2,1,0:T(2,128)S(1)}, u32[]{:S(2)}, u32[]{:S(2)}) async-start(f32[128,2,128]{2,1,0:T(2,128)} %get-tuple-element.5), calls=%async_computation.1 | async-start | bytes 262144 | tf_op jit(solution)/shard_map/all_to_all | solution.py:141
  75.8 0.0 collective-permute-done.1
  75.9 9.7 %collective-permute-start.2 = (f32[2,8,8,256]{3,2,1,0:T(8,128)S(1)}, f32[2,8,8,256]{3,2,1,0:T(8,128)S(1)}, u32[]{:S(2)}, u32[]{:S(2)}) collective-permute-start(f32[2,8,8,256]{3,2,1,0:T(8,128)S(1)} %dynamic-slice_bitcast_fusion.2), channel_id=1, source_target_pairs={{0,256},{32,288},{64,320},{96,352},{128,384},{160,416},{192,448},{... | collective-permute-start | bytes 393224 | tf_op jit(solution)/shard_map/ppermute | solution.py:105
  85.7 0.0 all-to-all-done.1
  85.7 0.7 gather_fusion.2
  86.4 3.4 %collective-permute-done.2 = f32[2,8,8,256]{3,2,1,0:T(8,128)S(1)} collective-permute-done((f32[2,8,8,256]{3,2,1,0:T(8,128)S(1)}, f32[2,8,8,256]{3,2,1,0:T(8,128)S(1)}, u32[]{:S(2)}, u32[]{:S(2)}) %collective-permute-start.2) | collective-permute-done | bytes 131104 | tf_op jit(solution)/shard_map/ppermute | solution.py:105
  89.8 7.8 %collective-permute-start.3 = (f32[1,8,8,256]{3,2,1,0:T(8,128)S(1)}, f32[1,8,8,256]{3,2,1,0:T(8,128)S(1)}, u32[]{:S(2)}, u32[]{:S(2)}) collective-permute-start(f32[1,8,8,256]{3,2,1,0:T(8,128)S(1)} %constant_dynamic-slice_fusion), channel_id=1, source_target_pairs={{0,128},{32,160},{64,192},{96,224},{128,0},{160,32},{192,64},{224,... | collective-permute-start | bytes 196616 | tf_op jit(solution)/shard_map/ppermute | solution.py:105
  97.6 0.8 bitcast_select_fusion
  98.3 3.1 %collective-permute-done.3 = f32[1,8,8,256]{3,2,1,0:T(8,128)S(1)} collective-permute-done((f32[1,8,8,256]{3,2,1,0:T(8,128)S(1)}, f32[1,8,8,256]{3,2,1,0:T(8,128)S(1)}, u32[]{:S(2)}, u32[]{:S(2)}) %collective-permute-start.3) | collective-permute-done | bytes 65568 | tf_op jit(solution)/shard_map/ppermute | solution.py:105
  101.4 0.6 fusion
  (16 shorter events, 0.2 us)
Async XLA Ops:
  0.6 0.7 copy-start
  1.3 0.8 copy-start.7
  2.2 1.3 %copy-start.5 = (f32[1,64,2,128]{3,2,1,0:T(2,128)S(1)}, f32[1,64,2,128]{3,2,1,0:T(2,128)}, u32[]{:S(2)}) copy-start(f32[1,64,2,128]{3,2,1,0:T(2,128)} %param.11) | copy-start | bytes 196612
  2.7 0.7 copy-start.8
  3.5 0.8 copy-start.4
  3.7 0.8 copy-start.6
  5.3 11.8 %copy-start.2 = (f32[8,128,256]{2,1,0:T(8,128)S(1)}, f32[8,128,256]{2,1,0:T(8,128)}, u32[]{:S(2)}) copy-start(f32[8,128,256]{2,1,0:T(8,128)} %param.7) | copy-start | bytes 3145732
  6.5 27.1 %all-to-all-start = ((f32[128,6,128]{2,1,0:T(8,128)}), f32[128,6,128]{2,1,0:T(8,128)S(1)}, u32[]{:S(2)}, u32[]{:S(2)}) async-start(f32[128,6,128]{2,1,0:T(8,128)} %select_select_fusion), calls=%async_computation | async-start | bytes 1048576 | tf_op jit(solution)/shard_map/all_to_all | solution.py:135
  33.6 1.6 %copy-start.1 = (f32[128,6,128]{2,1,0:T(8,128)}, f32[128,6,128]{2,1,0:T(8,128)S(1)}, u32[]{:S(2)}) copy-start(f32[128,6,128]{2,1,0:T(8,128)S(1)} %all-to-all-done.data_ref) | copy-start | bytes 1179652
  49.4 16.7 %copy-start.3 = (f32[16,8,8,256]{3,2,1,0:T(8,128)S(1)}, f32[16,8,8,256]{3,2,1,0:T(8,128)}, u32[]{:S(2)}) copy-start(f32[16,8,8,256]{3,2,1,0:T(8,128)} %get-tuple-element.4) | copy-start | bytes 3145732
  50.6 15.6 %collective-permute-start = (f32[4,2,8,8,256]{4,3,2,1,0:T(8,128)S(1)}, f32[4,2,8,8,256]{4,3,2,1,0:T(8,128)S(1)}, u32[]{:S(2)}, u32[]{:S(2)}) collective-permute-start(f32[4,2,8,8,256]{4,3,2,1,0:T(8,128)S(1)} %dynamic-slice_bitcast_fusion), channel_id=1, source_target_pairs={{0,64},{32,96},{64,0},{96,32},{128,192},{160,224},{192,128},{224,1... | collective-permute-start | bytes 1572872 | tf_op jit(solution)/shard_map/ppermute | solution.py:94
  66.2 9.6 %collective-permute-start.1 = (f32[4,8,8,256]{3,2,1,0:T(8,128)S(1)}, f32[4,8,8,256]{3,2,1,0:T(8,128)S(1)}, u32[]{:S(2)}, u32[]{:S(2)}) collective-permute-start(f32[4,8,8,256]{3,2,1,0:T(8,128)S(1)} %dynamic-slice_bitcast_fusion.1), channel_id=1, source_target_pairs={{0,32},{32,0},{64,96},{96,64},{128,160},{160,128},{192,224},{224,1... | collective-permute-start | bytes 786440 | tf_op jit(solution)/shard_map/ppermute | solution.py:94
  69.4 16.3 %all-to-all-start.1 = ((f32[128,2,128]{2,1,0:T(2,128)}), f32[128,2,128]{2,1,0:T(2,128)S(1)}, u32[]{:S(2)}, u32[]{:S(2)}) async-start(f32[128,2,128]{2,1,0:T(2,128)} %get-tuple-element.5), calls=%async_computation.1 | async-start | bytes 262144 | tf_op jit(solution)/shard_map/all_to_all | solution.py:141
  75.9 13.8 %collective-permute-start.2 = (f32[2,8,8,256]{3,2,1,0:T(8,128)S(1)}, f32[2,8,8,256]{3,2,1,0:T(8,128)S(1)}, u32[]{:S(2)}, u32[]{:S(2)}) collective-permute-start(f32[2,8,8,256]{3,2,1,0:T(8,128)S(1)} %dynamic-slice_bitcast_fusion.2), channel_id=1, source_target_pairs={{0,256},{32,288},{64,320},{96,352},{128,384},{160,416},{192,448},{... | collective-permute-start | bytes 393224 | tf_op jit(solution)/shard_map/ppermute | solution.py:105
  89.8 11.6 %collective-permute-start.3 = (f32[1,8,8,256]{3,2,1,0:T(8,128)S(1)}, f32[1,8,8,256]{3,2,1,0:T(8,128)S(1)}, u32[]{:S(2)}, u32[]{:S(2)}) collective-permute-start(f32[1,8,8,256]{3,2,1,0:T(8,128)S(1)} %constant_dynamic-slice_fusion), channel_id=1, source_target_pairs={{0,128},{32,160},{64,192},{96,224},{128,0},{160,32},{192,64},{224,... | collective-permute-start | bytes 196616 | tf_op jit(solution)/shard_map/ppermute | solution.py:105

commit v11 on v8

--- a/solution.py
+++ b/solution.py
@@ -55,7 +55,7 @@
         grad_ref[:, pl.ds(tile, 1)] += contrib.reshape(chunks, 1, rows, 2 * width)
         return carry
 
-    lax.fori_loop(0, slots, body, 0, unroll=16)
+    lax.fori_loop(0, slots, body, 0, unroll=32)
 
 
 def _grid_call(labels, data, tiles_t, chunks):
@@ -137,10 +137,11 @@
     payload = jnp.concatenate([observed[0], weights[0][:, None, :], coords, label_row], axis=1)
     match = send_slot[None, :] == jnp.arange(slots_all, dtype=jnp.int32)[:, None]
     source = jnp.sum(jnp.where(match, jnp.arange(block_count, dtype=jnp.int32)[None, :], 0), axis=1)
-    filled = jnp.any(match, axis=1)
-    outgoing = jnp.where(filled[:, None, None], jnp.take(payload, source, axis=0), 0.0)
+    source = jnp.where(jnp.any(match, axis=1), source, block_count)
+    padded = jnp.concatenate([payload, jnp.zeros((1,) + payload.shape[1:], payload.dtype)], axis=0)
+    outgoing = jnp.take(padded, source, axis=0)
     incoming = lax.all_to_all(outgoing, "bl", split_axis=0, concat_axis=0, tiled=True)
-    labels = jnp.max(incoming[:, 5, :], axis=1).astype(jnp.int32)
+    labels = jnp.max(incoming[:, 5, :].astype(jnp.int32), axis=1)
     tiles_t = jnp.swapaxes(grid.astype(jnp.bfloat16), 1, 2)
     residual_all, gradient = _grid_call(labels, incoming, tiles_t, chan)
     share_rows = tile_width // chan

time: 93.1 us -> 93.6 us (level)
  other arithmetic: 6.67 us -> 7.87 us
    reduce_max x1, other arithmetic: 1.03 us -> 2.87 us  [shards(): labels = jnp.max(incoming[:, 5, :].astype(jnp.int32), axis=1)]
where the time goes in v11:
time: 93.6 us; the launch traced here: 93 us
  starting transfers between devices  38.9 us (42%)
  waiting for transfers between devices  25.8 us (28%)
  Pallas kernels  13.5 us (14%)
  other arithmetic  7.87 us (8%)
  local copies, waits for them, and re-layouts  5.96 us (6%)
  between operations  1.05 us (1%)
    all_to_all x1, waiting for transfers between devices, shards(): lax.all_to_all(outgoing, 'bl', split_axis=0, concat_axis=0, tiled=True)  15.7 us
    ppermute x2, starting transfers between devices, _chan_reduce(): acc = keep + lax.ppermute(give, 'chan', pairs)  14.8 us
    pallas_call x1, Pallas kernels, _grid_call(): pl.pallas_call(_grid_kernel, out_shape=(jax.ShapeDtypeStruct((slots, 2, v...  13.5 us
    ppermute x3, starting transfers between devices, _chan_reduce(): lax.ppermute(piece, 'chan', _ring_pairs(size_hi, size_lo, k, True))  9.88 us
    all_to_all x1, starting transfers between devices, shards(): lax.all_to_all(outgoing, 'bl', split_axis=0, concat_axis=0, tiled=True)  9.51 us
    ppermute x2, waiting for transfers between devices, _chan_reduce(): acc = keep + lax.ppermute(give, 'chan', pairs)  5.46 us
    all_to_all x1, starting transfers between devices, shards(): lax.all_to_all(residual_all, 'bl', split_axis=0, concat_axis=0, tiled=True)  4.65 us
    ppermute x3, waiting for transfers between devices, _chan_reduce(): lax.ppermute(piece, 'chan', _ring_pairs(size_hi, size_lo, k, True))  4.6 us
  transfers between devices with their start and end apart: 7, of which 4 were waited for; matrix products, arithmetic and copies ran while one was open for 4% of the time, Pallas kernels for 0%

profile of v11, /device:TPU:10, one launch (start us, length us, event | category | flops | bytes accessed | tf_op | source)
XLA Modules:
  0.0 93.0 jit_solution(3952874793661894145)
XLA Ops:
  0.6 0.0 copy-start
  0.6 0.7 fusion.10
  1.3 0.0 copy-done
  1.3 0.0 copy-start.6
  1.3 0.8 gather_fusion
  2.1 0.0 copy-done.6
  2.1 0.1 fusion.5
  2.2 0.0 copy-start.4
  2.2 0.1 reduce_window_sum.11
  2.3 0.2 select_reduce_fusion.1
  2.5 0.1 select_reduce_fusion
  2.6 0.1 fusion.4
  2.7 0.0 copy-start.7
  2.8 0.7 copy-done.7
  3.4 0.1 copy.15
  3.5 0.0 copy-done.4
  3.5 0.0 copy-start.3
  3.5 0.1 bitcast_add_fusion.3
  3.7 0.0 copy-start.5
  3.7 0.1 broadcast_in_dim.66
  3.8 0.6 copy-done.3
  4.4 0.1 copy-done.5
  4.5 0.1 select_maximum_fusion
  4.6 0.8 gather_fusion.1
  5.3 0.0 copy-start.2
  5.4 1.0 %broadcast_select_fusion = f32[128,6,128]{2,1,0:T(8,128)} fusion(f32[128,6,128]{2,1,0:T(8,128)S(1)} %gather_fusion.1, pred[128]{0:T(512)(128)(4,1)S(1)} %compare_and_fusion.1), kind=kLoop, calls=%fused_computation.14 | loop fusion | flops 98304 | bytes 786560 | tf_op jit(solution)/shard_map/jit(_take)/select_n | solution.py:142
  6.4 9.5 %all-to-all-start = ((f32[128,6,128]{2,1,0:T(8,128)}), f32[128,6,128]{2,1,0:T(8,128)S(1)}, u32[]{:S(2)}, u32[]{:S(2)}) async-start(f32[128,6,128]{2,1,0:T(8,128)} %broadcast_select_fusion), calls=%async_computation | async-start | bytes 1048576 | tf_op jit(solution)/shard_map/all_to_all | solution.py:143
  15.9 0.0 copy-done.2
  16.0 1.0 %copy.17 = bf16[8,128,256]{1,2,0:T(8,128)(2,1)} copy(f32[8,128,256]{2,1,0:T(8,128)S(1)} %copy-done.2) | data formatting | bytes 1572864 | tf_op args[0]
  17.0 15.7 %all-to-all-done.data_ref = f32[128,6,128]{2,1,0:T(8,128)S(1)} async-done(((f32[128,6,128]{2,1,0:T(8,128)}), f32[128,6,128]{2,1,0:T(8,128)S(1)}, u32[]{:S(2)}, u32[]{:S(2)}) %all-to-all-start) | async-done | bytes 393248 | tf_op jit(solution)/shard_map/all_to_all | solution.py:143
  32.7 0.0 copy-start.1
  32.7 2.9 %fusion.2.labels_ref = s32[128]{0:T(128)} fusion(f32[128,6,128]{2,1,0:T(8,128)S(1)} %all-to-all-done.data_ref), kind=kLoop, calls=%fused_computation.18 | loop fusion | flops 32640 | bytes 66048 | tf_op jit(solution)/shard_map/reduce_max | solution.py:144
  35.5 0.0 copy-done.1
  35.5 13.5 %shard_map.86 = (f32[128,2,128]{2,1,0:T(2,128)}, f32[16,8,8,256]{3,2,1,0:T(8,128)}) custom-call(s32[128]{0:T(128)} %fusion.2.labels_ref, f32[128,6,128]{2,1,0:T(8,128)} %copy-done.1, bf16[8,256,128]{2,1,0:T(8,128)(2,1)} %bitcast.70), custom_call_target="tpu_custom_call" | custom-call | tf_op jit(solution)/shard_map/pallas_call | solution.py:65
  49.0 1.2 %dynamic-slice_bitcast_fusion.2 = (f32[4,8,8,256]{3,2,1,0:T(8,128)S(1)}, f32[4,8,8,256]{3,2,1,0:T(8,128)S(1)}, f32[4,8,8,256]{3,2,1,0:T(8,128)S(1)}) fusion(f32[4,4,8,8,256]{4,3,2,1,0:T(8,128)} %bitcast.71, s32[]{:T(128)S(6)} %select_n.237, s32[]{:T(128)S(6)} %select_n.241, s32[]{:T(128)S(6)} %select_n.239), kind=kLoop, calls=%fused_computation.13 | loop fusion | bytes 1572876 | tf_op jit(solution)/shard_map/jit(dynamic_index_in_dim)/squeeze | solution.py:100
  50.2 3.4 %collective-permute-start = (f32[4,8,8,256]{3,2,1,0:T(8,128)S(1)}, f32[4,8,8,256]{3,2,1,0:T(8,128)S(1)}, u32[]{:S(2)}, u32[]{:S(2)}) collective-permute-start(f32[4,8,8,256]{3,2,1,0:T(8,128)S(1)} %get-tuple-element.8), channel_id=1, source_target_pairs={{0,32},{32,64},{64,96},{96,0},{128,160},{160,192},{192,224},{224,1... | collective-permute-start | bytes 786440 | tf_op jit(solution)/shard_map/ppermute | solution.py:101
  53.6 2.4 %collective-permute-start.2 = (f32[4,8,8,256]{3,2,1,0:T(8,128)S(1)}, f32[4,8,8,256]{3,2,1,0:T(8,128)S(1)}, u32[]{:S(2)}, u32[]{:S(2)}) collective-permute-start(f32[4,8,8,256]{3,2,1,0:T(8,128)S(1)} %get-tuple-element.9), channel_id=1, source_target_pairs={{0,96},{32,0},{64,32},{96,64},{128,224},{160,128},{192,160},{224,1... | collective-permute-start | bytes 786440 | tf_op jit(solution)/shard_map/ppermute | solution.py:101
  56.1 4.0 %collective-permute-start.1 = (f32[4,8,8,256]{3,2,1,0:T(8,128)S(1)}, f32[4,8,8,256]{3,2,1,0:T(8,128)S(1)}, u32[]{:S(2)}, u32[]{:S(2)}) collective-permute-start(f32[4,8,8,256]{3,2,1,0:T(8,128)S(1)} %get-tuple-element.10), channel_id=1, source_target_pairs={{0,64},{32,96},{64,0},{96,32},{128,192},{160,224},{192,128},{224,1... | collective-permute-start | bytes 786440 | tf_op jit(solution)/shard_map/ppermute | solution.py:101
  60.2 4.7 %all-to-all-start.1 = ((f32[128,2,128]{2,1,0:T(2,128)}), f32[128,2,128]{2,1,0:T(2,128)S(1)}, u32[]{:S(2)}, u32[]{:S(2)}) async-start(f32[128,2,128]{2,1,0:T(2,128)} %get-tuple-element.5), calls=%async_computation.1 | async-start | bytes 262144 | tf_op jit(solution)/shard_map/all_to_all | solution.py:149
  64.9 0.0 collective-permute-done
  64.9 0.0 collective-permute-done.2
  64.9 4.6 %collective-permute-done.1 = f32[4,8,8,256]{3,2,1,0:T(8,128)S(1)} collective-permute-done((f32[4,8,8,256]{3,2,1,0:T(8,128)S(1)}, f32[4,8,8,256]{3,2,1,0:T(8,128)S(1)}, u32[]{:S(2)}, u32[]{:S(2)}) %collective-permute-start.1) | collective-permute-done | bytes 262176 | tf_op jit(solution)/shard_map/ppermute | solution.py:101
  69.5 1.0 %fusion.1 = f32[4,8,8,256]{3,2,1,0:T(8,128)S(1)} fusion(f32[4,8,8,256]{3,2,1,0:T(8,128)S(1)} %collective-permute-done.2, f32[4,8,8,256]{3,2,1,0:T(8,128)S(1)} %collective-permute-done.1, f32[4,8,8,256]{3,2,1,0:T(8,128)S(1)} %collective-permute-done, f32[4,4,8,8,256]{4,3,2,1,0:T(8,128)} %bitcast.72, s32[]{:T(128)S(6)} %select_n.235), kind=kLoop, calls=%fused_computation.10 | loop fusion | flops 196608 | bytes 1310724 | tf_op jit(solution)/shard_map/add | solution.py:101
  70.6 10.0 %collective-permute-start.3 = (f32[2,8,8,256]{3,2,1,0:T(8,128)S(1)}, f32[2,8,8,256]{3,2,1,0:T(8,128)S(1)}, u32[]{:S(2)}, u32[]{:S(2)}) collective-permute-start(f32[2,8,8,256]{3,2,1,0:T(8,128)S(1)} %dynamic-slice_bitcast_fusion.3), channel_id=1, source_target_pairs={{0,256},{32,288},{64,320},{96,352},{128,384},{160,416},{192,448},{... | collective-permute-start | bytes 393224 | tf_op jit(solution)/shard_map/ppermute | solution.py:112
  80.6 0.0 all-to-all-done.1
  80.6 0.7 gather_fusion.2
  81.3 4.0 %collective-permute-done.3 = f32[2,8,8,256]{3,2,1,0:T(8,128)S(1)} collective-permute-done((f32[2,8,8,256]{3,2,1,0:T(8,128)S(1)}, f32[2,8,8,256]{3,2,1,0:T(8,128)S(1)}, u32[]{:S(2)}, u32[]{:S(2)}) %collective-permute-start.3) | collective-permute-done | bytes 131104 | tf_op jit(solution)/shard_map/ppermute | solution.py:112
  85.3 4.8 %collective-permute-start.4 = (f32[1,8,8,256]{3,2,1,0:T(8,128)S(1)}, f32[1,8,8,256]{3,2,1,0:T(8,128)S(1)}, u32[]{:S(2)}, u32[]{:S(2)}) collective-permute-start(f32[1,8,8,256]{3,2,1,0:T(8,128)S(1)} %constant_dynamic-slice_fusion), channel_id=1, source_target_pairs={{0,128},{32,160},{64,192},{96,224},{128,0},{160,32},{192,64},{224,... | collective-permute-start | bytes 196616 | tf_op jit(solution)/shard_map/ppermute | solution.py:112
  90.1 0.8 bitcast_select_fusion
  90.9 1.5 %collective-permute-done.4 = f32[1,8,8,256]{3,2,1,0:T(8,128)S(1)} collective-permute-done((f32[1,8,8,256]{3,2,1,0:T(8,128)S(1)}, f32[1,8,8,256]{3,2,1,0:T(8,128)S(1)}, u32[]{:S(2)}, u32[]{:S(2)}) %collective-permute-start.4) | collective-permute-done | bytes 65568 | tf_op jit(solution)/shard_map/ppermute | solution.py:112
  92.4 0.6 fusion.3
  (14 shorter events, 0.2 us)
Async XLA Ops:
  0.6 0.7 copy-start
  1.3 0.8 copy-start.6
  2.2 1.3 %copy-start.4 = (f32[1,64,2,128]{3,2,1,0:T(2,128)S(1)}, f32[1,64,2,128]{3,2,1,0:T(2,128)}, u32[]{:S(2)}) copy-start(f32[1,64,2,128]{3,2,1,0:T(2,128)} %param.11) | copy-start | bytes 196612
  2.7 0.7 copy-start.7
  3.5 0.8 copy-start.3
  3.7 0.8 copy-start.5
  5.3 10.6 %copy-start.2 = (f32[8,128,256]{2,1,0:T(8,128)S(1)}, f32[8,128,256]{2,1,0:T(8,128)}, u32[]{:S(2)}) copy-start(f32[8,128,256]{2,1,0:T(8,128)} %param.7) | copy-start | bytes 3145732
  6.4 26.3 %all-to-all-start = ((f32[128,6,128]{2,1,0:T(8,128)}), f32[128,6,128]{2,1,0:T(8,128)S(1)}, u32[]{:S(2)}, u32[]{:S(2)}) async-start(f32[128,6,128]{2,1,0:T(8,128)} %broadcast_select_fusion), calls=%async_computation | async-start | bytes 1048576 | tf_op jit(solution)/shard_map/all_to_all | solution.py:143
  32.7 2.9 %copy-start.1 = (f32[128,6,128]{2,1,0:T(8,128)}, f32[128,6,128]{2,1,0:T(8,128)S(1)}, u32[]{:S(2)}) copy-start(f32[128,6,128]{2,1,0:T(8,128)S(1)} %all-to-all-done.data_ref) | copy-start | bytes 1179652
  50.2 14.7 %collective-permute-start = (f32[4,8,8,256]{3,2,1,0:T(8,128)S(1)}, f32[4,8,8,256]{3,2,1,0:T(8,128)S(1)}, u32[]{:S(2)}, u32[]{:S(2)}) collective-permute-start(f32[4,8,8,256]{3,2,1,0:T(8,128)S(1)} %get-tuple-element.8), channel_id=1, source_target_pairs={{0,32},{32,64},{64,96},{96,0},{128,160},{160,192},{192,224},{224,1... | collective-permute-start | bytes 786440 | tf_op jit(solution)/shard_map/ppermute | solution.py:101
  53.6 11.2 %collective-permute-start.2 = (f32[4,8,8,256]{3,2,1,0:T(8,128)S(1)}, f32[4,8,8,256]{3,2,1,0:T(8,128)S(1)}, u32[]{:S(2)}, u32[]{:S(2)}) collective-permute-start(f32[4,8,8,256]{3,2,1,0:T(8,128)S(1)} %get-tuple-element.9), channel_id=1, source_target_pairs={{0,96},{32,0},{64,32},{96,64},{128,224},{160,128},{192,160},{224,1... | collective-permute-start | bytes 786440 | tf_op jit(solution)/shard_map/ppermute | solution.py:101
  56.1 13.4 %collective-permute-start.1 = (f32[4,8,8,256]{3,2,1,0:T(8,128)S(1)}, f32[4,8,8,256]{3,2,1,0:T(8,128)S(1)}, u32[]{:S(2)}, u32[]{:S(2)}) collective-permute-start(f32[4,8,8,256]{3,2,1,0:T(8,128)S(1)} %get-tuple-element.10), channel_id=1, source_target_pairs={{0,64},{32,96},{64,0},{96,32},{128,192},{160,224},{192,128},{224,1... | collective-permute-start | bytes 786440 | tf_op jit(solution)/shard_map/ppermute | solution.py:101
  60.2 20.4 %all-to-all-start.1 = ((f32[128,2,128]{2,1,0:T(2,128)}), f32[128,2,128]{2,1,0:T(2,128)S(1)}, u32[]{:S(2)}, u32[]{:S(2)}) async-start(f32[128,2,128]{2,1,0:T(2,128)} %get-tuple-element.5), calls=%async_computation.1 | async-start | bytes 262144 | tf_op jit(solution)/shard_map/all_to_all | solution.py:149
  70.6 14.7 %collective-permute-start.3 = (f32[2,8,8,256]{3,2,1,0:T(8,128)S(1)}, f32[2,8,8,256]{3,2,1,0:T(8,128)S(1)}, u32[]{:S(2)}, u32[]{:S(2)}) collective-permute-start(f32[2,8,8,256]{3,2,1,0:T(8,128)S(1)} %dynamic-slice_bitcast_fusion.3), channel_id=1, source_target_pairs={{0,256},{32,288},{64,320},{96,352},{128,384},{160,416},{192,448},{... | collective-permute-start | bytes 393224 | tf_op jit(solution)/shard_map/ppermute | solution.py:112
  85.3 7.1 %collective-permute-start.4 = (f32[1,8,8,256]{3,2,1,0:T(8,128)S(1)}, f32[1,8,8,256]{3,2,1,0:T(8,128)S(1)}, u32[]{:S(2)}, u32[]{:S(2)}) collective-permute-start(f32[1,8,8,256]{3,2,1,0:T(8,128)S(1)} %constant_dynamic-slice_fusion), channel_id=1, source_target_pairs={{0,128},{32,160},{64,192},{96,224},{128,0},{160,32},{192,64},{224,... | collective-permute-start | bytes 196616 | tf_op jit(solution)/shard_map/ppermute | solution.py:112

commit v12 on v11

--- a/solution.py
+++ b/solution.py
@@ -141,7 +141,7 @@
     padded = jnp.concatenate([payload, jnp.zeros((1,) + payload.shape[1:], payload.dtype)], axis=0)
     outgoing = jnp.take(padded, source, axis=0)
     incoming = lax.all_to_all(outgoing, "bl", split_axis=0, concat_axis=0, tiled=True)
-    labels = jnp.max(incoming[:, 5, :].astype(jnp.int32), axis=1)
+    labels = jnp.max(incoming[:, 5, :], axis=1).astype(jnp.int32)
     tiles_t = jnp.swapaxes(grid.astype(jnp.bfloat16), 1, 2)
     residual_all, gradient = _grid_call(labels, incoming, tiles_t, chan)
     share_rows = tile_width // chan

time: 93.6 us -> 92.3 us (0.986)
  other arithmetic: 7.87 us -> 6.55 us
    reduce_max x1, other arithmetic: 2.87 us -> 1.03 us  [shards(): labels = jnp.max(incoming[:, 5, :], axis=1).astype(jnp.int32)]
where the time goes in v12:
time: 92.3 us; the launch traced here: 91.7 us
  starting transfers between devices  38.9 us (42%)
  waiting for transfers between devices  25.8 us (28%)
  Pallas kernels  13.5 us (15%)
  other arithmetic  6.55 us (7%)
  local copies, waits for them, and re-layouts  5.96 us (6%)
  between operations  1.06 us (1%)
    all_to_all x1, waiting for transfers between devices, shards(): lax.all_to_all(outgoing, 'bl', split_axis=0, concat_axis=0, tiled=True)  15.7 us
    ppermute x2, starting transfers between devices, _chan_reduce(): acc = keep + lax.ppermute(give, 'chan', pairs)  14.9 us
    pallas_call x1, Pallas kernels, _grid_call(): pl.pallas_call(_grid_kernel, out_shape=(jax.ShapeDtypeStruct((slots, 2, v...  13.5 us
    ppermute x3, starting transfers between devices, _chan_reduce(): lax.ppermute(piece, 'chan', _ring_pairs(size_hi, size_lo, k, True))  9.89 us
    all_to_all x1, starting transfers between devices, shards(): lax.all_to_all(outgoing, 'bl', split_axis=0, concat_axis=0, tiled=True)  9.51 us
    ppermute x2, waiting for transfers between devices, _chan_reduce(): acc = keep + lax.ppermute(give, 'chan', pairs)  5.37 us
    ppermute x3, waiting for transfers between devices, _chan_reduce(): lax.ppermute(piece, 'chan', _ring_pairs(size_hi, size_lo, k, True))  4.7 us
    all_to_all x1, starting transfers between devices, shards(): lax.all_to_all(residual_all, 'bl', split_axis=0, concat_axis=0, tiled=True)  4.62 us
  transfers between devices with their start and end apart: 7, of which 4 were waited for; matrix products, arithmetic and copies ran while one was open for 4% of the time, Pallas kernels for 0%

profile of v12, /device:TPU:10, one launch (start us, length us, event | category | flops | bytes accessed | tf_op | source)
XLA Modules:
  0.0 91.7 jit_solution(2011205741544329483)
XLA Ops:
  0.6 0.0 copy-start
  0.6 0.7 fusion.9
  1.3 0.0 copy-done
  1.3 0.0 copy-start.6
  1.3 0.8 gather_fusion
  2.1 0.0 copy-done.6
  2.1 0.1 fusion.4
  2.2 0.0 copy-start.4
  2.2 0.1 reduce_window_sum.11
  2.3 0.2 select_reduce_fusion.1
  2.5 0.1 select_reduce_fusion
  2.6 0.1 fusion.3
  2.7 0.0 copy-start.7
  2.8 0.7 copy-done.7
  3.4 0.1 copy.15
  3.5 0.0 copy-done.4
  3.5 0.0 copy-start.3
  3.5 0.1 bitcast_add_fusion.3
  3.7 0.0 copy-start.5
  3.7 0.1 broadcast_in_dim.66
  3.8 0.6 copy-done.3
  4.4 0.1 copy-done.5
  4.5 0.1 select_maximum_fusion
  4.6 0.8 gather_fusion.1
  5.3 0.0 copy-start.2
  5.4 1.0 %broadcast_select_fusion = f32[128,6,128]{2,1,0:T(8,128)} fusion(f32[128,6,128]{2,1,0:T(8,128)S(1)} %gather_fusion.1, pred[128]{0:T(512)(128)(4,1)S(1)} %compare_and_fusion.1), kind=kLoop, calls=%fused_computation.14 | loop fusion | flops 98304 | bytes 786560 | tf_op jit(solution)/shard_map/jit(_take)/select_n | solution.py:142
  6.4 9.5 %all-to-all-start = ((f32[128,6,128]{2,1,0:T(8,128)}), f32[128,6,128]{2,1,0:T(8,128)S(1)}, u32[]{:S(2)}, u32[]{:S(2)}) async-start(f32[128,6,128]{2,1,0:T(8,128)} %broadcast_select_fusion), calls=%async_computation | async-start | bytes 1048576 | tf_op jit(solution)/shard_map/all_to_all | solution.py:143
  15.9 0.0 copy-done.2
  16.0 1.0 %copy.17 = bf16[8,128,256]{1,2,0:T(8,128)(2,1)} copy(f32[8,128,256]{2,1,0:T(8,128)S(1)} %copy-done.2) | data formatting | bytes 1572864 | tf_op args[0]
  17.0 15.7 %all-to-all-done.data_ref = f32[128,6,128]{2,1,0:T(8,128)S(1)} async-done(((f32[128,6,128]{2,1,0:T(8,128)}), f32[128,6,128]{2,1,0:T(8,128)S(1)}, u32[]{:S(2)}, u32[]{:S(2)}) %all-to-all-start) | async-done | bytes 393248 | tf_op jit(solution)/shard_map/all_to_all | solution.py:143
  32.7 0.0 copy-start.1
  32.7 1.0 %slice_reduce_fusion = f32[128]{0:T(128)S(1)} fusion(f32[128,6,128]{2,1,0:T(8,128)S(1)} %all-to-all-done.data_ref), kind=kLoop, calls=%fused_computation.17 | loop fusion | flops 16256 | bytes 66048 | tf_op jit(solution)/shard_map/reduce_max | solution.py:144
  33.7 0.5 convert_element_type.30.labels_ref
  34.2 0.0 copy-done.1
  34.2 13.5 %shard_map.86 = (f32[128,2,128]{2,1,0:T(2,128)}, f32[16,8,8,256]{3,2,1,0:T(8,128)}) custom-call(s32[128]{0:T(128)} %convert_element_type.30.labels_ref, f32[128,6,128]{2,1,0:T(8,128)} %copy-done.1, bf16[8,256,128]{2,1,0:T(8,128)(2,1)} %bitcast.70), custom_call_target="tpu_custom_call" | custom-call | tf_op jit(solution)/shard_map/pallas_call | solution.py:65
  47.7 1.2 %dynamic-slice_bitcast_fusion.2 = (f32[4,8,8,256]{3,2,1,0:T(8,128)S(1)}, f32[4,8,8,256]{3,2,1,0:T(8,128)S(1)}, f32[4,8,8,256]{3,2,1,0:T(8,128)S(1)}) fusion(f32[4,4,8,8,256]{4,3,2,1,0:T(8,128)} %bitcast.71, s32[]{:T(128)S(6)} %select_n.237, s32[]{:T(128)S(6)} %select_n.241, s32[]{:T(128)S(6)} %select_n.239), kind=kLoop, calls=%fused_computation.13 | loop fusion | bytes 1572876 | tf_op jit(solution)/shard_map/jit(dynamic_index_in_dim)/squeeze | solution.py:100
  48.9 3.4 %collective-permute-start = (f32[4,8,8,256]{3,2,1,0:T(8,128)S(1)}, f32[4,8,8,256]{3,2,1,0:T(8,128)S(1)}, u32[]{:S(2)}, u32[]{:S(2)}) collective-permute-start(f32[4,8,8,256]{3,2,1,0:T(8,128)S(1)} %get-tuple-element.8), channel_id=1, source_target_pairs={{0,32},{32,64},{64,96},{96,0},{128,160},{160,192},{192,224},{224,1... | collective-permute-start | bytes 786440 | tf_op jit(solution)/shard_map/ppermute | solution.py:101
  52.3 2.4 %collective-permute-start.2 = (f32[4,8,8,256]{3,2,1,0:T(8,128)S(1)}, f32[4,8,8,256]{3,2,1,0:T(8,128)S(1)}, u32[]{:S(2)}, u32[]{:S(2)}) collective-permute-start(f32[4,8,8,256]{3,2,1,0:T(8,128)S(1)} %get-tuple-element.9), channel_id=1, source_target_pairs={{0,96},{32,0},{64,32},{96,64},{128,224},{160,128},{192,160},{224,1... | collective-permute-start | bytes 786440 | tf_op jit(solution)/shard_map/ppermute | solution.py:101
  54.7 4.0 %collective-permute-start.1 = (f32[4,8,8,256]{3,2,1,0:T(8,128)S(1)}, f32[4,8,8,256]{3,2,1,0:T(8,128)S(1)}, u32[]{:S(2)}, u32[]{:S(2)}) collective-permute-start(f32[4,8,8,256]{3,2,1,0:T(8,128)S(1)} %get-tuple-element.10), channel_id=1, source_target_pairs={{0,64},{32,96},{64,0},{96,32},{128,192},{160,224},{192,128},{224,1... | collective-permute-start | bytes 786440 | tf_op jit(solution)/shard_map/ppermute | solution.py:101
  58.9 4.6 %all-to-all-start.1 = ((f32[128,2,128]{2,1,0:T(2,128)}), f32[128,2,128]{2,1,0:T(2,128)S(1)}, u32[]{:S(2)}, u32[]{:S(2)}) async-start(f32[128,2,128]{2,1,0:T(2,128)} %get-tuple-element.5), calls=%async_computation.1 | async-start | bytes 262144 | tf_op jit(solution)/shard_map/all_to_all | solution.py:149
  63.5 0.0 collective-permute-done
  63.5 0.0 collective-permute-done.2
  63.5 4.7 %collective-permute-done.1 = f32[4,8,8,256]{3,2,1,0:T(8,128)S(1)} collective-permute-done((f32[4,8,8,256]{3,2,1,0:T(8,128)S(1)}, f32[4,8,8,256]{3,2,1,0:T(8,128)S(1)}, u32[]{:S(2)}, u32[]{:S(2)}) %collective-permute-start.1) | collective-permute-done | bytes 262176 | tf_op jit(solution)/shard_map/ppermute | solution.py:101
  68.2 1.0 %fusion.1 = f32[4,8,8,256]{3,2,1,0:T(8,128)S(1)} fusion(f32[4,8,8,256]{3,2,1,0:T(8,128)S(1)} %collective-permute-done.2, f32[4,8,8,256]{3,2,1,0:T(8,128)S(1)} %collective-permute-done.1, f32[4,8,8,256]{3,2,1,0:T(8,128)S(1)} %collective-permute-done, f32[4,4,8,8,256]{4,3,2,1,0:T(8,128)} %bitcast.72, s32[]{:T(128)S(6)} %select_n.235), kind=kLoop, calls=%fused_computation.10 | loop fusion | flops 196608 | bytes 1310724 | tf_op jit(solution)/shard_map/add | solution.py:101
  69.3 9.9 %collective-permute-start.3 = (f32[2,8,8,256]{3,2,1,0:T(8,128)S(1)}, f32[2,8,8,256]{3,2,1,0:T(8,128)S(1)}, u32[]{:S(2)}, u32[]{:S(2)}) collective-permute-start(f32[2,8,8,256]{3,2,1,0:T(8,128)S(1)} %dynamic-slice_bitcast_fusion.3), channel_id=1, source_target_pairs={{0,256},{32,288},{64,320},{96,352},{128,384},{160,416},{192,448},{... | collective-permute-start | bytes 393224 | tf_op jit(solution)/shard_map/ppermute | solution.py:112
  79.3 0.0 all-to-all-done.1
  79.3 0.7 gather_fusion.2
  80.0 3.9 %collective-permute-done.3 = f32[2,8,8,256]{3,2,1,0:T(8,128)S(1)} collective-permute-done((f32[2,8,8,256]{3,2,1,0:T(8,128)S(1)}, f32[2,8,8,256]{3,2,1,0:T(8,128)S(1)}, u32[]{:S(2)}, u32[]{:S(2)}) %collective-permute-start.3) | collective-permute-done | bytes 131104 | tf_op jit(solution)/shard_map/ppermute | solution.py:112
  83.9 4.9 %collective-permute-start.4 = (f32[1,8,8,256]{3,2,1,0:T(8,128)S(1)}, f32[1,8,8,256]{3,2,1,0:T(8,128)S(1)}, u32[]{:S(2)}, u32[]{:S(2)}) collective-permute-start(f32[1,8,8,256]{3,2,1,0:T(8,128)S(1)} %constant_dynamic-slice_fusion), channel_id=1, source_target_pairs={{0,128},{32,160},{64,192},{96,224},{128,0},{160,32},{192,64},{224,... | collective-permute-start | bytes 196616 | tf_op jit(solution)/shard_map/ppermute | solution.py:112
  88.8 0.8 bitcast_select_fusion
  89.6 1.5 %collective-permute-done.4 = f32[1,8,8,256]{3,2,1,0:T(8,128)S(1)} collective-permute-done((f32[1,8,8,256]{3,2,1,0:T(8,128)S(1)}, f32[1,8,8,256]{3,2,1,0:T(8,128)S(1)}, u32[]{:S(2)}, u32[]{:S(2)}) %collective-permute-start.4) | collective-permute-done | bytes 65568 | tf_op jit(solution)/shard_map/ppermute | solution.py:112
  91.1 0.6 fusion.2
  (14 shorter events, 0.2 us)
Async XLA Ops:
  0.6 0.7 copy-start
  1.3 0.8 copy-start.6
  2.2 1.3 %copy-start.4 = (f32[1,64,2,128]{3,2,1,0:T(2,128)S(1)}, f32[1,64,2,128]{3,2,1,0:T(2,128)}, u32[]{:S(2)}) copy-start(f32[1,64,2,128]{3,2,1,0:T(2,128)} %param.11) | copy-start | bytes 196612
  2.7 0.7 copy-start.7
  3.5 0.8 copy-start.3
  3.7 0.8 copy-start.5
  5.3 10.6 %copy-start.2 = (f32[8,128,256]{2,1,0:T(8,128)S(1)}, f32[8,128,256]{2,1,0:T(8,128)}, u32[]{:S(2)}) copy-start(f32[8,128,256]{2,1,0:T(8,128)} %param.7) | copy-start | bytes 3145732
  6.4 26.3 %all-to-all-start = ((f32[128,6,128]{2,1,0:T(8,128)}), f32[128,6,128]{2,1,0:T(8,128)S(1)}, u32[]{:S(2)}, u32[]{:S(2)}) async-start(f32[128,6,128]{2,1,0:T(8,128)} %broadcast_select_fusion), calls=%async_computation | async-start | bytes 1048576 | tf_op jit(solution)/shard_map/all_to_all | solution.py:143
  32.7 1.6 %copy-start.1 = (f32[128,6,128]{2,1,0:T(8,128)}, f32[128,6,128]{2,1,0:T(8,128)S(1)}, u32[]{:S(2)}) copy-start(f32[128,6,128]{2,1,0:T(8,128)S(1)} %all-to-all-done.data_ref) | copy-start | bytes 1179652
  48.9 14.6 %collective-permute-start = (f32[4,8,8,256]{3,2,1,0:T(8,128)S(1)}, f32[4,8,8,256]{3,2,1,0:T(8,128)S(1)}, u32[]{:S(2)}, u32[]{:S(2)}) collective-permute-start(f32[4,8,8,256]{3,2,1,0:T(8,128)S(1)} %get-tuple-element.8), channel_id=1, source_target_pairs={{0,32},{32,64},{64,96},{96,0},{128,160},{160,192},{192,224},{224,1... | collective-permute-start | bytes 786440 | tf_op jit(solution)/shard_map/ppermute | solution.py:101
  52.3 11.2 %collective-permute-start.2 = (f32[4,8,8,256]{3,2,1,0:T(8,128)S(1)}, f32[4,8,8,256]{3,2,1,0:T(8,128)S(1)}, u32[]{:S(2)}, u32[]{:S(2)}) collective-permute-start(f32[4,8,8,256]{3,2,1,0:T(8,128)S(1)} %get-tuple-element.9), channel_id=1, source_target_pairs={{0,96},{32,0},{64,32},{96,64},{128,224},{160,128},{192,160},{224,1... | collective-permute-start | bytes 786440 | tf_op jit(solution)/shard_map/ppermute | solution.py:101
  54.7 13.5 %collective-permute-start.1 = (f32[4,8,8,256]{3,2,1,0:T(8,128)S(1)}, f32[4,8,8,256]{3,2,1,0:T(8,128)S(1)}, u32[]{:S(2)}, u32[]{:S(2)}) collective-permute-start(f32[4,8,8,256]{3,2,1,0:T(8,128)S(1)} %get-tuple-element.10), channel_id=1, source_target_pairs={{0,64},{32,96},{64,0},{96,32},{128,192},{160,224},{192,128},{224,1... | collective-permute-start | bytes 786440 | tf_op jit(solution)/shard_map/ppermute | solution.py:101
  58.9 20.4 %all-to-all-start.1 = ((f32[128,2,128]{2,1,0:T(2,128)}), f32[128,2,128]{2,1,0:T(2,128)S(1)}, u32[]{:S(2)}, u32[]{:S(2)}) async-start(f32[128,2,128]{2,1,0:T(2,128)} %get-tuple-element.5), calls=%async_computation.1 | async-start | bytes 262144 | tf_op jit(solution)/shard_map/all_to_all | solution.py:149
  69.3 14.6 %collective-permute-start.3 = (f32[2,8,8,256]{3,2,1,0:T(8,128)S(1)}, f32[2,8,8,256]{3,2,1,0:T(8,128)S(1)}, u32[]{:S(2)}, u32[]{:S(2)}) collective-permute-start(f32[2,8,8,256]{3,2,1,0:T(8,128)S(1)} %dynamic-slice_bitcast_fusion.3), channel_id=1, source_target_pairs={{0,256},{32,288},{64,320},{96,352},{128,384},{160,416},{192,448},{... | collective-permute-start | bytes 393224 | tf_op jit(solution)/shard_map/ppermute | solution.py:112
  83.9 7.1 %collective-permute-start.4 = (f32[1,8,8,256]{3,2,1,0:T(8,128)S(1)}, f32[1,8,8,256]{3,2,1,0:T(8,128)S(1)}, u32[]{:S(2)}, u32[]{:S(2)}) collective-permute-start(f32[1,8,8,256]{3,2,1,0:T(8,128)S(1)} %constant_dynamic-slice_fusion), channel_id=1, source_target_pairs={{0,128},{32,160},{64,192},{96,224},{128,0},{160,32},{192,64},{224,... | collective-permute-start | bytes 196616 | tf_op jit(solution)/shard_map/ppermute | solution.py:112

commit v13 on v12

--- a/solution.py
+++ b/solution.py
@@ -94,23 +94,20 @@
     size_hi = chunks // size_lo
     c = lax.axis_index("chan")
     hi, lo = c // size_lo, c % size_lo
-    parts = gradient.reshape((size_hi, size_lo) + gradient.shape[1:])
-    acc = lax.dynamic_index_in_dim(parts, lo, 1, keepdims=False)
-    for k in range(1, size_lo):
-        piece = lax.dynamic_index_in_dim(parts, (lo + k) % size_lo, 1, keepdims=False)
-        acc = acc + lax.ppermute(piece, "chan", _ring_pairs(size_hi, size_lo, k, True))
+    acc = gradient.reshape((2, size_hi // 2, size_lo) + gradient.shape[1:])
     for bit in (2, 1):
-        halves = acc.reshape((2, acc.shape[0] // 2) + acc.shape[1:]) if bit == 2 else acc.reshape(
-            (2, 1) + acc.shape[1:]
-        )
         mine = (hi // bit) % 2
-        keep = lax.dynamic_index_in_dim(halves, mine, 0, keepdims=False)
-        give = lax.dynamic_index_in_dim(halves, 1 - mine, 0, keepdims=False)
+        keep = lax.dynamic_index_in_dim(acc, mine, 0, keepdims=False)
+        give = lax.dynamic_index_in_dim(acc, 1 - mine, 0, keepdims=False)
         pairs = [
             (h * size_lo + l, (h ^ bit) * size_lo + l) for h in range(size_hi) for l in range(size_lo)
         ]
         acc = keep + lax.ppermute(give, "chan", pairs)
-    return acc[0]
+    out = lax.dynamic_index_in_dim(acc, lo, 0, keepdims=False)
+    for k in range(1, size_lo):
+        piece = lax.dynamic_index_in_dim(acc, (lo + k) % size_lo, 0, keepdims=False)
+        out = out + lax.ppermute(piece, "chan", _ring_pairs(size_hi, size_lo, k, True))
+    return out
 
 
 def shards(grid, tile_list, owner_map, offsets, positions, observed, weights):

time: 92.3 us -> 116 us (1.26)
  the two profiles are of different devices: /device:TPU:10 before, /device:TPU:1 now
where the time goes in v13:
time: 116 us; the launch traced here: 115 us
  starting transfers between devices  52 us (45%)
  waiting for transfers between devices  36.2 us (31%)
  Pallas kernels  13.8 us (12%)
  local copies, waits for them, and re-layouts  5.99 us (5%)
  other arithmetic  5.62 us (5%)
    ppermute x2, starting transfers between devices, _chan_reduce(): acc = keep + lax.ppermute(give, 'chan', pairs)  26.4 us
    ppermute x2, waiting for transfers between devices, _chan_reduce(): acc = keep + lax.ppermute(give, 'chan', pairs)  18.4 us
    all_to_all x1, waiting for transfers between devices, shards(): lax.all_to_all(outgoing, 'bl', split_axis=0, concat_axis=0, tiled=True)  15.5 us
    pallas_call x1, Pallas kernels, _grid_call(): pl.pallas_call(_grid_kernel, out_shape=(jax.ShapeDtypeStruct((slots, 2, v...  13.8 us
    all_to_all x1, starting transfers between devices, shards(): lax.all_to_all(outgoing, 'bl', split_axis=0, concat_axis=0, tiled=True)  10.6 us
    ppermute x3, starting transfers between devices, _chan_reduce(): lax.ppermute(piece, 'chan', _ring_pairs(size_hi, size_lo, k, True))  9.92 us
    all_to_all x1, starting transfers between devices, shards(): lax.all_to_all(residual_all, 'bl', split_axis=0, concat_axis=0, tiled=True)  5.13 us
    unnamed x19, local copies, waits for them, and re-layouts  2.34 us
  transfers between devices with their start and end apart: 7, of which 4 were waited for; matrix products, arithmetic and copies ran while one was open for 2% of the time, Pallas kernels for 0%

profile of v13, /device:TPU:1, one launch (start us, length us, event | category | flops | bytes accessed | tf_op | source)
XLA Modules:
  0.0 114.7 jit_solution(11272802868858198581)
XLA Ops:
  0.6 0.0 copy-start
  0.6 0.7 fusion.10
  1.3 0.0 copy-done
  1.3 0.0 copy-start.7
  1.3 0.8 gather_fusion
  2.1 0.0 copy-done.7
  2.1 0.1 fusion.5
  2.2 0.0 copy-start.5
  2.2 0.1 reduce_window_sum.11
  2.3 0.2 select_reduce_fusion.1
  2.5 0.1 select_reduce_fusion
  2.6 0.1 fusion.4
  2.7 0.0 copy-start.8
  2.8 0.7 copy-done.8
  3.4 0.1 copy.15
  3.5 0.0 copy-done.5
  3.5 0.0 copy-start.4
  3.5 0.1 bitcast_add_fusion.3
  3.7 0.0 copy-start.6
  3.7 0.1 broadcast_in_dim.66
  3.8 0.6 copy-done.4
  4.4 0.1 copy-done.6
  4.5 0.1 select_maximum_fusion
  4.6 0.8 gather_fusion.1
  5.3 0.0 copy-start.2
  5.4 1.0 broadcast_select_fusion
  6.4 10.6 %all-to-all-start = ((f32[128,6,128]{2,1,0:T(8,128)}), f32[128,6,128]{2,1,0:T(8,128)S(1)}, u32[]{:S(2)}, u32[]{:S(2)}) async-start(f32[128,6,128]{2,1,0:T(8,128)} %broadcast_select_fusion), calls=%async_computation | async-start | bytes 1048576 | tf_op jit(solution)/shard_map/all_to_all | solution.py:140
  17.0 0.0 copy-done.2
  17.0 1.0 copy.17
  18.0 15.5 %all-to-all-done.data_ref = f32[128,6,128]{2,1,0:T(8,128)S(1)} async-done(((f32[128,6,128]{2,1,0:T(8,128)}), f32[128,6,128]{2,1,0:T(8,128)S(1)}, u32[]{:S(2)}, u32[]{:S(2)}) %all-to-all-start) | async-done | bytes 393248 | tf_op jit(solution)/shard_map/all_to_all | solution.py:140
  33.5 0.0 copy-start.1
  33.5 1.0 slice_reduce_fusion
  34.5 0.5 convert_element_type.30.labels_ref
  35.0 0.0 copy-done.1
  35.0 13.8 %shard_map.86 = (f32[128,2,128]{2,1,0:T(2,128)}, f32[16,8,8,256]{3,2,1,0:T(8,128)}) custom-call(s32[128]{0:T(128)} %convert_element_type.30.labels_ref, f32[128,6,128]{2,1,0:T(8,128)} %copy-done.1, bf16[8,256,128]{2,1,0:T(8,128)(2,1)} %bitcast.73), custom_call_target="tpu_custom_call" | custom-call | tf_op jit(solution)/shard_map/pallas_call | solution.py:65
  48.8 0.0 copy-start.3
  48.8 1.2 %dynamic-slice_bitcast_fusion = f32[2,4,8,8,256]{4,3,2,1,0:T(8,128)S(1)} fusion(f32[2,2,4,8,8,256]{5,4,3,2,1,0:T(8,128)} %bitcast.74, s32[]{:T(128)S(6)} %select_n.238), kind=kLoop, calls=%fused_computation.4 | loop fusion | bytes 1048580 | tf_op jit(solution)/shard_map/jit(dynamic_index_in_dim)/squeeze | solution.py:101
  50.0 9.7 %collective-permute-start = (f32[2,4,8,8,256]{4,3,2,1,0:T(8,128)S(1)}, f32[2,4,8,8,256]{4,3,2,1,0:T(8,128)S(1)}, u32[]{:S(2)}, u32[]{:S(2)}) collective-permute-start(f32[2,4,8,8,256]{4,3,2,1,0:T(8,128)S(1)} %dynamic-slice_bitcast_fusion), channel_id=1, source_target_pairs={{0,256},{32,288},{64,320},{96,352},{128,384},{160,416},{192,448},{... | collective-permute-start | bytes 1572872 | tf_op jit(solution)/shard_map/ppermute | solution.py:105
  59.8 5.1 %all-to-all-start.1 = ((f32[128,2,128]{2,1,0:T(2,128)}), f32[128,2,128]{2,1,0:T(2,128)S(1)}, u32[]{:S(2)}, u32[]{:S(2)}) async-start(f32[128,2,128]{2,1,0:T(2,128)} %get-tuple-element.5), calls=%async_computation.1 | async-start | bytes 262144 | tf_op jit(solution)/shard_map/all_to_all | solution.py:146
  64.9 7.0 %collective-permute-done = f32[2,4,8,8,256]{4,3,2,1,0:T(8,128)S(1)} collective-permute-done((f32[2,4,8,8,256]{4,3,2,1,0:T(8,128)S(1)}, f32[2,4,8,8,256]{4,3,2,1,0:T(8,128)S(1)}, u32[]{:S(2)}, u32[]{:S(2)}) %collective-permute-start) | collective-permute-done | bytes 524320 | tf_op jit(solution)/shard_map/ppermute | solution.py:105
  71.9 0.0 copy-done.3
  71.9 0.1 bitcast_add_fusion
  72.0 16.7 %collective-permute-start.1 = (f32[4,8,8,256]{3,2,1,0:T(8,128)S(1)}, f32[4,8,8,256]{3,2,1,0:T(8,128)S(1)}, u32[]{:S(2)}, u32[]{:S(2)}) collective-permute-start(f32[4,8,8,256]{3,2,1,0:T(8,128)S(1)} %dynamic-slice_bitcast_fusion.1), channel_id=1, source_target_pairs={{0,128},{32,160},{64,192},{96,224},{128,0},{160,32},{192,64},{224,... | collective-permute-start | bytes 786440 | tf_op jit(solution)/shard_map/ppermute | solution.py:105
  88.8 0.0 all-to-all-done.1
  88.8 0.7 gather_fusion.2
  89.5 11.4 %collective-permute-done.1 = f32[4,8,8,256]{3,2,1,0:T(8,128)S(1)} collective-permute-done((f32[4,8,8,256]{3,2,1,0:T(8,128)S(1)}, f32[4,8,8,256]{3,2,1,0:T(8,128)S(1)}, u32[]{:S(2)}, u32[]{:S(2)}) %collective-permute-start.1) | collective-permute-done | bytes 262176 | tf_op jit(solution)/shard_map/ppermute | solution.py:105
  101.0 3.1 %collective-permute-start.2 = (f32[8,8,256]{2,1,0:T(8,128)S(1)}, f32[8,8,256]{2,1,0:T(8,128)S(1)}, u32[]{:S(2)}, u32[]{:S(2)}) collective-permute-start(f32[8,8,256]{2,1,0:T(8,128)S(1)} %get-tuple-element.8), channel_id=1, source_target_pairs={{0,32},{32,64},{64,96},{96,0},{128,160},{160,192},{192,224},{224,1... | collective-permute-start | bytes 196616 | tf_op jit(solution)/shard_map/ppermute | solution.py:109
  104.1 3.4 %collective-permute-start.4 = (f32[8,8,256]{2,1,0:T(8,128)S(1)}, f32[8,8,256]{2,1,0:T(8,128)S(1)}, u32[]{:S(2)}, u32[]{:S(2)}) collective-permute-start(f32[8,8,256]{2,1,0:T(8,128)S(1)} %get-tuple-element.9), channel_id=1, source_target_pairs={{0,96},{32,0},{64,32},{96,64},{128,224},{160,128},{192,160},{224,1... | collective-permute-start | bytes 196616 | tf_op jit(solution)/shard_map/ppermute | solution.py:109
  107.5 3.4 %collective-permute-start.3 = (f32[8,8,256]{2,1,0:T(8,128)S(1)}, f32[8,8,256]{2,1,0:T(8,128)S(1)}, u32[]{:S(2)}, u32[]{:S(2)}) collective-permute-start(f32[8,8,256]{2,1,0:T(8,128)S(1)} %get-tuple-element.10), channel_id=1, source_target_pairs={{0,64},{32,96},{64,0},{96,32},{128,192},{160,224},{192,128},{224,1... | collective-permute-start | bytes 196616 | tf_op jit(solution)/shard_map/ppermute | solution.py:109
  111.0 0.8 bitcast_select_fusion
  111.7 0.0 collective-permute-done.2
  111.7 0.0 collective-permute-done.4
  111.7 2.3 %collective-permute-done.3 = f32[8,8,256]{2,1,0:T(8,128)S(1)} collective-permute-done((f32[8,8,256]{2,1,0:T(8,128)S(1)}, f32[8,8,256]{2,1,0:T(8,128)S(1)}, u32[]{:S(2)}, u32[]{:S(2)}) %collective-permute-start.3) | collective-permute-done | bytes 65568 | tf_op jit(solution)/shard_map/ppermute | solution.py:109
  114.0 0.7 fusion.3
  (14 shorter events, 0.2 us)
Async XLA Ops:
  0.6 0.7 copy-start
  1.3 0.8 copy-start.7
  2.2 1.3 %copy-start.5 = (f32[1,64,2,128]{3,2,1,0:T(2,128)S(1)}, f32[1,64,2,128]{3,2,1,0:T(2,128)}, u32[]{:S(2)}) copy-start(f32[1,64,2,128]{3,2,1,0:T(2,128)} %param.11) | copy-start | bytes 196612
  2.7 0.7 copy-start.8
  3.5 0.8 copy-start.4
  3.7 0.8 copy-start.6
  5.3 11.6 %copy-start.2 = (f32[8,128,256]{2,1,0:T(8,128)S(1)}, f32[8,128,256]{2,1,0:T(8,128)}, u32[]{:S(2)}) copy-start(f32[8,128,256]{2,1,0:T(8,128)} %param.7) | copy-start | bytes 3145732
  6.4 27.1 %all-to-all-start = ((f32[128,6,128]{2,1,0:T(8,128)}), f32[128,6,128]{2,1,0:T(8,128)S(1)}, u32[]{:S(2)}, u32[]{:S(2)}) async-start(f32[128,6,128]{2,1,0:T(8,128)} %broadcast_select_fusion), calls=%async_computation | async-start | bytes 1048576 | tf_op jit(solution)/shard_map/all_to_all | solution.py:140
  33.5 1.6 %copy-start.1 = (f32[128,6,128]{2,1,0:T(8,128)}, f32[128,6,128]{2,1,0:T(8,128)S(1)}, u32[]{:S(2)}) copy-start(f32[128,6,128]{2,1,0:T(8,128)S(1)} %all-to-all-done.data_ref) | copy-start | bytes 1179652
  48.8 23.1 %copy-start.3 = (f32[16,8,8,256]{3,2,1,0:T(8,128)S(1)}, f32[16,8,8,256]{3,2,1,0:T(8,128)}, u32[]{:S(2)}) copy-start(f32[16,8,8,256]{3,2,1,0:T(8,128)} %get-tuple-element.4) | copy-start | bytes 3145732
  50.0 21.9 %collective-permute-start = (f32[2,4,8,8,256]{4,3,2,1,0:T(8,128)S(1)}, f32[2,4,8,8,256]{4,3,2,1,0:T(8,128)S(1)}, u32[]{:S(2)}, u32[]{:S(2)}) collective-permute-start(f32[2,4,8,8,256]{4,3,2,1,0:T(8,128)S(1)} %dynamic-slice_bitcast_fusion), channel_id=1, source_target_pairs={{0,256},{32,288},{64,320},{96,352},{128,384},{160,416},{192,448},{... | collective-permute-start | bytes 1572872 | tf_op jit(solution)/shard_map/ppermute | solution.py:105
  59.8 29.0 %all-to-all-start.1 = ((f32[128,2,128]{2,1,0:T(2,128)}), f32[128,2,128]{2,1,0:T(2,128)S(1)}, u32[]{:S(2)}, u32[]{:S(2)}) async-start(f32[128,2,128]{2,1,0:T(2,128)} %get-tuple-element.5), calls=%async_computation.1 | async-start | bytes 262144 | tf_op jit(solution)/shard_map/all_to_all | solution.py:146
  72.0 28.9 %collective-permute-start.1 = (f32[4,8,8,256]{3,2,1,0:T(8,128)S(1)}, f32[4,8,8,256]{3,2,1,0:T(8,128)S(1)}, u32[]{:S(2)}, u32[]{:S(2)}) collective-permute-start(f32[4,8,8,256]{3,2,1,0:T(8,128)S(1)} %dynamic-slice_bitcast_fusion.1), channel_id=1, source_target_pairs={{0,128},{32,160},{64,192},{96,224},{128,0},{160,32},{192,64},{224,... | collective-permute-start | bytes 786440 | tf_op jit(solution)/shard_map/ppermute | solution.py:105
  101.0 10.7 %collective-permute-start.2 = (f32[8,8,256]{2,1,0:T(8,128)S(1)}, f32[8,8,256]{2,1,0:T(8,128)S(1)}, u32[]{:S(2)}, u32[]{:S(2)}) collective-permute-start(f32[8,8,256]{2,1,0:T(8,128)S(1)} %get-tuple-element.8), channel_id=1, source_target_pairs={{0,32},{32,64},{64,96},{96,0},{128,160},{160,192},{192,224},{224,1... | collective-permute-start | bytes 196616 | tf_op jit(solution)/shard_map/ppermute | solution.py:109
  104.1 7.6 %collective-permute-start.4 = (f32[8,8,256]{2,1,0:T(8,128)S(1)}, f32[8,8,256]{2,1,0:T(8,128)S(1)}, u32[]{:S(2)}, u32[]{:S(2)}) collective-permute-start(f32[8,8,256]{2,1,0:T(8,128)S(1)} %get-tuple-element.9), channel_id=1, source_target_pairs={{0,96},{32,0},{64,32},{96,64},{128,224},{160,128},{192,160},{224,1... | collective-permute-start | bytes 196616 | tf_op jit(solution)/shard_map/ppermute | solution.py:109
  107.5 6.5 %collective-permute-start.3 = (f32[8,8,256]{2,1,0:T(8,128)S(1)}, f32[8,8,256]{2,1,0:T(8,128)S(1)}, u32[]{:S(2)}, u32[]{:S(2)}) collective-permute-start(f32[8,8,256]{2,1,0:T(8,128)S(1)} %get-tuple-element.10), channel_id=1, source_target_pairs={{0,64},{32,96},{64,0},{96,32},{128,192},{160,224},{192,128},{224,1... | collective-permute-start | bytes 196616 | tf_op jit(solution)/shard_map/ppermute | solution.py:109

commit v14 on v12

--- a/solution.py
+++ b/solution.py
@@ -113,6 +113,62 @@
     return acc[0]
 
 
+def _dispatch_kernel(tile_ref, owner_ref, off_ref, pos_ref, obs_ref, w_ref, out_ref, slot_ref, count_ref):
+    blocks, _, vis = pos_ref.shape
+    owners = count_ref.shape[0]
+    capacity = out_ref.shape[0] // owners
+    tile_dev = owner_ref.shape[0] // owners
+    out_ref[...] = jnp.zeros(out_ref.shape, out_ref.dtype)
+
+    def clear(o, carry):
+        count_ref[o] = 0
+        return carry
+
+    lax.fori_loop(0, owners, clear, 0)
+
+    def body(b, carry):
+        slot = owner_ref[tile_ref[b]]
+        owner = slot // tile_dev
+        local = slot % tile_dev
+        rank = jnp.minimum(count_ref[owner], capacity - 1)
+        count_ref[owner] = rank + 1
+        dest = owner * capacity + rank
+        slot_ref[b] = dest
+        pos = pos_ref[b]
+        coord_u = off_ref[2 * b].astype(jnp.float32) + pos[0:1]
+        coord_v = off_ref[2 * b + 1].astype(jnp.float32) + pos[1:2]
+        label = jnp.full((1, vis), local.astype(jnp.float32), jnp.float32)
+        out_ref[dest] = jnp.concatenate(
+            [obs_ref[b], w_ref[pl.ds(b, 1), :], coord_u, coord_v, label], axis=0
+        )
+        return carry
+
+    lax.fori_loop(0, blocks, body, 0)
+
+
+def _dispatch_call(tile_ids, owner_map, offsets, positions, observed, weights, owners, capacity):
+    blocks, _, vis = positions.shape
+    smem = pltpu.MemorySpace.SMEM
+    vmem = pltpu.MemorySpace.VMEM
+    return pl.pallas_call(
+        _dispatch_kernel,
+        out_shape=(
+            jax.ShapeDtypeStruct((owners * capacity, 6, vis), jnp.float32),
+            jax.ShapeDtypeStruct((blocks,), jnp.int32),
+        ),
+        in_specs=[
+            pl.BlockSpec(memory_space=smem),
+            pl.BlockSpec(memory_space=smem),
+            pl.BlockSpec(memory_space=smem),
+            pl.BlockSpec(memory_space=vmem),
+            pl.BlockSpec(memory_space=vmem),
+            pl.BlockSpec(memory_space=vmem),
+        ],
+        out_specs=(pl.BlockSpec(memory_space=vmem), pl.BlockSpec(memory_space=smem)),
+        scratch_shapes=[pltpu.SMEM((owners,), jnp.int32)],
+    )(tile_ids, owner_map, offsets.reshape(-1), positions, observed, weights)
+
+
 def shards(grid, tile_list, owner_map, offsets, positions, observed, weights):
     owners = lax.axis_size("bl")
     chan = lax.axis_size("chan")
@@ -122,24 +178,9 @@
     capacity = 2 * block_count // owners
     slots_all = owners * capacity
     tile_ids = tile_list[0]
-    slot_index = jnp.take(owner_map, tile_ids, axis=0)
-    owner_index = slot_index // tile_dev
-    local_slot = slot_index % tile_dev
-    owner_onehot = (owner_index[:, None] == jnp.arange(owners, dtype=jnp.int32)[None, :]).astype(
-        jnp.int32
+    outgoing, send_slot = _dispatch_call(
+        tile_ids, owner_map, offsets[0], positions[0], observed[0], weights[0], owners, capacity
     )
-    earlier_count = jnp.cumsum(owner_onehot, axis=0) - owner_onehot
-    place_rank = jnp.sum(owner_onehot * earlier_count, axis=1)
-    send_slot = owner_index * capacity + place_rank
-    coords = offsets[0].astype(jnp.float32)[..., None] + positions[0]
-    vis = coords.shape[-1]
-    label_row = jnp.broadcast_to(local_slot.astype(jnp.float32)[:, None, None], (block_count, 1, vis))
-    payload = jnp.concatenate([observed[0], weights[0][:, None, :], coords, label_row], axis=1)
-    match = send_slot[None, :] == jnp.arange(slots_all, dtype=jnp.int32)[:, None]
-    source = jnp.sum(jnp.where(match, jnp.arange(block_count, dtype=jnp.int32)[None, :], 0), axis=1)
-    source = jnp.where(jnp.any(match, axis=1), source, block_count)
-    padded = jnp.concatenate([payload, jnp.zeros((1,) + payload.shape[1:], payload.dtype)], axis=0)
-    outgoing = jnp.take(padded, source, axis=0)
     incoming = lax.all_to_all(outgoing, "bl", split_axis=0, concat_axis=0, tiled=True)
     labels = jnp.max(incoming[:, 5, :], axis=1).astype(jnp.int32)
     tiles_t = jnp.swapaxes(grid.astype(jnp.bfloat16), 1, 2)

time: 92.3 us -> 91.4 us (level)
  the two profiles are of different devices: /device:TPU:10 before, /device:TPU:1 now
where the time goes in v14:
time: 91.4 us; the launch traced here: 89.7 us
  starting transfers between devices  44.3 us (48%)
  waiting for transfers between devices  18.6 us (20%)
  Pallas kernels  16.7 us (18%)
  local copies, waits for them, and re-layouts  5.06 us (6%)
  other arithmetic  4.02 us (4%)
  between operations  0.96 us (1%)
    ppermute x2, starting transfers between devices, _chan_reduce(): acc = keep + lax.ppermute(give, 'chan', pairs)  18.1 us
    all_to_all x1, waiting for transfers between devices, shards(): lax.all_to_all(outgoing, 'bl', split_axis=0, concat_axis=0, tiled=True)  15.5 us
    pallas_call x1, Pallas kernels, _grid_call(): pl.pallas_call(_grid_kernel, out_shape=(jax.ShapeDtypeStruct((slots, 2, v...  13.5 us
    all_to_all x1, starting transfers between devices, shards(): lax.all_to_all(outgoing, 'bl', split_axis=0, concat_axis=0, tiled=True)  10.6 us
    ppermute x3, starting transfers between devices, _chan_reduce(): lax.ppermute(piece, 'chan', _ring_pairs(size_hi, size_lo, k, True))  9.95 us
    all_to_all x1, starting transfers between devices, shards(): lax.all_to_all(residual_all, 'bl', split_axis=0, concat_axis=0, tiled=True)  5.66 us
    pallas_call x1, Pallas kernels, _dispatch_call(): pl.pallas_call(_dispatch_kernel, out_shape=(jax.ShapeDtypeStruct((owners...  3.21 us
    ppermute x2, waiting for transfers between devices, _chan_reduce(): acc = keep + lax.ppermute(give, 'chan', pairs)  3.16 us
  transfers between devices with their start and end apart: 7, of which 3 were waited for; matrix products, arithmetic and copies ran while one was open for 4% of the time, Pallas kernels for 0%

profile of v14, /device:TPU:1, one launch (start us, length us, event | category | flops | bytes accessed | tf_op | source)
XLA Modules:
  0.0 89.7 jit_solution(9887805216853060939)
XLA Ops:
  0.6 0.0 copy-start.1
  0.6 0.9 copy.11
  1.5 0.7 reshape_squeeze.3.off_ref
  2.1 3.2 %shard_map.86 = (f32[128,6,128]{2,1,0:T(8,128)}, s32[64]{0:T(128)}) custom-call(s32[64]{0:T(128)} %bitcast.39, s32[256]{0:T(256)} %owner_ref.1, s32[128]{0:T(128)} %reshape_squeeze.3.off_ref, f32[64,2,128]{2,1,0:T(2,128)} %bitcast.36, f32[64,2,128]{2,1,0:T(2,128)} %bitcast.37, f32[64,128]{1,0:T(8,128)} %bitcast.38), custom_call_target="tpu_custom_call" | custom-call | tf_op jit(solution)/shard_map/pallas_call | solution.py:153
  5.4 10.6 %all-to-all-start = ((f32[128,6,128]{2,1,0:T(8,128)}), f32[128,6,128]{2,1,0:T(8,128)S(1)}, u32[]{:S(2)}, u32[]{:S(2)}) async-start(f32[128,6,128]{2,1,0:T(8,128)} %get-tuple-element.6), calls=%async_computation | async-start | bytes 1048576 | tf_op jit(solution)/shard_map/all_to_all | solution.py:184
  16.0 0.0 copy-done.1
  16.0 1.0 %copy.12 = bf16[8,128,256]{1,2,0:T(8,128)(2,1)} copy(f32[8,128,256]{2,1,0:T(8,128)S(1)} %copy-done.1) | data formatting | bytes 1572864 | tf_op args[0]
  17.0 15.5 %all-to-all-done.data_ref = f32[128,6,128]{2,1,0:T(8,128)S(1)} async-done(((f32[128,6,128]{2,1,0:T(8,128)}), f32[128,6,128]{2,1,0:T(8,128)S(1)}, u32[]{:S(2)}, u32[]{:S(2)}) %all-to-all-start) | async-done | bytes 393248 | tf_op jit(solution)/shard_map/all_to_all | solution.py:184
  32.5 0.0 copy-start
  32.5 1.0 %slice_reduce_fusion = f32[128]{0:T(128)S(1)} fusion(f32[128,6,128]{2,1,0:T(8,128)S(1)} %all-to-all-done.data_ref), kind=kLoop, calls=%fused_computation.10 | loop fusion | flops 16256 | bytes 66048 | tf_op jit(solution)/shard_map/reduce_max | solution.py:185
  33.5 0.5 convert_element_type.6.labels_ref
  34.0 0.0 copy-done
  34.0 13.5 %shard_map.87 = (f32[128,2,128]{2,1,0:T(2,128)}, f32[16,8,8,256]{3,2,1,0:T(8,128)}) custom-call(s32[128]{0:T(128)} %convert_element_type.6.labels_ref, f32[128,6,128]{2,1,0:T(8,128)} %copy-done, bf16[8,256,128]{2,1,0:T(8,128)(2,1)} %bitcast.31), custom_call_target="tpu_custom_call" | custom-call | tf_op jit(solution)/shard_map/pallas_call | solution.py:65
  47.6 1.2 %dynamic-slice_bitcast_fusion.2 = (f32[4,8,8,256]{3,2,1,0:T(8,128)S(1)}, f32[4,8,8,256]{3,2,1,0:T(8,128)S(1)}, f32[4,8,8,256]{3,2,1,0:T(8,128)S(1)}) fusion(f32[4,4,8,8,256]{4,3,2,1,0:T(8,128)} %bitcast.32, s32[]{:T(128)S(6)} %select_n.85, s32[]{:T(128)S(6)} %select_n.89, s32[]{:T(128)S(6)} %select_n.87), kind=kLoop, calls=%fused_computation.7 | loop fusion | bytes 1572876 | tf_op jit(solution)/shard_map/jit(dynamic_index_in_dim)/squeeze | solution.py:100
  48.7 3.1 %collective-permute-start = (f32[4,8,8,256]{3,2,1,0:T(8,128)S(1)}, f32[4,8,8,256]{3,2,1,0:T(8,128)S(1)}, u32[]{:S(2)}, u32[]{:S(2)}) collective-permute-start(f32[4,8,8,256]{3,2,1,0:T(8,128)S(1)} %get-tuple-element.10), channel_id=1, source_target_pairs={{0,32},{32,64},{64,96},{96,0},{128,160},{160,192},{192,224},{224,1... | collective-permute-start | bytes 786440 | tf_op jit(solution)/shard_map/ppermute | solution.py:101
  51.9 3.4 %collective-permute-start.2 = (f32[4,8,8,256]{3,2,1,0:T(8,128)S(1)}, f32[4,8,8,256]{3,2,1,0:T(8,128)S(1)}, u32[]{:S(2)}, u32[]{:S(2)}) collective-permute-start(f32[4,8,8,256]{3,2,1,0:T(8,128)S(1)} %get-tuple-element.11), channel_id=1, source_target_pairs={{0,96},{32,0},{64,32},{96,64},{128,224},{160,128},{192,160},{224,1... | collective-permute-start | bytes 786440 | tf_op jit(solution)/shard_map/ppermute | solution.py:101
  55.3 3.5 %collective-permute-start.1 = (f32[4,8,8,256]{3,2,1,0:T(8,128)S(1)}, f32[4,8,8,256]{3,2,1,0:T(8,128)S(1)}, u32[]{:S(2)}, u32[]{:S(2)}) collective-permute-start(f32[4,8,8,256]{3,2,1,0:T(8,128)S(1)} %get-tuple-element.12), channel_id=1, source_target_pairs={{0,64},{32,96},{64,0},{96,32},{128,192},{160,224},{192,128},{224,1... | collective-permute-start | bytes 786440 | tf_op jit(solution)/shard_map/ppermute | solution.py:101
  58.8 0.0 copy-start.2
  58.8 0.6 copy-done.2
  59.5 5.7 %all-to-all-start.1 = ((f32[128,2,128]{2,1,0:T(2,128)}), f32[128,2,128]{2,1,0:T(2,128)S(1)}, u32[]{:S(2)}, u32[]{:S(2)}) async-start(f32[128,2,128]{2,1,0:T(2,128)} %get-tuple-element.9), calls=%async_computation.1 | async-start | bytes 262144 | tf_op jit(solution)/shard_map/all_to_all | solution.py:190
  65.1 0.0 collective-permute-done
  65.1 0.0 collective-permute-done.2
  65.1 0.0 collective-permute-done.1
  65.2 1.0 %fusion.1 = f32[4,8,8,256]{3,2,1,0:T(8,128)S(1)} fusion(f32[4,8,8,256]{3,2,1,0:T(8,128)S(1)} %collective-permute-done.2, f32[4,8,8,256]{3,2,1,0:T(8,128)S(1)} %collective-permute-done.1, f32[4,8,8,256]{3,2,1,0:T(8,128)S(1)} %collective-permute-done, f32[4,4,8,8,256]{4,3,2,1,0:T(8,128)} %bitcast.33, s32[]{:T(128)S(6)} %select_n.83), kind=kLoop, calls=%fused_computation.4 | loop fusion | flops 196608 | bytes 1310724 | tf_op jit(solution)/shard_map/add | solution.py:101
  66.2 9.7 %collective-permute-start.3 = (f32[2,8,8,256]{3,2,1,0:T(8,128)S(1)}, f32[2,8,8,256]{3,2,1,0:T(8,128)S(1)}, u32[]{:S(2)}, u32[]{:S(2)}) collective-permute-start(f32[2,8,8,256]{3,2,1,0:T(8,128)S(1)} %dynamic-slice_bitcast_fusion.3), channel_id=1, source_target_pairs={{0,256},{32,288},{64,320},{96,352},{128,384},{160,416},{192,448},{... | collective-permute-start | bytes 393224 | tf_op jit(solution)/shard_map/ppermute | solution.py:112
  76.0 0.0 all-to-all-done.1
  76.0 0.7 gather_fusion
  76.7 2.3 %collective-permute-done.3 = f32[2,8,8,256]{3,2,1,0:T(8,128)S(1)} collective-permute-done((f32[2,8,8,256]{3,2,1,0:T(8,128)S(1)}, f32[2,8,8,256]{3,2,1,0:T(8,128)S(1)}, u32[]{:S(2)}, u32[]{:S(2)}) %collective-permute-start.3) | collective-permute-done | bytes 131104 | tf_op jit(solution)/shard_map/ppermute | solution.py:112
  79.0 8.4 %collective-permute-start.4 = (f32[1,8,8,256]{3,2,1,0:T(8,128)S(1)}, f32[1,8,8,256]{3,2,1,0:T(8,128)S(1)}, u32[]{:S(2)}, u32[]{:S(2)}) collective-permute-start(f32[1,8,8,256]{3,2,1,0:T(8,128)S(1)} %constant_dynamic-slice_fusion), channel_id=1, source_target_pairs={{0,128},{32,160},{64,192},{96,224},{128,0},{160,32},{192,64},{224,... | collective-permute-start | bytes 196616 | tf_op jit(solution)/shard_map/ppermute | solution.py:112
  87.4 0.8 bitcast_select_fusion
  88.2 0.9 collective-permute-done.4
  89.1 0.6 fusion.2
  (6 shorter events, 0.1 us)
Async XLA Ops:
  0.6 15.4 %copy-start.1 = (f32[8,128,256]{2,1,0:T(8,128)S(1)}, f32[8,128,256]{2,1,0:T(8,128)}, u32[]{:S(2)}) copy-start(f32[8,128,256]{2,1,0:T(8,128)} %param.7) | copy-start | bytes 3145732
  5.4 27.1 %all-to-all-start = ((f32[128,6,128]{2,1,0:T(8,128)}), f32[128,6,128]{2,1,0:T(8,128)S(1)}, u32[]{:S(2)}, u32[]{:S(2)}) async-start(f32[128,6,128]{2,1,0:T(8,128)} %get-tuple-element.6), calls=%async_computation | async-start | bytes 1048576 | tf_op jit(solution)/shard_map/all_to_all | solution.py:184
  32.5 1.6 %copy-start = (f32[128,6,128]{2,1,0:T(8,128)}, f32[128,6,128]{2,1,0:T(8,128)S(1)}, u32[]{:S(2)}) copy-start(f32[128,6,128]{2,1,0:T(8,128)S(1)} %all-to-all-done.data_ref) | copy-start | bytes 1179652
  48.7 16.4 %collective-permute-start = (f32[4,8,8,256]{3,2,1,0:T(8,128)S(1)}, f32[4,8,8,256]{3,2,1,0:T(8,128)S(1)}, u32[]{:S(2)}, u32[]{:S(2)}) collective-permute-start(f32[4,8,8,256]{3,2,1,0:T(8,128)S(1)} %get-tuple-element.10), channel_id=1, source_target_pairs={{0,32},{32,64},{64,96},{96,0},{128,160},{160,192},{192,224},{224,1... | collective-permute-start | bytes 786440 | tf_op jit(solution)/shard_map/ppermute | solution.py:101
  51.9 13.3 %collective-permute-start.2 = (f32[4,8,8,256]{3,2,1,0:T(8,128)S(1)}, f32[4,8,8,256]{3,2,1,0:T(8,128)S(1)}, u32[]{:S(2)}, u32[]{:S(2)}) collective-permute-start(f32[4,8,8,256]{3,2,1,0:T(8,128)S(1)} %get-tuple-element.11), channel_id=1, source_target_pairs={{0,96},{32,0},{64,32},{96,64},{128,224},{160,128},{192,160},{224,1... | collective-permute-start | bytes 786440 | tf_op jit(solution)/shard_map/ppermute | solution.py:101
  55.3 9.9 %collective-permute-start.1 = (f32[4,8,8,256]{3,2,1,0:T(8,128)S(1)}, f32[4,8,8,256]{3,2,1,0:T(8,128)S(1)}, u32[]{:S(2)}, u32[]{:S(2)}) collective-permute-start(f32[4,8,8,256]{3,2,1,0:T(8,128)S(1)} %get-tuple-element.12), channel_id=1, source_target_pairs={{0,64},{32,96},{64,0},{96,32},{128,192},{160,224},{192,128},{224,1... | collective-permute-start | bytes 786440 | tf_op jit(solution)/shard_map/ppermute | solution.py:101
  58.8 0.7 copy-start.2
  59.5 16.6 %all-to-all-start.1 = ((f32[128,2,128]{2,1,0:T(2,128)}), f32[128,2,128]{2,1,0:T(2,128)S(1)}, u32[]{:S(2)}, u32[]{:S(2)}) async-start(f32[128,2,128]{2,1,0:T(2,128)} %get-tuple-element.9), calls=%async_computation.1 | async-start | bytes 262144 | tf_op jit(solution)/shard_map/all_to_all | solution.py:190
  66.2 12.8 %collective-permute-start.3 = (f32[2,8,8,256]{3,2,1,0:T(8,128)S(1)}, f32[2,8,8,256]{3,2,1,0:T(8,128)S(1)}, u32[]{:S(2)}, u32[]{:S(2)}) collective-permute-start(f32[2,8,8,256]{3,2,1,0:T(8,128)S(1)} %dynamic-slice_bitcast_fusion.3), channel_id=1, source_target_pairs={{0,256},{32,288},{64,320},{96,352},{128,384},{160,416},{192,448},{... | collective-permute-start | bytes 393224 | tf_op jit(solution)/shard_map/ppermute | solution.py:112
  79.0 10.0 %collective-permute-start.4 = (f32[1,8,8,256]{3,2,1,0:T(8,128)S(1)}, f32[1,8,8,256]{3,2,1,0:T(8,128)S(1)}, u32[]{:S(2)}, u32[]{:S(2)}) collective-permute-start(f32[1,8,8,256]{3,2,1,0:T(8,128)S(1)} %constant_dynamic-slice_fusion), channel_id=1, source_target_pairs={{0,128},{32,160},{64,192},{96,224},{128,0},{160,32},{192,64},{224,... | collective-permute-start | bytes 196616 | tf_op jit(solution)/shard_map/ppermute | solution.py:112

commit v15 on v14

--- a/solution.py
+++ b/solution.py
@@ -135,15 +135,15 @@
         dest = owner * capacity + rank
         slot_ref[b] = dest
         pos = pos_ref[b]
-        coord_u = off_ref[2 * b].astype(jnp.float32) + pos[0:1]
-        coord_v = off_ref[2 * b + 1].astype(jnp.float32) + pos[1:2]
+        coord_u = off_ref[b, 0].astype(jnp.float32) + pos[0:1]
+        coord_v = off_ref[b, 1].astype(jnp.float32) + pos[1:2]
         label = jnp.full((1, vis), local.astype(jnp.float32), jnp.float32)
         out_ref[dest] = jnp.concatenate(
             [obs_ref[b], w_ref[pl.ds(b, 1), :], coord_u, coord_v, label], axis=0
         )
         return carry
 
-    lax.fori_loop(0, blocks, body, 0)
+    lax.fori_loop(0, blocks, body, 0, unroll=8)
 
 
 def _dispatch_call(tile_ids, owner_map, offsets, positions, observed, weights, owners, capacity):
@@ -166,7 +166,7 @@
         ],
         out_specs=(pl.BlockSpec(memory_space=vmem), pl.BlockSpec(memory_space=smem)),
         scratch_shapes=[pltpu.SMEM((owners,), jnp.int32)],
-    )(tile_ids, owner_map, offsets.reshape(-1), positions, observed, weights)
+    )(tile_ids, owner_map, offsets, positions, observed, weights)
 
 
 def shards(grid, tile_list, owner_map, offsets, positions, observed, weights):

time: 91.4 us -> 91.2 us (level)
    unnamed x8 -> x9, local copies, waits for them, and re-layouts: 2.53 us -> 2.36 us
where the time goes in v15:
time: 91.2 us; the launch traced here: 89.5 us
  starting transfers between devices  44.3 us (49%)
  waiting for transfers between devices  18.6 us (20%)
  Pallas kernels  16.7 us (18%)
  local copies, waits for them, and re-layouts  4.93 us (5%)
  other arithmetic  4.02 us (4%)
  between operations  0.97 us (1%)
    ppermute x2, starting transfers between devices, _chan_reduce(): acc = keep + lax.ppermute(give, 'chan', pairs)  18.1 us
    all_to_all x1, waiting for transfers between devices, shards(): lax.all_to_all(outgoing, 'bl', split_axis=0, concat_axis=0, tiled=True)  15.4 us
    pallas_call x1, Pallas kernels, _grid_call(): pl.pallas_call(_grid_kernel, out_shape=(jax.ShapeDtypeStruct((slots, 2, v...  13.5 us
    all_to_all x1, starting transfers between devices, shards(): lax.all_to_all(outgoing, 'bl', split_axis=0, concat_axis=0, tiled=True)  10.6 us
    ppermute x3, starting transfers between devices, _chan_reduce(): lax.ppermute(piece, 'chan', _ring_pairs(size_hi, size_lo, k, True))  9.92 us
    all_to_all x1, starting transfers between devices, shards(): lax.all_to_all(residual_all, 'bl', split_axis=0, concat_axis=0, tiled=True)  5.67 us
    ppermute x2, waiting for transfers between devices, _chan_reduce(): acc = keep + lax.ppermute(give, 'chan', pairs)  3.17 us
    pallas_call x1, Pallas kernels, _dispatch_call(): pl.pallas_call(_dispatch_kernel, out_shape=(jax.ShapeDtypeStruct((owners...  3.14 us
  transfers between devices with their start and end apart: 7, of which 3 were waited for; matrix products, arithmetic and copies ran while one was open for 4% of the time, Pallas kernels for 0%

profile of v15, /device:TPU:1, one launch (start us, length us, event | category | flops | bytes accessed | tf_op | source)
XLA Modules:
  0.0 89.5 jit_solution(6431333060317587176)
XLA Ops:
  0.6 0.0 copy-start.2
  0.6 0.0 copy-start.1
  0.6 0.7 copy-done.2
  1.3 0.7 copy.9.off_ref
  2.0 3.1 %shard_map.86 = (f32[128,6,128]{2,1,0:T(8,128)}, s32[64]{0:T(128)}) custom-call(s32[64]{0:T(128)} %bitcast.41, s32[256]{0:T(256)} %owner_ref.1, s32[64,2]{1,0:T(8,128)} %copy.9.off_ref, f32[64,2,128]{2,1,0:T(2,128)} %bitcast.37, f32[64,2,128]{2,1,0:T(2,128)} %bitcast.38, f32[64,128]{1,0:T(8,128)} %bitcast.39), custom_call_target="tpu_custom_call" | custom-call | tf_op jit(solution)/shard_map/pallas_call | solution.py:153
  5.2 10.6 %all-to-all-start = ((f32[128,6,128]{2,1,0:T(8,128)}), f32[128,6,128]{2,1,0:T(8,128)S(1)}, u32[]{:S(2)}, u32[]{:S(2)}) async-start(f32[128,6,128]{2,1,0:T(8,128)} %get-tuple-element.6), calls=%async_computation | async-start | bytes 1048576 | tf_op jit(solution)/shard_map/all_to_all | solution.py:184
  15.8 0.0 copy-done.1
  15.8 1.0 %copy.10 = bf16[8,128,256]{1,2,0:T(8,128)(2,1)} copy(f32[8,128,256]{2,1,0:T(8,128)S(1)} %copy-done.1) | data formatting | bytes 1572864 | tf_op args[0]
  16.9 15.4 %all-to-all-done.data_ref = f32[128,6,128]{2,1,0:T(8,128)S(1)} async-done(((f32[128,6,128]{2,1,0:T(8,128)}), f32[128,6,128]{2,1,0:T(8,128)S(1)}, u32[]{:S(2)}, u32[]{:S(2)}) %all-to-all-start) | async-done | bytes 393248 | tf_op jit(solution)/shard_map/all_to_all | solution.py:184
  32.3 0.0 copy-start
  32.3 1.0 %slice_reduce_fusion = f32[128]{0:T(128)S(1)} fusion(f32[128,6,128]{2,1,0:T(8,128)S(1)} %all-to-all-done.data_ref), kind=kLoop, calls=%fused_computation.10 | loop fusion | flops 16256 | bytes 66048 | tf_op jit(solution)/shard_map/reduce_max | solution.py:185
  33.3 0.5 convert_element_type.6.labels_ref
  33.8 0.0 copy-done
  33.9 13.5 %shard_map.87 = (f32[128,2,128]{2,1,0:T(2,128)}, f32[16,8,8,256]{3,2,1,0:T(8,128)}) custom-call(s32[128]{0:T(128)} %convert_element_type.6.labels_ref, f32[128,6,128]{2,1,0:T(8,128)} %copy-done, bf16[8,256,128]{2,1,0:T(8,128)(2,1)} %bitcast.32), custom_call_target="tpu_custom_call" | custom-call | tf_op jit(solution)/shard_map/pallas_call | solution.py:65
  47.4 1.2 %dynamic-slice_bitcast_fusion.2 = (f32[4,8,8,256]{3,2,1,0:T(8,128)S(1)}, f32[4,8,8,256]{3,2,1,0:T(8,128)S(1)}, f32[4,8,8,256]{3,2,1,0:T(8,128)S(1)}) fusion(f32[4,4,8,8,256]{4,3,2,1,0:T(8,128)} %bitcast.33, s32[]{:T(128)S(6)} %select_n.85, s32[]{:T(128)S(6)} %select_n.89, s32[]{:T(128)S(6)} %select_n.87), kind=kLoop, calls=%fused_computation.7 | loop fusion | bytes 1572876 | tf_op jit(solution)/shard_map/jit(dynamic_index_in_dim)/squeeze | solution.py:100
  48.6 3.1 %collective-permute-start = (f32[4,8,8,256]{3,2,1,0:T(8,128)S(1)}, f32[4,8,8,256]{3,2,1,0:T(8,128)S(1)}, u32[]{:S(2)}, u32[]{:S(2)}) collective-permute-start(f32[4,8,8,256]{3,2,1,0:T(8,128)S(1)} %get-tuple-element.10), channel_id=1, source_target_pairs={{0,32},{32,64},{64,96},{96,0},{128,160},{160,192},{192,224},{224,1... | collective-permute-start | bytes 786440 | tf_op jit(solution)/shard_map/ppermute | solution.py:101
  51.7 3.4 %collective-permute-start.2 = (f32[4,8,8,256]{3,2,1,0:T(8,128)S(1)}, f32[4,8,8,256]{3,2,1,0:T(8,128)S(1)}, u32[]{:S(2)}, u32[]{:S(2)}) collective-permute-start(f32[4,8,8,256]{3,2,1,0:T(8,128)S(1)} %get-tuple-element.11), channel_id=1, source_target_pairs={{0,96},{32,0},{64,32},{96,64},{128,224},{160,128},{192,160},{224,1... | collective-permute-start | bytes 786440 | tf_op jit(solution)/shard_map/ppermute | solution.py:101
  55.1 3.4 %collective-permute-start.1 = (f32[4,8,8,256]{3,2,1,0:T(8,128)S(1)}, f32[4,8,8,256]{3,2,1,0:T(8,128)S(1)}, u32[]{:S(2)}, u32[]{:S(2)}) collective-permute-start(f32[4,8,8,256]{3,2,1,0:T(8,128)S(1)} %get-tuple-element.12), channel_id=1, source_target_pairs={{0,64},{32,96},{64,0},{96,32},{128,192},{160,224},{192,128},{224,1... | collective-permute-start | bytes 786440 | tf_op jit(solution)/shard_map/ppermute | solution.py:101
  58.6 0.0 copy-start.3
  58.6 0.6 copy-done.3
  59.2 5.7 %all-to-all-start.1 = ((f32[128,2,128]{2,1,0:T(2,128)}), f32[128,2,128]{2,1,0:T(2,128)S(1)}, u32[]{:S(2)}, u32[]{:S(2)}) async-start(f32[128,2,128]{2,1,0:T(2,128)} %get-tuple-element.9), calls=%async_computation.1 | async-start | bytes 262144 | tf_op jit(solution)/shard_map/all_to_all | solution.py:190
  64.9 0.0 collective-permute-done
  64.9 0.0 collective-permute-done.2
  64.9 0.0 collective-permute-done.1
  64.9 1.0 %fusion.1 = f32[4,8,8,256]{3,2,1,0:T(8,128)S(1)} fusion(f32[4,8,8,256]{3,2,1,0:T(8,128)S(1)} %collective-permute-done.2, f32[4,8,8,256]{3,2,1,0:T(8,128)S(1)} %collective-permute-done.1, f32[4,8,8,256]{3,2,1,0:T(8,128)S(1)} %collective-permute-done, f32[4,4,8,8,256]{4,3,2,1,0:T(8,128)} %bitcast.34, s32[]{:T(128)S(6)} %select_n.83), kind=kLoop, calls=%fused_computation.4 | loop fusion | flops 196608 | bytes 1310724 | tf_op jit(solution)/shard_map/add | solution.py:101
  66.0 9.8 %collective-permute-start.3 = (f32[2,8,8,256]{3,2,1,0:T(8,128)S(1)}, f32[2,8,8,256]{3,2,1,0:T(8,128)S(1)}, u32[]{:S(2)}, u32[]{:S(2)}) collective-permute-start(f32[2,8,8,256]{3,2,1,0:T(8,128)S(1)} %dynamic-slice_bitcast_fusion.3), channel_id=1, source_target_pairs={{0,256},{32,288},{64,320},{96,352},{128,384},{160,416},{192,448},{... | collective-permute-start | bytes 393224 | tf_op jit(solution)/shard_map/ppermute | solution.py:112
  75.8 0.0 all-to-all-done.1
  75.8 0.7 gather_fusion
  76.5 2.3 %collective-permute-done.3 = f32[2,8,8,256]{3,2,1,0:T(8,128)S(1)} collective-permute-done((f32[2,8,8,256]{3,2,1,0:T(8,128)S(1)}, f32[2,8,8,256]{3,2,1,0:T(8,128)S(1)}, u32[]{:S(2)}, u32[]{:S(2)}) %collective-permute-start.3) | collective-permute-done | bytes 131104 | tf_op jit(solution)/shard_map/ppermute | solution.py:112
  78.8 8.4 %collective-permute-start.4 = (f32[1,8,8,256]{3,2,1,0:T(8,128)S(1)}, f32[1,8,8,256]{3,2,1,0:T(8,128)S(1)}, u32[]{:S(2)}, u32[]{:S(2)}) collective-permute-start(f32[1,8,8,256]{3,2,1,0:T(8,128)S(1)} %constant_dynamic-slice_fusion), channel_id=1, source_target_pairs={{0,128},{32,160},{64,192},{96,224},{128,0},{160,32},{192,64},{224,... | collective-permute-start | bytes 196616 | tf_op jit(solution)/shard_map/ppermute | solution.py:112
  87.2 0.8 bitcast_select_fusion
  87.9 0.9 collective-permute-done.4
  88.8 0.6 fusion.2
  (6 shorter events, 0.1 us)
Async XLA Ops:
  0.6 0.7 copy-start.2
  0.6 15.2 %copy-start.1 = (f32[8,128,256]{2,1,0:T(8,128)S(1)}, f32[8,128,256]{2,1,0:T(8,128)}, u32[]{:S(2)}) copy-start(f32[8,128,256]{2,1,0:T(8,128)} %param.7) | copy-start | bytes 3145732
  5.2 27.1 %all-to-all-start = ((f32[128,6,128]{2,1,0:T(8,128)}), f32[128,6,128]{2,1,0:T(8,128)S(1)}, u32[]{:S(2)}, u32[]{:S(2)}) async-start(f32[128,6,128]{2,1,0:T(8,128)} %get-tuple-element.6), calls=%async_computation | async-start | bytes 1048576 | tf_op jit(solution)/shard_map/all_to_all | solution.py:184
  32.3 1.6 %copy-start = (f32[128,6,128]{2,1,0:T(8,128)}, f32[128,6,128]{2,1,0:T(8,128)S(1)}, u32[]{:S(2)}) copy-start(f32[128,6,128]{2,1,0:T(8,128)S(1)} %all-to-all-done.data_ref) | copy-start | bytes 1179652
  48.6 16.4 %collective-permute-start = (f32[4,8,8,256]{3,2,1,0:T(8,128)S(1)}, f32[4,8,8,256]{3,2,1,0:T(8,128)S(1)}, u32[]{:S(2)}, u32[]{:S(2)}) collective-permute-start(f32[4,8,8,256]{3,2,1,0:T(8,128)S(1)} %get-tuple-element.10), channel_id=1, source_target_pairs={{0,32},{32,64},{64,96},{96,0},{128,160},{160,192},{192,224},{224,1... | collective-permute-start | bytes 786440 | tf_op jit(solution)/shard_map/ppermute | solution.py:101
  51.7 13.2 %collective-permute-start.2 = (f32[4,8,8,256]{3,2,1,0:T(8,128)S(1)}, f32[4,8,8,256]{3,2,1,0:T(8,128)S(1)}, u32[]{:S(2)}, u32[]{:S(2)}) collective-permute-start(f32[4,8,8,256]{3,2,1,0:T(8,128)S(1)} %get-tuple-element.11), channel_id=1, source_target_pairs={{0,96},{32,0},{64,32},{96,64},{128,224},{160,128},{192,160},{224,1... | collective-permute-start | bytes 786440 | tf_op jit(solution)/shard_map/ppermute | solution.py:101
  55.1 9.9 %collective-permute-start.1 = (f32[4,8,8,256]{3,2,1,0:T(8,128)S(1)}, f32[4,8,8,256]{3,2,1,0:T(8,128)S(1)}, u32[]{:S(2)}, u32[]{:S(2)}) collective-permute-start(f32[4,8,8,256]{3,2,1,0:T(8,128)S(1)} %get-tuple-element.12), channel_id=1, source_target_pairs={{0,64},{32,96},{64,0},{96,32},{128,192},{160,224},{192,128},{224,1... | collective-permute-start | bytes 786440 | tf_op jit(solution)/shard_map/ppermute | solution.py:101
  58.6 0.7 copy-start.3
  59.2 16.6 %all-to-all-start.1 = ((f32[128,2,128]{2,1,0:T(2,128)}), f32[128,2,128]{2,1,0:T(2,128)S(1)}, u32[]{:S(2)}, u32[]{:S(2)}) async-start(f32[128,2,128]{2,1,0:T(2,128)} %get-tuple-element.9), calls=%async_computation.1 | async-start | bytes 262144 | tf_op jit(solution)/shard_map/all_to_all | solution.py:190
  66.0 12.8 %collective-permute-start.3 = (f32[2,8,8,256]{3,2,1,0:T(8,128)S(1)}, f32[2,8,8,256]{3,2,1,0:T(8,128)S(1)}, u32[]{:S(2)}, u32[]{:S(2)}) collective-permute-start(f32[2,8,8,256]{3,2,1,0:T(8,128)S(1)} %dynamic-slice_bitcast_fusion.3), channel_id=1, source_target_pairs={{0,256},{32,288},{64,320},{96,352},{128,384},{160,416},{192,448},{... | collective-permute-start | bytes 393224 | tf_op jit(solution)/shard_map/ppermute | solution.py:112
  78.8 10.0 %collective-permute-start.4 = (f32[1,8,8,256]{3,2,1,0:T(8,128)S(1)}, f32[1,8,8,256]{3,2,1,0:T(8,128)S(1)}, u32[]{:S(2)}, u32[]{:S(2)}) collective-permute-start(f32[1,8,8,256]{3,2,1,0:T(8,128)S(1)} %constant_dynamic-slice_fusion), channel_id=1, source_target_pairs={{0,128},{32,160},{64,192},{96,224},{128,0},{160,32},{192,64},{224,... | collective-permute-start | bytes 196616 | tf_op jit(solution)/shard_map/ppermute | solution.py:112

commit v16 on v14

--- a/solution.py
+++ b/solution.py
@@ -27,9 +27,10 @@
     return jnp.where(inside, jnp.exp(kernel_beta * (root_term - 1.0)), 0.0)
 
 
-def _grid_kernel(labels_ref, data_ref, tiles_ref, res_ref, grad_ref):
+def _grid_kernel(labels_ref, place_ref, data_ref, tiles_ref, res_ref, grad_ref):
     slots = data_ref.shape[0]
-    chunks, _, rows, _ = grad_ref.shape
+    ring, size_hi, _, rows, _ = grad_ref.shape
+    place = place_ref[0]
     width = tiles_ref.shape[2]
     vis = data_ref.shape[2]
     grad_ref[...] = jnp.zeros(grad_ref.shape, grad_ref.dtype)
@@ -37,7 +38,7 @@
 
     def body(s, carry):
         d = data_ref[s]
-        tile = labels_ref[s]
+        tile = labels_ref[s].astype(jnp.int32)
         quarter = d[3:5, :] * (1.0 / half_support)
         ku_t = _spheroid_scaled(cells - quarter[0:1]).astype(jnp.bfloat16)
         kv_t = _spheroid_scaled(cells - quarter[1:2]).astype(jnp.bfloat16).astype(jnp.float32)
@@ -52,13 +53,16 @@
         contrib = lax.dot_general(
             ku_t, spread_t, (((1,), (1,)), ((), ())), preferred_element_type=jnp.float32
         )
-        grad_ref[:, pl.ds(tile, 1)] += contrib.reshape(chunks, 1, rows, 2 * width)
+        pieces = contrib.reshape(size_hi, ring, 1, rows, 2 * width)
+        for x in range(ring):
+            shift = (x - place + ring) % ring
+            grad_ref[pl.ds(shift, 1), :, pl.ds(tile, 1)] += pieces[:, x][None]
         return carry
 
     lax.fori_loop(0, slots, body, 0, unroll=32)
 
 
-def _grid_call(labels, data, tiles_t, chunks):
+def _grid_call(labels, place, data, tiles_t, chunks, ring):
     slots, _, vis = data.shape
     tile_count, wide, width = tiles_t.shape
     vmem = pltpu.MemorySpace.VMEM
@@ -66,15 +70,18 @@
         _grid_kernel,
         out_shape=(
             jax.ShapeDtypeStruct((slots, 2, vis), jnp.float32),
-            jax.ShapeDtypeStruct((chunks, tile_count, width // chunks, wide), jnp.float32),
+            jax.ShapeDtypeStruct(
+                (ring, chunks // ring, tile_count, width // chunks, wide), jnp.float32
+            ),
         ),
         in_specs=[
             pl.BlockSpec(memory_space=pltpu.MemorySpace.SMEM),
+            pl.BlockSpec(memory_space=pltpu.MemorySpace.SMEM),
             pl.BlockSpec(memory_space=vmem),
             pl.BlockSpec(memory_space=vmem),
         ],
         out_specs=(pl.BlockSpec(memory_space=vmem), pl.BlockSpec(memory_space=vmem)),
-    )(labels, data, tiles_t)
+    )(labels, place, data, tiles_t)
 
 
 def _ring_pairs(size_hi, size_lo, shift, along_lo):
@@ -89,16 +96,12 @@
 
 
 def _chan_reduce(gradient):
-    chunks = gradient.shape[0]
-    size_lo = 4
-    size_hi = chunks // size_lo
+    size_lo, size_hi = gradient.shape[0], gradient.shape[1]
     c = lax.axis_index("chan")
     hi, lo = c // size_lo, c % size_lo
-    parts = gradient.reshape((size_hi, size_lo) + gradient.shape[1:])
-    acc = lax.dynamic_index_in_dim(parts, lo, 1, keepdims=False)
+    acc = gradient[0]
     for k in range(1, size_lo):
-        piece = lax.dynamic_index_in_dim(parts, (lo + k) % size_lo, 1, keepdims=False)
-        acc = acc + lax.ppermute(piece, "chan", _ring_pairs(size_hi, size_lo, k, True))
+        acc = acc + lax.ppermute(gradient[k], "chan", _ring_pairs(size_hi, size_lo, k, True))
     for bit in (2, 1):
         halves = acc.reshape((2, acc.shape[0] // 2) + acc.shape[1:]) if bit == 2 else acc.reshape(
             (2, 1) + acc.shape[1:]
@@ -182,9 +185,11 @@
         tile_ids, owner_map, offsets[0], positions[0], observed[0], weights[0], owners, capacity
     )
     incoming = lax.all_to_all(outgoing, "bl", split_axis=0, concat_axis=0, tiled=True)
-    labels = jnp.max(incoming[:, 5, :], axis=1).astype(jnp.int32)
+    labels = jnp.max(incoming[:, 5, :], axis=1)
+    ring = 4
+    place = (lax.axis_index("chan") % ring).astype(jnp.int32).reshape(1)
     tiles_t = jnp.swapaxes(grid.astype(jnp.bfloat16), 1, 2)
-    residual_all, gradient = _grid_call(labels, incoming, tiles_t, chan)
+    residual_all, gradient = _grid_call(labels, place, incoming, tiles_t, chan, ring)
     share_rows = tile_width // chan
     grad_share = _chan_reduce(gradient)
     returned = lax.all_to_all(residual_all, "bl", split_axis=0, concat_axis=0, tiled=True)

time: 91.4 us -> 91.6 us (level)
  no operation moved by 1% of the time
where the time goes in v16:
time: 91.6 us; the launch traced here: 89.9 us
  starting transfers between devices  44.4 us (48%)
  waiting for transfers between devices  18.7 us (20%)
  Pallas kernels  16.9 us (18%)
  local copies, waits for them, and re-layouts  5.05 us (6%)
  other arithmetic  4 us (4%)
    ppermute x2, starting transfers between devices, _chan_reduce(): acc = keep + lax.ppermute(give, 'chan', pairs)  18.2 us
    all_to_all x1, waiting for transfers between devices, shards(): lax.all_to_all(outgoing, 'bl', split_axis=0, concat_axis=0, tiled=True)  15.5 us
    pallas_call x1, Pallas kernels, _grid_call(): pl.pallas_call(_grid_kernel, out_shape=(jax.ShapeDtypeStruct((slots, 2, v...  13.7 us
    all_to_all x1, starting transfers between devices, shards(): lax.all_to_all(outgoing, 'bl', split_axis=0, concat_axis=0, tiled=True)  10.6 us
    ppermute x3, starting transfers between devices, _chan_reduce(): lax.ppermute(gradient[k], 'chan', _ring_pairs(size_hi, size_lo, k, True))  9.96 us
    all_to_all x1, starting transfers between devices, shards(): lax.all_to_all(residual_all, 'bl', split_axis=0, concat_axis=0, tiled=True)  5.64 us
    pallas_call x1, Pallas kernels, _dispatch_call(): pl.pallas_call(_dispatch_kernel, out_shape=(jax.ShapeDtypeStruct((owners...  3.21 us
    ppermute x2, waiting for transfers between devices, _chan_reduce(): acc = keep + lax.ppermute(give, 'chan', pairs)  3.17 us
  transfers between devices with their start and end apart: 7, of which 3 were waited for; matrix products, arithmetic and copies ran while one was open for 4% of the time, Pallas kernels for 0%

profile of v16, /device:TPU:1, one launch (start us, length us, event | category | flops | bytes accessed | tf_op | source)
XLA Modules:
  0.0 89.9 jit_solution(12951460818942811514)
XLA Ops:
  0.6 0.0 copy-start.1
  0.6 0.9 copy.11
  1.5 0.7 reshape_squeeze.3.off_ref
  2.1 3.2 %shard_map.86 = (f32[128,6,128]{2,1,0:T(8,128)}, s32[64]{0:T(128)}) custom-call(s32[64]{0:T(128)} %bitcast.37, s32[256]{0:T(256)} %owner_ref.1, s32[128]{0:T(128)} %reshape_squeeze.3.off_ref, f32[64,2,128]{2,1,0:T(2,128)} %bitcast.34, f32[64,2,128]{2,1,0:T(2,128)} %bitcast.35, f32[64,128]{1,0:T(8,128)} %bitcast.36), custom_call_target="tpu_custom_call" | custom-call | tf_op jit(solution)/shard_map/pallas_call | solution.py:156
  5.4 10.6 %all-to-all-start = ((f32[128,6,128]{2,1,0:T(8,128)}), f32[128,6,128]{2,1,0:T(8,128)S(1)}, u32[]{:S(2)}, u32[]{:S(2)}) async-start(f32[128,6,128]{2,1,0:T(8,128)} %get-tuple-element.6), calls=%async_computation | async-start | bytes 1048576 | tf_op jit(solution)/shard_map/all_to_all | solution.py:187
  16.0 0.0 copy-done.1
  16.0 1.0 %copy.12 = bf16[8,128,256]{1,2,0:T(8,128)(2,1)} copy(f32[8,128,256]{2,1,0:T(8,128)S(1)} %copy-done.1) | data formatting | bytes 1572864 | tf_op args[0]
  17.0 15.5 %all-to-all-done.data_ref = f32[128,6,128]{2,1,0:T(8,128)S(1)} async-done(((f32[128,6,128]{2,1,0:T(8,128)}), f32[128,6,128]{2,1,0:T(8,128)S(1)}, u32[]{:S(2)}, u32[]{:S(2)}) %all-to-all-start) | async-done | bytes 393248 | tf_op jit(solution)/shard_map/all_to_all | solution.py:187
  32.5 0.0 copy-start
  32.5 1.5 %slice_reduce_fusion.labels_ref = f32[128]{0:T(128)} fusion(f32[128,6,128]{2,1,0:T(8,128)S(1)} %all-to-all-done.data_ref), kind=kLoop, calls=%fused_computation.10 | loop fusion | flops 16256 | bytes 66048 | tf_op jit(solution)/shard_map/reduce_max | solution.py:188
  34.0 0.0 copy-done
  34.0 13.7 %shard_map.87 = (f32[128,2,128]{2,1,0:T(2,128)}, f32[4,4,8,8,256]{4,3,2,1,0:T(8,128)}) custom-call(f32[128]{0:T(128)} %slice_reduce_fusion.labels_ref, s32[1]{0:T(128)} %bitcast.4.place_ref, f32[128,6,128]{2,1,0:T(8,128)} %copy-done, bf16[8,256,128]{2,1,0:T(8,128)(2,1)} %bitcast.31), custom_call_target="tpu_custom_call" | custom-call | tf_op jit(solution)/shard_map/pallas_call | solution.py:69
  47.7 1.2 %slice_bitcast_fusion.2 = (f32[4,8,8,256]{3,2,1,0:T(8,128)S(1)}, f32[4,8,8,256]{3,2,1,0:T(8,128)S(1)}, f32[4,8,8,256]{3,2,1,0:T(8,128)S(1)}) fusion(f32[4,4,8,8,256]{4,3,2,1,0:T(8,128)} %get-tuple-element.7), kind=kLoop, calls=%fused_computation.7 | loop fusion | bytes 1572864 | tf_op jit(solution)/shard_map/squeeze | solution.py:104
  48.9 3.1 %collective-permute-start = (f32[4,8,8,256]{3,2,1,0:T(8,128)S(1)}, f32[4,8,8,256]{3,2,1,0:T(8,128)S(1)}, u32[]{:S(2)}, u32[]{:S(2)}) collective-permute-start(f32[4,8,8,256]{3,2,1,0:T(8,128)S(1)} %get-tuple-element.10), channel_id=1, source_target_pairs={{0,32},{32,64},{64,96},{96,0},{128,160},{160,192},{192,224},{224,1... | collective-permute-start | bytes 786440 | tf_op jit(solution)/shard_map/ppermute | solution.py:104
  52.1 3.4 %collective-permute-start.2 = (f32[4,8,8,256]{3,2,1,0:T(8,128)S(1)}, f32[4,8,8,256]{3,2,1,0:T(8,128)S(1)}, u32[]{:S(2)}, u32[]{:S(2)}) collective-permute-start(f32[4,8,8,256]{3,2,1,0:T(8,128)S(1)} %get-tuple-element.11), channel_id=1, source_target_pairs={{0,96},{32,0},{64,32},{96,64},{128,224},{160,128},{192,160},{224,1... | collective-permute-start | bytes 786440 | tf_op jit(solution)/shard_map/ppermute | solution.py:104
  55.4 3.5 %collective-permute-start.1 = (f32[4,8,8,256]{3,2,1,0:T(8,128)S(1)}, f32[4,8,8,256]{3,2,1,0:T(8,128)S(1)}, u32[]{:S(2)}, u32[]{:S(2)}) collective-permute-start(f32[4,8,8,256]{3,2,1,0:T(8,128)S(1)} %get-tuple-element.12), channel_id=1, source_target_pairs={{0,64},{32,96},{64,0},{96,32},{128,192},{160,224},{192,128},{224,1... | collective-permute-start | bytes 786440 | tf_op jit(solution)/shard_map/ppermute | solution.py:104
  59.0 0.0 copy-start.2
  59.0 0.6 copy-done.2
  59.6 5.6 %all-to-all-start.1 = ((f32[128,2,128]{2,1,0:T(2,128)}), f32[128,2,128]{2,1,0:T(2,128)S(1)}, u32[]{:S(2)}, u32[]{:S(2)}) async-start(f32[128,2,128]{2,1,0:T(2,128)} %get-tuple-element.9), calls=%async_computation.1 | async-start | bytes 262144 | tf_op jit(solution)/shard_map/all_to_all | solution.py:195
  65.3 0.0 collective-permute-done
  65.3 0.0 collective-permute-done.2
  65.3 0.0 collective-permute-done.1
  65.3 1.0 %fusion.1 = f32[4,8,8,256]{3,2,1,0:T(8,128)S(1)} fusion(f32[4,8,8,256]{3,2,1,0:T(8,128)S(1)} %collective-permute-done.2, f32[4,8,8,256]{3,2,1,0:T(8,128)S(1)} %collective-permute-done.1, f32[4,8,8,256]{3,2,1,0:T(8,128)S(1)} %collective-permute-done, f32[4,4,8,8,256]{4,3,2,1,0:T(8,128)} %get-tuple-element.7), kind=kLoop, calls=%fused_computation.4 | loop fusion | flops 196608 | bytes 1310720 | tf_op jit(solution)/shard_map/add | solution.py:104
  66.4 9.8 %collective-permute-start.3 = (f32[2,8,8,256]{3,2,1,0:T(8,128)S(1)}, f32[2,8,8,256]{3,2,1,0:T(8,128)S(1)}, u32[]{:S(2)}, u32[]{:S(2)}) collective-permute-start(f32[2,8,8,256]{3,2,1,0:T(8,128)S(1)} %dynamic-slice_bitcast_fusion), channel_id=1, source_target_pairs={{0,256},{32,288},{64,320},{96,352},{128,384},{160,416},{192,448},{... | collective-permute-start | bytes 393224 | tf_op jit(solution)/shard_map/ppermute | solution.py:115
  76.2 0.0 all-to-all-done.1
  76.2 0.7 gather_fusion
  76.9 2.3 %collective-permute-done.3 = f32[2,8,8,256]{3,2,1,0:T(8,128)S(1)} collective-permute-done((f32[2,8,8,256]{3,2,1,0:T(8,128)S(1)}, f32[2,8,8,256]{3,2,1,0:T(8,128)S(1)}, u32[]{:S(2)}, u32[]{:S(2)}) %collective-permute-start.3) | collective-permute-done | bytes 131104 | tf_op jit(solution)/shard_map/ppermute | solution.py:115
  79.2 8.4 %collective-permute-start.4 = (f32[1,8,8,256]{3,2,1,0:T(8,128)S(1)}, f32[1,8,8,256]{3,2,1,0:T(8,128)S(1)}, u32[]{:S(2)}, u32[]{:S(2)}) collective-permute-start(f32[1,8,8,256]{3,2,1,0:T(8,128)S(1)} %constant_dynamic-slice_fusion), channel_id=1, source_target_pairs={{0,128},{32,160},{64,192},{96,224},{128,0},{160,32},{192,64},{224,... | collective-permute-start | bytes 196616 | tf_op jit(solution)/shard_map/ppermute | solution.py:115
  87.6 0.8 bitcast_select_fusion
  88.4 0.9 collective-permute-done.4
  89.3 0.6 fusion.2
  (6 shorter events, 0.1 us)
Async XLA Ops:
  0.6 15.3 %copy-start.1 = (f32[8,128,256]{2,1,0:T(8,128)S(1)}, f32[8,128,256]{2,1,0:T(8,128)}, u32[]{:S(2)}) copy-start(f32[8,128,256]{2,1,0:T(8,128)} %param.7) | copy-start | bytes 3145732
  5.4 27.1 %all-to-all-start = ((f32[128,6,128]{2,1,0:T(8,128)}), f32[128,6,128]{2,1,0:T(8,128)S(1)}, u32[]{:S(2)}, u32[]{:S(2)}) async-start(f32[128,6,128]{2,1,0:T(8,128)} %get-tuple-element.6), calls=%async_computation | async-start | bytes 1048576 | tf_op jit(solution)/shard_map/all_to_all | solution.py:187
  32.5 1.5 %copy-start = (f32[128,6,128]{2,1,0:T(8,128)}, f32[128,6,128]{2,1,0:T(8,128)S(1)}, u32[]{:S(2)}) copy-start(f32[128,6,128]{2,1,0:T(8,128)S(1)} %all-to-all-done.data_ref) | copy-start | bytes 1179652
  48.9 16.4 %collective-permute-start = (f32[4,8,8,256]{3,2,1,0:T(8,128)S(1)}, f32[4,8,8,256]{3,2,1,0:T(8,128)S(1)}, u32[]{:S(2)}, u32[]{:S(2)}) collective-permute-start(f32[4,8,8,256]{3,2,1,0:T(8,128)S(1)} %get-tuple-element.10), channel_id=1, source_target_pairs={{0,32},{32,64},{64,96},{96,0},{128,160},{160,192},{192,224},{224,1... | collective-permute-start | bytes 786440 | tf_op jit(solution)/shard_map/ppermute | solution.py:104
  52.1 13.2 %collective-permute-start.2 = (f32[4,8,8,256]{3,2,1,0:T(8,128)S(1)}, f32[4,8,8,256]{3,2,1,0:T(8,128)S(1)}, u32[]{:S(2)}, u32[]{:S(2)}) collective-permute-start(f32[4,8,8,256]{3,2,1,0:T(8,128)S(1)} %get-tuple-element.11), channel_id=1, source_target_pairs={{0,96},{32,0},{64,32},{96,64},{128,224},{160,128},{192,160},{224,1... | collective-permute-start | bytes 786440 | tf_op jit(solution)/shard_map/ppermute | solution.py:104
  55.4 9.9 %collective-permute-start.1 = (f32[4,8,8,256]{3,2,1,0:T(8,128)S(1)}, f32[4,8,8,256]{3,2,1,0:T(8,128)S(1)}, u32[]{:S(2)}, u32[]{:S(2)}) collective-permute-start(f32[4,8,8,256]{3,2,1,0:T(8,128)S(1)} %get-tuple-element.12), channel_id=1, source_target_pairs={{0,64},{32,96},{64,0},{96,32},{128,192},{160,224},{192,128},{224,1... | collective-permute-start | bytes 786440 | tf_op jit(solution)/shard_map/ppermute | solution.py:104
  59.0 0.7 copy-start.2
  59.6 16.6 %all-to-all-start.1 = ((f32[128,2,128]{2,1,0:T(2,128)}), f32[128,2,128]{2,1,0:T(2,128)S(1)}, u32[]{:S(2)}, u32[]{:S(2)}) async-start(f32[128,2,128]{2,1,0:T(2,128)} %get-tuple-element.9), calls=%async_computation.1 | async-start | bytes 262144 | tf_op jit(solution)/shard_map/all_to_all | solution.py:195
  66.4 12.8 %collective-permute-start.3 = (f32[2,8,8,256]{3,2,1,0:T(8,128)S(1)}, f32[2,8,8,256]{3,2,1,0:T(8,128)S(1)}, u32[]{:S(2)}, u32[]{:S(2)}) collective-permute-start(f32[2,8,8,256]{3,2,1,0:T(8,128)S(1)} %dynamic-slice_bitcast_fusion), channel_id=1, source_target_pairs={{0,256},{32,288},{64,320},{96,352},{128,384},{160,416},{192,448},{... | collective-permute-start | bytes 393224 | tf_op jit(solution)/shard_map/ppermute | solution.py:115
  79.2 10.1 %collective-permute-start.4 = (f32[1,8,8,256]{3,2,1,0:T(8,128)S(1)}, f32[1,8,8,256]{3,2,1,0:T(8,128)S(1)}, u32[]{:S(2)}, u32[]{:S(2)}) collective-permute-start(f32[1,8,8,256]{3,2,1,0:T(8,128)S(1)} %constant_dynamic-slice_fusion), channel_id=1, source_target_pairs={{0,128},{32,160},{64,192},{96,224},{128,0},{160,32},{192,64},{224,... | collective-permute-start | bytes 196616 | tf_op jit(solution)/shard_map/ppermute | solution.py:115

commit v17 on v14

--- a/solution.py
+++ b/solution.py
@@ -55,7 +55,7 @@
         grad_ref[:, pl.ds(tile, 1)] += contrib.reshape(chunks, 1, rows, 2 * width)
         return carry
 
-    lax.fori_loop(0, slots, body, 0, unroll=32)
+    lax.fori_loop(0, slots, body, 0, unroll=64)
 
 
 def _grid_call(labels, data, tiles_t, chunks):

time: 91.4 us -> 91 us (level)
  no operation moved by 1% of the time
where the time goes in v17:
time: 91 us; the launch traced here: 89.4 us
  starting transfers between devices  44.3 us (49%)
  waiting for transfers between devices  18.6 us (20%)
  Pallas kernels  16.4 us (18%)
  local copies, waits for them, and re-layouts  5.06 us (6%)
  other arithmetic  4.02 us (4%)
  between operations  0.96 us (1%)
    ppermute x2, starting transfers between devices, _chan_reduce(): acc = keep + lax.ppermute(give, 'chan', pairs)  18.1 us
    all_to_all x1, waiting for transfers between devices, shards(): lax.all_to_all(outgoing, 'bl', split_axis=0, concat_axis=0, tiled=True)  15.5 us
    pallas_call x1, Pallas kernels, _grid_call(): pl.pallas_call(_grid_kernel, out_shape=(jax.ShapeDtypeStruct((slots, 2, v...  13.2 us
    all_to_all x1, starting transfers between devices, shards(): lax.all_to_all(outgoing, 'bl', split_axis=0, concat_axis=0, tiled=True)  10.6 us
    ppermute x3, starting transfers between devices, _chan_reduce(): lax.ppermute(piece, 'chan', _ring_pairs(size_hi, size_lo, k, True))  9.93 us
    all_to_all x1, starting transfers between devices, shards(): lax.all_to_all(residual_all, 'bl', split_axis=0, concat_axis=0, tiled=True)  5.7 us
    pallas_call x1, Pallas kernels, _dispatch_call(): pl.pallas_call(_dispatch_kernel, out_shape=(jax.ShapeDtypeStruct((owners...  3.21 us
    ppermute x2, waiting for transfers between devices, _chan_reduce(): acc = keep + lax.ppermute(give, 'chan', pairs)  3.17 us
  transfers between devices with their start and end apart: 7, of which 3 were waited for; matrix products, arithmetic and copies ran while one was open for 4% of the time, Pallas kernels for 0%

profile of v17, /device:TPU:1, one launch (start us, length us, event | category | flops | bytes accessed | tf_op | source)
XLA Modules:
  0.0 89.4 jit_solution(16474167911594690445)
XLA Ops:
  0.6 0.0 copy-start.1
  0.6 0.9 copy.11
  1.5 0.7 reshape_squeeze.3.off_ref
  2.1 3.2 %shard_map.86 = (f32[128,6,128]{2,1,0:T(8,128)}, s32[64]{0:T(128)}) custom-call(s32[64]{0:T(128)} %bitcast.39, s32[256]{0:T(256)} %owner_ref.1, s32[128]{0:T(128)} %reshape_squeeze.3.off_ref, f32[64,2,128]{2,1,0:T(2,128)} %bitcast.36, f32[64,2,128]{2,1,0:T(2,128)} %bitcast.37, f32[64,128]{1,0:T(8,128)} %bitcast.38), custom_call_target="tpu_custom_call" | custom-call | tf_op jit(solution)/shard_map/pallas_call | solution.py:153
  5.4 10.6 %all-to-all-start = ((f32[128,6,128]{2,1,0:T(8,128)}), f32[128,6,128]{2,1,0:T(8,128)S(1)}, u32[]{:S(2)}, u32[]{:S(2)}) async-start(f32[128,6,128]{2,1,0:T(8,128)} %get-tuple-element.6), calls=%async_computation | async-start | bytes 1048576 | tf_op jit(solution)/shard_map/all_to_all | solution.py:184
  16.0 0.0 copy-done.1
  16.0 1.0 %copy.12 = bf16[8,128,256]{1,2,0:T(8,128)(2,1)} copy(f32[8,128,256]{2,1,0:T(8,128)S(1)} %copy-done.1) | data formatting | bytes 1572864 | tf_op args[0]
  17.0 15.5 %all-to-all-done.data_ref = f32[128,6,128]{2,1,0:T(8,128)S(1)} async-done(((f32[128,6,128]{2,1,0:T(8,128)}), f32[128,6,128]{2,1,0:T(8,128)S(1)}, u32[]{:S(2)}, u32[]{:S(2)}) %all-to-all-start) | async-done | bytes 393248 | tf_op jit(solution)/shard_map/all_to_all | solution.py:184
  32.5 0.0 copy-start
  32.5 1.0 %slice_reduce_fusion = f32[128]{0:T(128)S(1)} fusion(f32[128,6,128]{2,1,0:T(8,128)S(1)} %all-to-all-done.data_ref), kind=kLoop, calls=%fused_computation.10 | loop fusion | flops 16256 | bytes 66048 | tf_op jit(solution)/shard_map/reduce_max | solution.py:185
  33.5 0.5 convert_element_type.6.labels_ref
  34.0 0.0 copy-done
  34.0 13.2 %shard_map.87 = (f32[128,2,128]{2,1,0:T(2,128)}, f32[16,8,8,256]{3,2,1,0:T(8,128)}) custom-call(s32[128]{0:T(128)} %convert_element_type.6.labels_ref, f32[128,6,128]{2,1,0:T(8,128)} %copy-done, bf16[8,256,128]{2,1,0:T(8,128)(2,1)} %bitcast.31), custom_call_target="tpu_custom_call" | custom-call | tf_op jit(solution)/shard_map/pallas_call | solution.py:65
  47.2 1.2 %dynamic-slice_bitcast_fusion.2 = (f32[4,8,8,256]{3,2,1,0:T(8,128)S(1)}, f32[4,8,8,256]{3,2,1,0:T(8,128)S(1)}, f32[4,8,8,256]{3,2,1,0:T(8,128)S(1)}) fusion(f32[4,4,8,8,256]{4,3,2,1,0:T(8,128)} %bitcast.32, s32[]{:T(128)S(6)} %select_n.85, s32[]{:T(128)S(6)} %select_n.89, s32[]{:T(128)S(6)} %select_n.87), kind=kLoop, calls=%fused_computation.7 | loop fusion | bytes 1572876 | tf_op jit(solution)/shard_map/jit(dynamic_index_in_dim)/squeeze | solution.py:100
  48.4 3.1 %collective-permute-start = (f32[4,8,8,256]{3,2,1,0:T(8,128)S(1)}, f32[4,8,8,256]{3,2,1,0:T(8,128)S(1)}, u32[]{:S(2)}, u32[]{:S(2)}) collective-permute-start(f32[4,8,8,256]{3,2,1,0:T(8,128)S(1)} %get-tuple-element.10), channel_id=1, source_target_pairs={{0,32},{32,64},{64,96},{96,0},{128,160},{160,192},{192,224},{224,1... | collective-permute-start | bytes 786440 | tf_op jit(solution)/shard_map/ppermute | solution.py:101
  51.5 3.4 %collective-permute-start.2 = (f32[4,8,8,256]{3,2,1,0:T(8,128)S(1)}, f32[4,8,8,256]{3,2,1,0:T(8,128)S(1)}, u32[]{:S(2)}, u32[]{:S(2)}) collective-permute-start(f32[4,8,8,256]{3,2,1,0:T(8,128)S(1)} %get-tuple-element.11), channel_id=1, source_target_pairs={{0,96},{32,0},{64,32},{96,64},{128,224},{160,128},{192,160},{224,1... | collective-permute-start | bytes 786440 | tf_op jit(solution)/shard_map/ppermute | solution.py:101
  54.9 3.4 %collective-permute-start.1 = (f32[4,8,8,256]{3,2,1,0:T(8,128)S(1)}, f32[4,8,8,256]{3,2,1,0:T(8,128)S(1)}, u32[]{:S(2)}, u32[]{:S(2)}) collective-permute-start(f32[4,8,8,256]{3,2,1,0:T(8,128)S(1)} %get-tuple-element.12), channel_id=1, source_target_pairs={{0,64},{32,96},{64,0},{96,32},{128,192},{160,224},{192,128},{224,1... | collective-permute-start | bytes 786440 | tf_op jit(solution)/shard_map/ppermute | solution.py:101
  58.4 0.0 copy-start.2
  58.4 0.6 copy-done.2
  59.1 5.7 %all-to-all-start.1 = ((f32[128,2,128]{2,1,0:T(2,128)}), f32[128,2,128]{2,1,0:T(2,128)S(1)}, u32[]{:S(2)}, u32[]{:S(2)}) async-start(f32[128,2,128]{2,1,0:T(2,128)} %get-tuple-element.9), calls=%async_computation.1 | async-start | bytes 262144 | tf_op jit(solution)/shard_map/all_to_all | solution.py:190
  64.8 0.0 collective-permute-done
  64.8 0.0 collective-permute-done.2
  64.8 0.0 collective-permute-done.1
  64.8 1.0 %fusion.1 = f32[4,8,8,256]{3,2,1,0:T(8,128)S(1)} fusion(f32[4,8,8,256]{3,2,1,0:T(8,128)S(1)} %collective-permute-done.2, f32[4,8,8,256]{3,2,1,0:T(8,128)S(1)} %collective-permute-done.1, f32[4,8,8,256]{3,2,1,0:T(8,128)S(1)} %collective-permute-done, f32[4,4,8,8,256]{4,3,2,1,0:T(8,128)} %bitcast.33, s32[]{:T(128)S(6)} %select_n.83), kind=kLoop, calls=%fused_computation.4 | loop fusion | flops 196608 | bytes 1310724 | tf_op jit(solution)/shard_map/add | solution.py:101
  65.9 9.7 %collective-permute-start.3 = (f32[2,8,8,256]{3,2,1,0:T(8,128)S(1)}, f32[2,8,8,256]{3,2,1,0:T(8,128)S(1)}, u32[]{:S(2)}, u32[]{:S(2)}) collective-permute-start(f32[2,8,8,256]{3,2,1,0:T(8,128)S(1)} %dynamic-slice_bitcast_fusion.3), channel_id=1, source_target_pairs={{0,256},{32,288},{64,320},{96,352},{128,384},{160,416},{192,448},{... | collective-permute-start | bytes 393224 | tf_op jit(solution)/shard_map/ppermute | solution.py:112
  75.7 0.0 all-to-all-done.1
  75.7 0.7 gather_fusion
  76.3 2.3 %collective-permute-done.3 = f32[2,8,8,256]{3,2,1,0:T(8,128)S(1)} collective-permute-done((f32[2,8,8,256]{3,2,1,0:T(8,128)S(1)}, f32[2,8,8,256]{3,2,1,0:T(8,128)S(1)}, u32[]{:S(2)}, u32[]{:S(2)}) %collective-permute-start.3) | collective-permute-done | bytes 131104 | tf_op jit(solution)/shard_map/ppermute | solution.py:112
  78.7 8.4 %collective-permute-start.4 = (f32[1,8,8,256]{3,2,1,0:T(8,128)S(1)}, f32[1,8,8,256]{3,2,1,0:T(8,128)S(1)}, u32[]{:S(2)}, u32[]{:S(2)}) collective-permute-start(f32[1,8,8,256]{3,2,1,0:T(8,128)S(1)} %constant_dynamic-slice_fusion), channel_id=1, source_target_pairs={{0,128},{32,160},{64,192},{96,224},{128,0},{160,32},{192,64},{224,... | collective-permute-start | bytes 196616 | tf_op jit(solution)/shard_map/ppermute | solution.py:112
  87.1 0.8 bitcast_select_fusion
  87.8 0.9 collective-permute-done.4
  88.7 0.6 fusion.2
  (6 shorter events, 0.1 us)
Async XLA Ops:
  0.6 15.4 %copy-start.1 = (f32[8,128,256]{2,1,0:T(8,128)S(1)}, f32[8,128,256]{2,1,0:T(8,128)}, u32[]{:S(2)}) copy-start(f32[8,128,256]{2,1,0:T(8,128)} %param.7) | copy-start | bytes 3145732
  5.4 27.1 %all-to-all-start = ((f32[128,6,128]{2,1,0:T(8,128)}), f32[128,6,128]{2,1,0:T(8,128)S(1)}, u32[]{:S(2)}, u32[]{:S(2)}) async-start(f32[128,6,128]{2,1,0:T(8,128)} %get-tuple-element.6), calls=%async_computation | async-start | bytes 1048576 | tf_op jit(solution)/shard_map/all_to_all | solution.py:184
  32.5 1.6 %copy-start = (f32[128,6,128]{2,1,0:T(8,128)}, f32[128,6,128]{2,1,0:T(8,128)S(1)}, u32[]{:S(2)}) copy-start(f32[128,6,128]{2,1,0:T(8,128)S(1)} %all-to-all-done.data_ref) | copy-start | bytes 1179652
  48.4 16.4 %collective-permute-start = (f32[4,8,8,256]{3,2,1,0:T(8,128)S(1)}, f32[4,8,8,256]{3,2,1,0:T(8,128)S(1)}, u32[]{:S(2)}, u32[]{:S(2)}) collective-permute-start(f32[4,8,8,256]{3,2,1,0:T(8,128)S(1)} %get-tuple-element.10), channel_id=1, source_target_pairs={{0,32},{32,64},{64,96},{96,0},{128,160},{160,192},{192,224},{224,1... | collective-permute-start | bytes 786440 | tf_op jit(solution)/shard_map/ppermute | solution.py:101
  51.5 13.3 %collective-permute-start.2 = (f32[4,8,8,256]{3,2,1,0:T(8,128)S(1)}, f32[4,8,8,256]{3,2,1,0:T(8,128)S(1)}, u32[]{:S(2)}, u32[]{:S(2)}) collective-permute-start(f32[4,8,8,256]{3,2,1,0:T(8,128)S(1)} %get-tuple-element.11), channel_id=1, source_target_pairs={{0,96},{32,0},{64,32},{96,64},{128,224},{160,128},{192,160},{224,1... | collective-permute-start | bytes 786440 | tf_op jit(solution)/shard_map/ppermute | solution.py:101
  54.9 9.9 %collective-permute-start.1 = (f32[4,8,8,256]{3,2,1,0:T(8,128)S(1)}, f32[4,8,8,256]{3,2,1,0:T(8,128)S(1)}, u32[]{:S(2)}, u32[]{:S(2)}) collective-permute-start(f32[4,8,8,256]{3,2,1,0:T(8,128)S(1)} %get-tuple-element.12), channel_id=1, source_target_pairs={{0,64},{32,96},{64,0},{96,32},{128,192},{160,224},{192,128},{224,1... | collective-permute-start | bytes 786440 | tf_op jit(solution)/shard_map/ppermute | solution.py:101
  58.4 0.7 copy-start.2
  59.1 16.6 %all-to-all-start.1 = ((f32[128,2,128]{2,1,0:T(2,128)}), f32[128,2,128]{2,1,0:T(2,128)S(1)}, u32[]{:S(2)}, u32[]{:S(2)}) async-start(f32[128,2,128]{2,1,0:T(2,128)} %get-tuple-element.9), calls=%async_computation.1 | async-start | bytes 262144 | tf_op jit(solution)/shard_map/all_to_all | solution.py:190
  65.9 12.7 %collective-permute-start.3 = (f32[2,8,8,256]{3,2,1,0:T(8,128)S(1)}, f32[2,8,8,256]{3,2,1,0:T(8,128)S(1)}, u32[]{:S(2)}, u32[]{:S(2)}) collective-permute-start(f32[2,8,8,256]{3,2,1,0:T(8,128)S(1)} %dynamic-slice_bitcast_fusion.3), channel_id=1, source_target_pairs={{0,256},{32,288},{64,320},{96,352},{128,384},{160,416},{192,448},{... | collective-permute-start | bytes 393224 | tf_op jit(solution)/shard_map/ppermute | solution.py:112
  78.7 10.0 %collective-permute-start.4 = (f32[1,8,8,256]{3,2,1,0:T(8,128)S(1)}, f32[1,8,8,256]{3,2,1,0:T(8,128)S(1)}, u32[]{:S(2)}, u32[]{:S(2)}) collective-permute-start(f32[1,8,8,256]{3,2,1,0:T(8,128)S(1)} %constant_dynamic-slice_fusion), channel_id=1, source_target_pairs={{0,128},{32,160},{64,192},{96,224},{128,0},{160,32},{192,64},{224,... | collective-permute-start | bytes 196616 | tf_op jit(solution)/shard_map/ppermute | solution.py:112
